TPU v7x, 32 devices: a whole 2x2x4 slice. The times are simulated.
32 devices in a mesh: nets: 8 (over z, x), region: 4 (over y, core).
Axes of the slice: x: 2, y: 2, z: 4, core: 2. Of those that a mesh axis runs over, the one named last changes fastest.
Arguments:
- logits: float32 [8192, 256], P('nets'), may hold values from -24 to 465
- tile_values: bfloat16 [8, 4, 384, 128, 128], P('nets', 'region'), may hold values from 0 to 1
- tile_pattern: int32 [8, 4, 384], P('nets', 'region'), may hold values from 0 to 2047
- tile_edge: int32 [8, 4, 384], P('nets', 'region'), may hold values from 0 to 63
- tile_counts: int32 [8, 4, 8], P('nets', 'region'), may hold values from 12 to 48, as said below
- capacity: int32 [4, 65536], P('region', 'nets'), may hold values from 0 to 2
Outputs:
- logit_grad: float32 [8192, 256], P('nets')
- usage: float32 [4, 65536], P('region', 'nets')
Inputs may be any that keep to these rules, and one draw needn't show every extreme that they name: `tile_counts`: each entry is at most 48; in every draw some owner receives 48 live slots from every group of a region, and every group has a full owner in every region.
All inputs are finite; a program needn't handle non-finite values.
Results may differ from a plain program's by a relative error of at most 0.0011.
Values may be sent and summed in bfloat16 or wider, within the bound.
No kernel may reach another device: no remote copies, remote signals or barrier semaphores. Data moves between devices by JAX's collectives and lax.ppermute only.
A program may use at most 64 MiB of HBM per device.

v0:
```python
import jax
import jax.numpy as jnp
from jax import lax
from jax.sharding import PartitionSpec as P


def shards(logits, tile_values, tile_pattern, tile_edge, tile_counts, capacity):
    groups = lax.axis_size("nets")
    tile_block = tile_values[0, 0]
    tile_count = tile_block.shape[0]
    block_size = tile_block.shape[1]
    slot_count = tile_count // groups
    pattern_idx = tile_pattern[0, 0]
    edge_idx = tile_edge[0, 0]
    counts = tile_counts[0, 0]
    live_slot = (jnp.arange(slot_count, dtype=jnp.int32)[None, :] < counts[:, None]).reshape(
        tile_count
    )
    weight_live = live_slot.astype(jnp.float32)
    probs = jax.nn.softmax(logits, axis=-1)
    probs_half = probs.astype(jnp.bfloat16).reshape(-1, block_size)
    picked = probs_half[pattern_idx]
    contrib = (
        jnp.einsum("tq,tqe->te", picked, tile_block, preferred_element_type=jnp.float32)
        * weight_live[:, None]
    )
    capacity_f = capacity.reshape(-1, block_size).astype(jnp.float32)
    owned_blocks = capacity_f.shape[0]
    owner_idx = jnp.arange(tile_count, dtype=jnp.int32) // slot_count
    target = owner_idx * owned_blocks + edge_idx
    partial_value = (
        jnp.zeros((groups * owned_blocks, block_size), jnp.float32).at[target].add(contrib)
    )
    usage_edges = lax.psum_scatter(partial_value, "nets", scatter_dimension=0, tiled=True)
    edge_grad = jax.nn.sigmoid(usage_edges - capacity_f).astype(jnp.bfloat16)
    all_grads = lax.all_gather(edge_grad, "nets", axis=0, tiled=True)
    slot_grads = all_grads[target]
    dp_tiles = (
        jnp.einsum("tqe,te->tq", tile_block, slot_grads, preferred_element_type=jnp.float32)
        * weight_live[:, None]
    )
    local_grad = (
        jnp.zeros((probs_half.shape[0], block_size), jnp.float32).at[pattern_idx].add(dp_tiles)
    )
    summed_grad = lax.psum(local_grad.reshape(logits.shape), "region")
    logit_grad = probs * (summed_grad - jnp.sum(probs * summed_grad, axis=-1, keepdims=True))
    return (logit_grad, usage_edges.reshape(capacity.shape))


def solution(mesh):
    in_specs = (
        P("nets", None),
        P("nets", "region", None, None, None),
        P("nets", "region", None),
        P("nets", "region", None),
        P("nets", "region", None),
        P("region", "nets"),
    )
    out_specs = (P("nets", None), P("region", "nets"))
    return jax.shard_map(shards, mesh=mesh, in_specs=in_specs, out_specs=out_specs, check_vma=False)
```

profile of v0, /device:TPU:0, one launch (start us, length us, event | category | flops | bytes accessed | tf_op | source)
XLA Modules:
  0.0 181.1 jit_solution(4683535861114849851)
XLA Ops:
  7.2 0.0 reduce-scatter.2.cloned.1.call-start
  7.2 0.7 fusion.17
  7.9 0.7 fusion.18
  8.6 1.4 reduce_max.9
  10.1 1.6 fusion.5
  11.7 0.7 fusion.16
  12.4 0.1 reshape.122
  12.5 1.6 fusion.21
  14.1 0.2 reshape.119
  14.2 1.4 gather_fusion
  15.7 6.4 %fusion.2 = f32[384,1,128]{2,1,0:T(1,128)S(1)} fusion(bf16[1,1,384,128,128]{4,3,2,1,0:T(8,128)(2,1)} %param.7, bf16[384,128,1]{1,0,2:T(8,128)(2,1)S(1)} %bitcast.18), kind=kOutput, calls=%fused_computation.6 | convolution fusion | flops 12582912 | bytes 12877824 | tf_op jit(solution)/shard_map/tq,tqe->te/dot_general | solution.py:24
  22.1 2.6 %scatter_custom_fusion = f32[512,128]{1,0:T(8,128)} fusion(s32[384]{0:T(512)S(1)} %fusion.18, f32[384,128]{1,0:T(8,128)S(1)} %bitcast.19, f32[]{:T(128)} %constant.11.clone.1, f32[384]{0:T(512)S(1)} %reshape.122), kind=kCustom, calls=%fused_computation.18 | custom fusion | flops 98304 | bytes 460804 | tf_op jit(solution)/shard_map/scatter-add | solution.py:32
  24.7 0.0 reduce-scatter.2.cloned.1.call-update
  24.7 0.0 all-reduce.2.cloned.1.call-start
  24.8 64.0 %reduce-scatter.2.cloned.1.call-done = f32[64,128]{1,0:T(8,128)} async-done(((f32[512,128]{1,0:T(8,128)}), f32[64,128]{1,0:T(8,128)}) %reduce-scatter.2.cloned.1.call-update) | async-done | bytes 32784 | tf_op jit(solution)/shard_map/reduce_scatter | solution.py:34
  88.8 0.8 divide_convert_fusion
  89.6 30.5 %all_gather.3 = bf16[512,128]{1,0:T(8,128)(2,1)S(1)} all-gather(bf16[64,128]{1,0:T(8,128)(2,1)S(1)} %divide_convert_fusion), channel_id=1, replica_groups=mesh['nets'=8,'region'=4] {'nets'}, dimensions={0}, use_global_device_ids=true | all-gather | bytes 147456 | tf_op jit(solution)/shard_map/all_gather | solution.py:36
  120.1 1.4 gather_fusion.1
  121.6 9.5 %fusion = f32[384,1,128]{2,1,0:T(1,128)S(1)} fusion(bf16[1,1,384,128,128]{4,3,2,1,0:T(8,128)(2,1)} %param.7, bf16[384,128,1]{1,0,2:T(8,128)(2,1)S(1)} %bitcast.20), kind=kOutput, calls=%fused_computation.4 | convolution fusion | flops 12582912 | bytes 12877824 | tf_op jit(solution)/shard_map/tqe,te->tq/dot_general | solution.py:39
  131.0 2.2 %scatter_custom_fusion.1 = f32[2048,128]{1,0:T(8,128)S(1)} fusion(s32[384]{0:T(512)S(1)} %fusion.17, f32[]{:T(128)} %constant.11.clone.1, f32[384,128]{1,0:T(8,128)S(1)} %bitcast.21, f32[384]{0:T(512)S(1)} %reshape.122), kind=kCustom, calls=%fused_computation.13 | custom fusion | flops 98304 | bytes 1247236 | tf_op jit(solution)/shard_map/scatter-add | solution.py:43
  133.3 1.3 reshape.120
  134.6 35.3 %all-reduce.2.cloned.1.call-done = f32[1024,256]{1,0:T(8,128)} async-done(((f32[1024,256]{1,0:T(8,128)}), f32[1024,256]{1,0:T(8,128)}) %all-reduce.2.cloned.1.call-update) | async-done | bytes 1048592 | tf_op jit(solution)/shard_map/psum | solution.py:45
  169.8 1.7 multiply_reduce_fusion
  171.6 2.7 %subtract_multiply_fusion = f32[1024,256]{1,0:T(8,128)} fusion(f32[1024,256]{1,0:T(8,128)} %all-reduce.2.cloned.1.call-done, f32[1024]{0:T(1024)S(1)} %multiply_reduce_fusion, f32[1024]{0:T(1024)S(1)} %fusion.5, f32[1024,256]{1,0:T(8,128)S(1)} %copy-done, f32[1024]{0:T(1024)S(1)} %reduce_max.9), kind=kLoop, calls=%fused_computation.8 | loop fusion | flops 1048576 | bytes 3158016 | tf_op jit(solution)/shard_map/mul | solution.py:46
  (8 shorter events, 0.1 us)
Async XLA Ops:
  7.2 81.7 %reduce-scatter.2.cloned.1.call-start = ((), (), s32[]{:S(2)}) async-start(), calls=%async_computation.1 | async-start | bytes 294912 | tf_op jit(solution)/shard_map/reduce_scatter | solution.py:34
  14.0 10.7 %copy-start.1 = (s32[1,8192]{1,0:T(1,128)S(1)}, s32[1,8192]{1,0:T(1,128)}, u32[]{:S(2)}) copy-start(s32[1,8192]{1,0:T(1,128)} %param.11) | copy-start | bytes 98308
  22.1 147.8 %copy-start = (f32[1024,256]{1,0:T(8,128)S(1)}, f32[1024,256]{1,0:T(8,128)}, u32[]{:S(2)}) copy-start(f32[1024,256]{1,0:T(8,128)} %param.6) | copy-start | bytes 3145732
  24.7 145.1 %all-reduce.2.cloned.1.call-start = ((), (), s32[]{:S(2)}) async-start(), calls=%async_computation.2 | async-start | bytes 2097152 | tf_op jit(solution)/shard_map/psum | solution.py:45
Sparse Core Ops, SparseCore 0:
  24.8 63.9 reduce-scatter.1
  134.7 35.1 all-reduce.1
where the time goes:
time: 182 us; the launch traced here: 181 us
  waiting for transfers between devices  99.3 us (55%)
  blocking collectives  30.5 us (17%)
  other arithmetic  16.8 us (9%)
  matrix products  15.8 us (9%)
  between operations  14.1 us (8%)
  local copies, waits for them, and re-layouts  4.42 us (2%)
    reduce_scatter x1, waiting for transfers between devices, shards(): lax.psum_scatter(partial_value, 'nets', scatter_dimension=0, tiled=True)  64 us
    psum x1, waiting for transfers between devices, shards(): summed_grad = lax.psum(local_grad.reshape(logits.shape), 'region')  35.3 us
    all_gather x1, blocking collectives, shards(): all_grads = lax.all_gather(edge_grad, 'nets', axis=0, tiled=True)  30.5 us
    dot_general x1, matrix products, shards(): jnp.einsum('tqe,te->tq', tile_block, slot_grads, preferred_element_type=j...  9.46 us
    dot_general x1, matrix products, shards(): jnp.einsum('tq,tqe->te', picked, tile_block, preferred_element_type=jnp.f...  6.35 us
  transfers between devices with their start and end apart: 2, of which 2 were waited for; matrix products, arithmetic and copies ran while one was open for 0% of the time, Pallas kernels for 0%

commit v1 on v0

--- a/solution.py
+++ b/solution.py
@@ -31,18 +31,33 @@
     partial_value = (
         jnp.zeros((groups * owned_blocks, block_size), jnp.float32).at[target].add(contrib)
     )
-    usage_edges = lax.psum_scatter(partial_value, "nets", scatter_dimension=0, tiled=True)
+    received = lax.all_to_all(
+        partial_value.reshape(groups, owned_blocks, block_size), "nets", 0, 0, tiled=False
+    )
+    usage_edges = jnp.sum(received, axis=0)
     edge_grad = jax.nn.sigmoid(usage_edges - capacity_f).astype(jnp.bfloat16)
-    all_grads = lax.all_gather(edge_grad, "nets", axis=0, tiled=True)
+    spread = jnp.broadcast_to(edge_grad[None], (groups, owned_blocks, block_size))
+    all_grads = lax.all_to_all(spread, "nets", 0, 0, tiled=False).reshape(-1, block_size)
     slot_grads = all_grads[target]
     dp_tiles = (
         jnp.einsum("tqe,te->tq", tile_block, slot_grads, preferred_element_type=jnp.float32)
         * weight_live[:, None]
     )
-    local_grad = (
-        jnp.zeros((probs_half.shape[0], block_size), jnp.float32).at[pattern_idx].add(dp_tiles)
+    idx_rows = -(-tile_count // block_size)
+    idx_f = jnp.zeros((idx_rows * block_size,), jnp.float32).at[:tile_count].set(
+        pattern_idx.astype(jnp.float32)
     )
-    summed_grad = lax.psum(local_grad.reshape(logits.shape), "region")
+    packed = jnp.concatenate([dp_tiles, idx_f.reshape(idx_rows, block_size)], axis=0)
+    gathered = lax.all_gather(packed, "region", axis=0, tiled=False)
+    all_dp = gathered[:, :tile_count].reshape(-1, block_size)
+    all_idx = (
+        gathered[:, tile_count:].reshape(gathered.shape[0], -1)[:, :tile_count]
+        .astype(jnp.int32)
+        .reshape(-1)
+    )
+    summed_grad = (
+        jnp.zeros((probs_half.shape[0], block_size), jnp.float32).at[all_idx].add(all_dp)
+    ).reshape(logits.shape)
     logit_grad = probs * (summed_grad - jnp.sum(probs * summed_grad, axis=-1, keepdims=True))
     return (logit_grad, usage_edges.reshape(capacity.shape))
 

time: 182 us -> 77.6 us (0.43)
  waiting for transfers between devices: 99.3 us -> 16.2 us
  blocking collectives: 30.5 us -> 8.72 us
  between operations: 14.1 us -> 0.79 us
  starting transfers between devices: 0.08 us -> 10.8 us
  other arithmetic: 16.8 us -> 20.6 us
    reduce_scatter x1 -> x0, waiting for transfers between devices: 64 us -> none  [shards(): lax.psum_scatter(partial_value, 'nets', scatter_dimension=0, tiled=True)]
    psum x1 -> x0, waiting for transfers between devices: 35.3 us -> none  [shards(): summed_grad = lax.psum(local_grad.reshape(logits.shape), 'region')]
    all_gather x1, blocking collectives: 30.5 us -> 8.72 us  [shards(): gathered = lax.all_gather(packed, 'region', axis=0, tiled=False)]
    all_to_all x0 -> x2, waiting for transfers between devices: none -> 16.2 us  [the longest x1 8.88 us: shards(): lax.all_to_all(partial_value.reshape(groups, owned_blocks, block_size), '...]
    all_to_all x0 -> x2, starting transfers between devices: none -> 10.8 us  [the longest x1 7.25 us: shards(): lax.all_to_all(partial_value.reshape(groups, owned_blocks, block_size), '...]
    scatter-add x1, other arithmetic: 2.23 us -> 9 us  [shards(): jnp.zeros((probs_half.shape[0], block_size), jnp.float32).at[all_idx]]
where the time goes in v1:
time: 77.6 us; the launch traced here: 77.1 us
  other arithmetic  20.6 us (27%)
  waiting for transfers between devices  16.2 us (21%)
  matrix products  15.8 us (20%)
  starting transfers between devices  10.8 us (14%)
  blocking collectives  8.72 us (11%)
  local copies, waits for them, and re-layouts  4.2 us (5%)
  between operations  0.79 us (1%)
    dot_general x1, matrix products, shards(): jnp.einsum('tqe,te->tq', tile_block, slot_grads, preferred_element_type=j...  9.46 us
    scatter-add x1, other arithmetic, shards(): jnp.zeros((probs_half.shape[0], block_size), jnp.float32).at[all_idx]  9 us
    all_to_all x1, waiting for transfers between devices, shards(): lax.all_to_all(partial_value.reshape(groups, owned_blocks, block_size), '...  8.88 us
    all_gather x1, blocking collectives, shards(): gathered = lax.all_gather(packed, 'region', axis=0, tiled=False)  8.72 us
    all_to_all x1, waiting for transfers between devices, shards(): lax.all_to_all(spread, 'nets', 0, 0, tiled=False).reshape(-1, block_size)  7.3 us
    all_to_all x1, starting transfers between devices, shards(): lax.all_to_all(partial_value.reshape(groups, owned_blocks, block_size), '...  7.25 us
    dot_general x1, matrix products, shards(): jnp.einsum('tq,tqe->te', picked, tile_block, preferred_element_type=jnp.f...  6.35 us
    all_to_all x1, starting transfers between devices, shards(): lax.all_to_all(spread, 'nets', 0, 0, tiled=False).reshape(-1, block_size)  3.59 us
  transfers between devices with their start and end apart: 2, of which 2 were waited for; matrix products, arithmetic and copies ran while one was open for 0% of the time, Pallas kernels for 0%

profile of v1, /device:TPU:0, one launch (start us, length us, event | category | flops | bytes accessed | tf_op | source)
XLA Modules:
  0.0 77.1 jit_solution(17821637135317472664)
XLA Ops:
  0.6 0.7 fusion.16
  1.3 0.7 fusion.17
  2.0 1.4 %reduce_max.9 = f32[1024]{0:T(1024)S(1)} reduce(f32[1024,256]{1,0:T(8,128)} %param.10, f32[]{:T(128)} %constant.52.clone.1), dimensions={1}, to_apply=%region_0.0 | reduce | flops 261120 | bytes 1052676 | tf_op jit(solution)/shard_map/reduce_max | solution.py:20
  3.5 1.6 %fusion.5 = f32[1024]{0:T(1024)S(1)} fusion(f32[1024,256]{1,0:T(8,128)} %param.10, f32[1024]{0:T(1024)S(1)} %reduce_max.9), kind=kLoop, calls=%fused_computation.12 | loop fusion | flops 523264 | bytes 1056768 | tf_op jit(solution)/shard_map/reduce_sum | solution.py:20
  5.1 0.7 fusion.15
  5.8 0.1 reshape.201
  5.9 1.6 %fusion.20 = bf16[1024,256]{1,0:T(8,128)(2,1)S(1)} fusion(f32[1024]{0:T(1024)S(1)} %fusion.5, f32[1024,256]{1,0:T(8,128)} %param.10, f32[1024]{0:T(1024)S(1)} %reduce_max.9), kind=kLoop, calls=%fused_computation.42 | loop fusion | flops 786432 | bytes 1581056 | tf_op jit(solution)/shard_map/convert_element_type | solution.py:21
  7.5 0.2 reshape.195
  7.7 1.4 %gather_fusion = bf16[384,128]{1,0:T(8,128)(2,1)S(1)} fusion(bf16[2048,128]{1,0:T(8,128)(2,1)S(1)} %reshape.195, s32[1024]{0:T(1024)S(1)} %pad_clamp_fusion.1), kind=kCustom, calls=%fused_computation | custom fusion | bytes 198144 | tf_op jit(solution)/shard_map/gather | solution.py:22
  9.1 6.4 %fusion.2 = f32[384,1,128]{2,1,0:T(1,128)S(1)} fusion(bf16[1,1,384,128,128]{4,3,2,1,0:T(8,128)(2,1)} %param.11, bf16[384,128,1]{1,0,2:T(8,128)(2,1)S(1)} %bitcast.25), kind=kOutput, calls=%fused_computation.6 | convolution fusion | flops 12582912 | bytes 12877824 | tf_op jit(solution)/shard_map/tq,tqe->te/dot_general | solution.py:24
  15.5 2.6 %scatter_custom_fusion = f32[512,128]{1,0:T(8,128)} fusion(s32[384]{0:T(512)S(1)} %fusion.16, f32[384,128]{1,0:T(8,128)S(1)} %bitcast.26, f32[]{:T(128)} %constant.53.clone.1, f32[384]{0:T(512)S(1)} %reshape.201), kind=kCustom, calls=%fused_computation.18 | custom fusion | flops 98304 | bytes 460804 | tf_op jit(solution)/shard_map/scatter-add | solution.py:32
  18.1 7.3 %all-to-all-start = ((f32[8,64,128]{2,1,0:T(8,128)}), f32[8,64,128]{2,1,0:T(8,128)S(1)}, u32[]{:S(2)}, u32[]{:S(2)}) async-start(f32[8,64,128]{2,1,0:T(8,128)} %bitcast.7), calls=%async_computation | async-start | bytes 524288 | tf_op jit(solution)/shard_map/all_to_all | solution.py:34
  25.4 8.9 %all-to-all-done = f32[8,64,128]{2,1,0:T(8,128)S(1)} async-done(((f32[8,64,128]{2,1,0:T(8,128)}), f32[8,64,128]{2,1,0:T(8,128)S(1)}, u32[]{:S(2)}, u32[]{:S(2)}) %all-to-all-start) | async-done | bytes 262176 | tf_op jit(solution)/shard_map/all_to_all | solution.py:34
  34.3 0.7 broadcast_in_dim.8
  35.0 3.6 %all-to-all-start.1 = ((bf16[8,64,128]{2,1,0:T(8,128)(2,1)}), bf16[8,64,128]{2,1,0:T(8,128)(2,1)S(1)}, u32[]{:S(2)}, u32[]{:S(2)}) async-start(bf16[8,64,128]{2,1,0:T(8,128)(2,1)} %broadcast_in_dim.8), calls=%async_computation.1 | async-start | bytes 262144 | tf_op jit(solution)/shard_map/all_to_all | solution.py:40
  38.6 7.3 %all-to-all-done.1 = bf16[8,64,128]{2,1,0:T(8,128)(2,1)S(1)} async-done(((bf16[8,64,128]{2,1,0:T(8,128)(2,1)}), bf16[8,64,128]{2,1,0:T(8,128)(2,1)S(1)}, u32[]{:S(2)}, u32[]{:S(2)}) %all-to-all-start.1) | async-done | bytes 131104 | tf_op jit(solution)/shard_map/all_to_all | solution.py:40
  45.9 1.4 %gather_fusion.1 = bf16[384,128]{1,0:T(8,128)(2,1)S(1)} fusion(bf16[512,128]{1,0:T(8,128)(2,1)S(1)} %bitcast.24, s32[1024]{0:T(1024)S(1)} %pad_clamp_fusion), kind=kCustom, calls=%fused_computation.1 | custom fusion | bytes 198144 | tf_op jit(solution)/shard_map/gather | solution.py:41
  47.4 9.5 %fusion = f32[384,1,128]{2,1,0:T(1,128)S(1)} fusion(bf16[1,1,384,128,128]{4,3,2,1,0:T(8,128)(2,1)} %param.11, bf16[384,128,1]{1,0,2:T(8,128)(2,1)S(1)} %bitcast.27), kind=kOutput, calls=%fused_computation.4 | convolution fusion | flops 12582912 | bytes 12877824 | tf_op jit(solution)/shard_map/tqe,te->tq/dot_general | solution.py:43
  56.9 0.1 broadcast_multiply_fusion
  57.0 8.7 %all-gather.1 = f32[4,387,128]{2,1,0:T(8,128)S(1)} all-gather(f32[1,387,128]{2,1,0:T(8,128)S(1)} %maximum_bitcast_fusion), channel_id=2, replica_groups=mesh['nets'=8,'region'=4] {'region'}, dimensions={0}, use_global_device_ids=true | all-gather | bytes 990720 | tf_op jit(solution)/shard_map/all_gather | solution.py:51
  65.9 9.0 %scatter_custom_fusion.1 = f32[2048,128]{1,0:T(8,128)S(1)} fusion(s32[1536]{0:T(1024)S(1)} %fusion.14, f32[1536,128]{1,0:T(8,128)S(1)} %bitcast.28, f32[]{:T(128)} %constant.53.clone.1), kind=kCustom, calls=%fused_computation.13 | custom fusion | flops 196608 | bytes 1048580 | tf_op jit(solution)/shard_map/scatter-add | solution.py:59
  74.9 0.3 reshape.199
  75.2 0.5 multiply_reduce_fusion
  75.7 1.4 %subtract_multiply_fusion = f32[1024,256]{1,0:T(8,128)} fusion(f32[1024,256]{1,0:T(8,128)S(1)} %reshape.199, f32[1024]{0:T(1024)S(1)} %multiply_reduce_fusion, f32[1024]{0:T(1024)S(1)} %fusion.5, f32[1024,256]{1,0:T(8,128)S(1)} %copy-done, f32[1024]{0:T(1024)S(1)} %reduce_max.9), kind=kLoop, calls=%fused_computation.8 | loop fusion | flops 1048576 | bytes 3158016 | tf_op jit(solution)/shard_map/mul | solution.py:61
  (19 shorter events, 0.2 us)
Async XLA Ops:
  7.5 17.9 %copy-start.2 = (s32[1,8192]{1,0:T(1,128)S(1)}, s32[1,8192]{1,0:T(1,128)}, u32[]{:S(2)}) copy-start(s32[1,8192]{1,0:T(1,128)} %param.15) | copy-start | bytes 98308
  7.7 31.0 %copy-start.3 = (s32[1,1,384]{2,1,0:T(1,128)S(1)}, s32[1,1,384]{2,1,0:T(1,128)}, u32[]{:S(2)}) copy-start(s32[1,1,384]{2,1,0:T(1,128)} %param.12) | copy-start | bytes 4612
  15.5 59.7 %copy-start = (f32[1024,256]{1,0:T(8,128)S(1)}, f32[1024,256]{1,0:T(8,128)}, u32[]{:S(2)}) copy-start(f32[1024,256]{1,0:T(8,128)} %param.10) | copy-start | bytes 3145732
  18.1 16.2 %all-to-all-start = ((f32[8,64,128]{2,1,0:T(8,128)}), f32[8,64,128]{2,1,0:T(8,128)S(1)}, u32[]{:S(2)}, u32[]{:S(2)}) async-start(f32[8,64,128]{2,1,0:T(8,128)} %bitcast.7), calls=%async_computation | async-start | bytes 524288 | tf_op jit(solution)/shard_map/all_to_all | solution.py:34
  34.3 42.8 %copy-start.1 = (f32[64,128]{1,0:T(8,128)}, f32[64,128]{1,0:T(8,128)S(1)}, u32[]{:S(2)}) copy-start(f32[64,128]{1,0:T(8,128)S(1)} %reduce_sum.28) | copy-start | bytes 98308
  35.0 10.9 %all-to-all-start.1 = ((bf16[8,64,128]{2,1,0:T(8,128)(2,1)}), bf16[8,64,128]{2,1,0:T(8,128)(2,1)S(1)}, u32[]{:S(2)}, u32[]{:S(2)}) async-start(bf16[8,64,128]{2,1,0:T(8,128)(2,1)} %broadcast_in_dim.8), calls=%async_computation.1 | async-start | bytes 262144 | tf_op jit(solution)/shard_map/all_to_all | solution.py:40

commit v2 on v1

--- a/solution.py
+++ b/solution.py
@@ -2,6 +2,29 @@
 import jax.numpy as jnp
 from jax import lax
 from jax.sharding import PartitionSpec as P
+
+
+def _one_hot(idx, size, dtype):
+    return (idx[:, None] == jnp.arange(size, dtype=jnp.int32)[None, :]).astype(dtype)
+
+
+def _take_rows(table, idx):
+    sel = _one_hot(idx, table.shape[0], table.dtype)
+    return jnp.dot(sel, table, preferred_element_type=jnp.float32).astype(table.dtype)
+
+
+def _add_rows(idx, rows, size):
+    hi = lax.reduce_precision(rows, exponent_bits=8, mantissa_bits=7)
+    rest = rows - hi
+    mid = lax.reduce_precision(rest, exponent_bits=8, mantissa_bits=7)
+    lo = rest - mid
+    parts = jnp.concatenate([hi, mid, lo], axis=1).astype(jnp.bfloat16)
+    sel = _one_hot(idx, size, jnp.bfloat16)
+    out = lax.dot_general(
+        sel, parts, (((0,), (0,)), ((), ())), preferred_element_type=jnp.float32
+    )
+    width = rows.shape[1]
+    return out[:, :width] + out[:, width : 2 * width] + out[:, 2 * width :]
 
 
 def shards(logits, tile_values, tile_pattern, tile_edge, tile_counts, capacity):
@@ -19,7 +42,7 @@
     weight_live = live_slot.astype(jnp.float32)
     probs = jax.nn.softmax(logits, axis=-1)
     probs_half = probs.astype(jnp.bfloat16).reshape(-1, block_size)
-    picked = probs_half[pattern_idx]
+    picked = _take_rows(probs_half, pattern_idx)
     contrib = (
         jnp.einsum("tq,tqe->te", picked, tile_block, preferred_element_type=jnp.float32)
         * weight_live[:, None]
@@ -28,9 +51,7 @@
     owned_blocks = capacity_f.shape[0]
     owner_idx = jnp.arange(tile_count, dtype=jnp.int32) // slot_count
     target = owner_idx * owned_blocks + edge_idx
-    partial_value = (
-        jnp.zeros((groups * owned_blocks, block_size), jnp.float32).at[target].add(contrib)
-    )
+    partial_value = _add_rows(target, contrib, groups * owned_blocks)
     received = lax.all_to_all(
         partial_value.reshape(groups, owned_blocks, block_size), "nets", 0, 0, tiled=False
     )
@@ -38,7 +59,7 @@
     edge_grad = jax.nn.sigmoid(usage_edges - capacity_f).astype(jnp.bfloat16)
     spread = jnp.broadcast_to(edge_grad[None], (groups, owned_blocks, block_size))
     all_grads = lax.all_to_all(spread, "nets", 0, 0, tiled=False).reshape(-1, block_size)
-    slot_grads = all_grads[target]
+    slot_grads = _take_rows(all_grads, target)
     dp_tiles = (
         jnp.einsum("tqe,te->tq", tile_block, slot_grads, preferred_element_type=jnp.float32)
         * weight_live[:, None]
@@ -55,9 +76,7 @@
         .astype(jnp.int32)
         .reshape(-1)
     )
-    summed_grad = (
-        jnp.zeros((probs_half.shape[0], block_size), jnp.float32).at[all_idx].add(all_dp)
-    ).reshape(logits.shape)
+    summed_grad = _add_rows(all_idx, all_dp, probs_half.shape[0]).reshape(logits.shape)
     logit_grad = probs * (summed_grad - jnp.sum(probs * summed_grad, axis=-1, keepdims=True))
     return (logit_grad, usage_edges.reshape(capacity.shape))
 

time: 77.6 us -> 70.7 us (0.911)
  other arithmetic: 20.6 us -> 10.1 us
  matrix products: 15.8 us -> 21.2 us
  local copies, waits for them, and re-layouts: 4.2 us -> 2.07 us
    scatter-add x2 -> x0, other arithmetic: 11.6 us -> none  [the longest x1 9 us: shards(): jnp.zeros((probs_half.shape[0], block_size), jnp.float32).at[all_idx]]
    dot_general x0 -> x4, matrix products: none -> 5.41 us  [the longest x2 4.41 us: _add_rows(): lax.dot_general(sel, parts, (((0,), (0,)), ((), ())), preferred_element_t...]
    gather x2 -> x0, local copies, waits for them, and re-layouts: 2.89 us -> none  [the longest x1 1.45 us: shards(): picked = probs_half[pattern_idx]]
    select_n x3 -> x0, other arithmetic: 1.43 us -> none  [the longest x1 0.71 us: shards(): jnp.zeros((groups * owned_blocks, block_size), jnp.float32).at[target]]
    unnamed x1 -> x3, other arithmetic: 0.02 us -> 1.41 us
    add x0 -> x3, other arithmetic: none -> 0.89 us  [the longest x2 0.88 us: _add_rows(): return out[:, :width] + out[:, width:2 * width] + out[:, 2 * width:]]
where the time goes in v2:
time: 70.7 us; the launch traced here: 70.2 us
  matrix products  21.2 us (30%)
  waiting for transfers between devices  16.2 us (23%)
  starting transfers between devices  10.8 us (15%)
  other arithmetic  10.1 us (14%)
  blocking collectives  8.9 us (13%)
  local copies, waits for them, and re-layouts  2.07 us (3%)
  between operations  0.79 us (1%)
    dot_general x1, matrix products, shards(): jnp.einsum('tqe,te->tq', tile_block, slot_grads, preferred_element_type=j...  9.46 us
    all_gather x1, blocking collectives, shards(): gathered = lax.all_gather(packed, 'region', axis=0, tiled=False)  8.9 us
    all_to_all x1, waiting for transfers between devices, shards(): lax.all_to_all(partial_value.reshape(groups, owned_blocks, block_size), '...  8.88 us
    all_to_all x1, waiting for transfers between devices, shards(): lax.all_to_all(spread, 'nets', 0, 0, tiled=False).reshape(-1, block_size)  7.32 us
    all_to_all x1, starting transfers between devices, shards(): lax.all_to_all(partial_value.reshape(groups, owned_blocks, block_size), '...  7.25 us
    dot_general x1, matrix products, shards(): jnp.einsum('tq,tqe->te', picked, tile_block, preferred_element_type=jnp.f...  6.36 us
    dot_general x2, matrix products, _add_rows(): lax.dot_general(sel, parts, (((0,), (0,)), ((), ())), preferred_element_t...  4.41 us
    all_to_all x1, starting transfers between devices, shards(): lax.all_to_all(spread, 'nets', 0, 0, tiled=False).reshape(-1, block_size)  3.59 us
  transfers between devices with their start and end apart: 2, of which 2 were waited for; matrix products, arithmetic and copies ran while one was open for 0% of the time, Pallas kernels for 0%

profile of v2, /device:TPU:0, one launch (start us, length us, event | category | flops | bytes accessed | tf_op | source)
XLA Modules:
  0.0 70.2 jit_solution(5227790056655657682)
XLA Ops:
  0.6 0.7 reduce.2
  1.3 0.7 reduce.3
  2.0 1.4 %reduce_max.9 = f32[1024]{0:T(1024)S(1)} reduce(f32[1024,256]{1,0:T(8,128)} %param.10, f32[]{:T(128)} %constant.45.clone.1), dimensions={1}, to_apply=%region_0.0 | reduce | flops 261120 | bytes 1052676 | tf_op jit(solution)/shard_map/reduce_max | solution.py:43
  3.5 1.6 %fusion.17 = f32[1024]{0:T(1024)S(1)} fusion(f32[1024,256]{1,0:T(8,128)} %param.10, f32[1024]{0:T(1024)S(1)} %reduce_max.9), kind=kLoop, calls=%fused_computation.29 | loop fusion | flops 523264 | bytes 1056768 | tf_op jit(solution)/shard_map/reduce_sum | solution.py:43
  5.1 0.7 %fusion.30 = f32[8,48]{1,0:T(8,128)S(1)} fusion(s32[8]{0:T(128)} %bitcast.36), kind=kLoop, calls=%fused_computation.57 | loop fusion | flops 768 | bytes 1568 | tf_op jit(solution)/shard_map/convert_element_type | solution.py:42
  5.9 1.6 %fusion.38 = bf16[1024,256]{1,0:T(8,128)(2,1)S(1)} fusion(f32[1024]{0:T(1024)S(1)} %fusion.17, f32[1024,256]{1,0:T(8,128)} %param.10, f32[1024]{0:T(1024)S(1)} %reduce_max.9), kind=kLoop, calls=%fused_computation.67 | loop fusion | flops 786432 | bytes 1581056 | tf_op jit(solution)/shard_map/convert_element_type | solution.py:44
  7.6 0.7 fusion.14
  8.3 6.4 %fusion.2 = f32[384,1,128]{2,1,0:T(1,128)S(1)} fusion(bf16[1,1,384,128,128]{4,3,2,1,0:T(8,128)(2,1)} %param.11, bf16[384,128,1]{1,0,2:T(8,128)(2,1)S(1)} %fusion.14), kind=kOutput, calls=%fused_computation.2 | convolution fusion | flops 12582912 | bytes 12877824 | tf_op jit(solution)/shard_map/tq,tqe->te/dot_general | solution.py:47
  14.8 0.5 fusion.19
  15.4 0.7 %slice_add_fusion.2 = f32[512,128]{1,0:T(8,128)} fusion(f32[512,384]{1,0:T(8,128)S(1)} %fusion.19), kind=kLoop, calls=%fused_computation.44 | loop fusion | flops 131072 | bytes 1048576 | tf_op jit(solution)/shard_map/add | solution.py:27
  16.1 7.3 %all-to-all-start = ((f32[8,64,128]{2,1,0:T(8,128)}), f32[8,64,128]{2,1,0:T(8,128)S(1)}, u32[]{:S(2)}, u32[]{:S(2)}) async-start(f32[8,64,128]{2,1,0:T(8,128)} %bitcast.5), calls=%async_computation | async-start | bytes 524288 | tf_op jit(solution)/shard_map/all_to_all | solution.py:55
  23.4 8.9 %all-to-all-done = f32[8,64,128]{2,1,0:T(8,128)S(1)} async-done(((f32[8,64,128]{2,1,0:T(8,128)}), f32[8,64,128]{2,1,0:T(8,128)S(1)}, u32[]{:S(2)}, u32[]{:S(2)}) %all-to-all-start) | async-done | bytes 262176 | tf_op jit(solution)/shard_map/all_to_all | solution.py:55
  32.4 0.7 broadcast_in_dim.2
  33.0 3.6 %all-to-all-start.1 = ((bf16[8,64,128]{2,1,0:T(8,128)(2,1)}), bf16[8,64,128]{2,1,0:T(8,128)(2,1)S(1)}, u32[]{:S(2)}, u32[]{:S(2)}) async-start(bf16[8,64,128]{2,1,0:T(8,128)(2,1)} %broadcast_in_dim.2), calls=%async_computation.1 | async-start | bytes 262144 | tf_op jit(solution)/shard_map/all_to_all | solution.py:61
  36.7 7.3 %all-to-all-done.1 = bf16[8,64,128]{2,1,0:T(8,128)(2,1)S(1)} async-done(((bf16[8,64,128]{2,1,0:T(8,128)(2,1)}), bf16[8,64,128]{2,1,0:T(8,128)(2,1)S(1)}, u32[]{:S(2)}, u32[]{:S(2)}) %all-to-all-start.1) | async-done | bytes 131104 | tf_op jit(solution)/shard_map/all_to_all | solution.py:61
  44.0 0.3 fusion.15
  44.3 9.5 %fusion = f32[384,1,128]{2,1,0:T(1,128)S(1)} fusion(bf16[1,1,384,128,128]{4,3,2,1,0:T(8,128)(2,1)} %param.11, bf16[384,128,1]{1,0,2:T(8,128)(2,1)S(1)} %fusion.15), kind=kOutput, calls=%fused_computation | convolution fusion | flops 12582912 | bytes 12877824 | tf_op jit(solution)/shard_map/tqe,te->tq/dot_general | solution.py:64
  53.9 8.9 %all-gather.1 = f32[4,387,128]{2,1,0:T(8,128)S(1)} all-gather(f32[1,387,128]{2,1,0:T(8,128)S(1)} %maximum_bitcast_fusion), channel_id=2, replica_groups=mesh['nets'=8,'region'=4] {'region'}, dimensions={0}, use_global_device_ids=true | all-gather | bytes 990720 | tf_op jit(solution)/shard_map/all_gather | solution.py:72
  62.9 0.2 reduce-precision_convert_fusion.1
  63.1 3.9 %fusion.4 = f32[2048,384]{1,0:T(8,128)S(1)} fusion(s32[1536]{0:T(1024)S(1)} %convert_element_type.73, bf16[1536,128]{1,0:T(8,128)(2,1)S(1)} %get-tuple-element.23, bf16[1536,128]{1,0:T(8,128)(2,1)S(1)} %get-tuple-element.24, bf16[1536,128]{1,0:T(8,128)(2,1)S(1)} %get-tuple-element.22), kind=kOutput, calls=%fused_computation.5 | convolution fusion | flops 2422603776 | bytes 4331520 | tf_op jit(solution)/shard_map/dot_general | solution.py:23
  67.2 0.3 reshape.119
  67.5 0.8 %copy-done = f32[1024,256]{1,0:T(8,128)S(1)} copy-done((f32[1024,256]{1,0:T(8,128)S(1)}, f32[1024,256]{1,0:T(8,128)}, u32[]{:S(2)}) %copy-start) | copy-done | bytes 1048600
  68.2 0.5 multiply_reduce_fusion
  68.7 1.4 %subtract_multiply_fusion = f32[1024,256]{1,0:T(8,128)} fusion(f32[1024,256]{1,0:T(8,128)S(1)} %reshape.119, f32[1024]{0:T(1024)S(1)} %multiply_reduce_fusion, f32[1024]{0:T(1024)S(1)} %fusion.17, f32[1024,256]{1,0:T(8,128)S(1)} %copy-done, f32[1024]{0:T(1024)S(1)} %reduce_max.9), kind=kLoop, calls=%fused_computation.25 | loop fusion | flops 1048576 | bytes 3158016 | tf_op jit(solution)/shard_map/mul | solution.py:80
  (21 shorter events, 0.9 us)
Async XLA Ops:
  14.7 8.7 %copy-start.2 = (s32[1,8192]{1,0:T(1,128)S(1)}, s32[1,8192]{1,0:T(1,128)}, u32[]{:S(2)}) copy-start(s32[1,8192]{1,0:T(1,128)} %param.15) | copy-start | bytes 98308
  14.7 21.9 %copy-start.3 = (s32[1,1,384]{2,1,0:T(1,128)S(1)}, s32[1,1,384]{2,1,0:T(1,128)}, u32[]{:S(2)}) copy-start(s32[1,1,384]{2,1,0:T(1,128)} %param.12) | copy-start | bytes 4612
  16.1 16.2 %all-to-all-start = ((f32[8,64,128]{2,1,0:T(8,128)}), f32[8,64,128]{2,1,0:T(8,128)S(1)}, u32[]{:S(2)}, u32[]{:S(2)}) async-start(f32[8,64,128]{2,1,0:T(8,128)} %bitcast.5), calls=%async_computation | async-start | bytes 524288 | tf_op jit(solution)/shard_map/all_to_all | solution.py:55
  32.3 21.4 %copy-start.1 = (f32[64,128]{1,0:T(8,128)}, f32[64,128]{1,0:T(8,128)S(1)}, u32[]{:S(2)}) copy-start(f32[64,128]{1,0:T(8,128)S(1)} %reduce_sum.28) | copy-start | bytes 98308
  33.0 10.9 %all-to-all-start.1 = ((bf16[8,64,128]{2,1,0:T(8,128)(2,1)}), bf16[8,64,128]{2,1,0:T(8,128)(2,1)S(1)}, u32[]{:S(2)}, u32[]{:S(2)}) async-start(bf16[8,64,128]{2,1,0:T(8,128)(2,1)} %broadcast_in_dim.2), calls=%async_computation.1 | async-start | bytes 262144 | tf_op jit(solution)/shard_map/all_to_all | solution.py:61
  67.0 1.2 %copy-start = (f32[1024,256]{1,0:T(8,128)S(1)}, f32[1024,256]{1,0:T(8,128)}, u32[]{:S(2)}) copy-start(f32[1024,256]{1,0:T(8,128)} %param.10) | copy-start | bytes 3145732

commit v3 on v2

--- a/solution.py
+++ b/solution.py
@@ -29,6 +29,7 @@
 
 def shards(logits, tile_values, tile_pattern, tile_edge, tile_counts, capacity):
     groups = lax.axis_size("nets")
+    me = lax.axis_index("nets")
     tile_block = tile_values[0, 0]
     tile_count = tile_block.shape[0]
     block_size = tile_block.shape[1]
@@ -36,37 +37,62 @@
     pattern_idx = tile_pattern[0, 0]
     edge_idx = tile_edge[0, 0]
     counts = tile_counts[0, 0]
-    live_slot = (jnp.arange(slot_count, dtype=jnp.int32)[None, :] < counts[:, None]).reshape(
-        tile_count
-    )
+    live_slot = jnp.arange(slot_count, dtype=jnp.int32)[None, :] < counts[:, None]
     weight_live = live_slot.astype(jnp.float32)
     probs = jax.nn.softmax(logits, axis=-1)
     probs_half = probs.astype(jnp.bfloat16).reshape(-1, block_size)
-    picked = _take_rows(probs_half, pattern_idx)
-    contrib = (
-        jnp.einsum("tq,tqe->te", picked, tile_block, preferred_element_type=jnp.float32)
-        * weight_live[:, None]
-    )
     capacity_f = capacity.reshape(-1, block_size).astype(jnp.float32)
     owned_blocks = capacity_f.shape[0]
-    owner_idx = jnp.arange(tile_count, dtype=jnp.int32) // slot_count
-    target = owner_idx * owned_blocks + edge_idx
-    partial_value = _add_rows(target, contrib, groups * owned_blocks)
-    received = lax.all_to_all(
-        partial_value.reshape(groups, owned_blocks, block_size), "nets", 0, 0, tiled=False
-    )
-    usage_edges = jnp.sum(received, axis=0)
+
+    def owner_slots(owner):
+        first = owner * slot_count
+        tiles = lax.dynamic_slice_in_dim(tile_block, first, slot_count, axis=0)
+        patterns = lax.dynamic_slice_in_dim(pattern_idx, first, slot_count, axis=0)
+        edges = lax.dynamic_slice_in_dim(edge_idx, first, slot_count, axis=0)
+        live = lax.dynamic_index_in_dim(weight_live, owner, axis=0, keepdims=False)
+        return tiles, patterns, edges, live
+
+    def owner_partial(owner):
+        tiles, patterns, edges, live = owner_slots(owner)
+        picked = _take_rows(probs_half, patterns)
+        contrib = (
+            jnp.einsum("tq,tqe->te", picked, tiles, preferred_element_type=jnp.float32)
+            * live[:, None]
+        )
+        return _add_rows(edges, contrib, owned_blocks)
+
+    usage_edges = None
+    for k in list(range(1, groups)) + [0]:
+        part = owner_partial((me + k) % groups)
+        if k:
+            perm = [(s, (s + k) % groups) for s in range(groups)]
+            part = lax.ppermute(part, "nets", perm)
+        usage_edges = part if usage_edges is None else usage_edges + part
     edge_grad = jax.nn.sigmoid(usage_edges - capacity_f).astype(jnp.bfloat16)
-    spread = jnp.broadcast_to(edge_grad[None], (groups, owned_blocks, block_size))
-    all_grads = lax.all_to_all(spread, "nets", 0, 0, tiled=False).reshape(-1, block_size)
-    slot_grads = _take_rows(all_grads, target)
-    dp_tiles = (
-        jnp.einsum("tqe,te->tq", tile_block, slot_grads, preferred_element_type=jnp.float32)
-        * weight_live[:, None]
-    )
+
+    def owner_terms(owner, grads):
+        tiles, patterns, edges, live = owner_slots(owner)
+        slot_grads = _take_rows(grads, edges)
+        dp = (
+            jnp.einsum("tqe,te->tq", tiles, slot_grads, preferred_element_type=jnp.float32)
+            * live[:, None]
+        )
+        return dp, patterns
+
+    dp_parts, idx_parts = [], []
+    for k in range(groups):
+        grads = edge_grad
+        if k:
+            perm = [(s, (s + k) % groups) for s in range(groups)]
+            grads = lax.ppermute(edge_grad, "nets", perm)
+        dp, patterns = owner_terms((me - k) % groups, grads)
+        dp_parts.append(dp)
+        idx_parts.append(patterns)
+    dp_tiles = jnp.concatenate(dp_parts, axis=0)
+    order_idx = jnp.concatenate(idx_parts, axis=0)
     idx_rows = -(-tile_count // block_size)
     idx_f = jnp.zeros((idx_rows * block_size,), jnp.float32).at[:tile_count].set(
-        pattern_idx.astype(jnp.float32)
+        order_idx.astype(jnp.float32)
     )
     packed = jnp.concatenate([dp_tiles, idx_f.reshape(idx_rows, block_size)], axis=0)
     gathered = lax.all_gather(packed, "region", axis=0, tiled=False)

time: 70.7 us -> 90.6 us (1.28)
  matrix products: 21.2 us -> 43.6 us
  starting transfers between devices: 10.8 us -> 21 us
  waiting for transfers between devices: 16.2 us -> 6.56 us
  other arithmetic: 10.1 us -> 7.45 us
  local copies, waits for them, and re-layouts: 2.07 us -> 1.03 us
    ppermute x0 -> x14, starting transfers between devices: none -> 21 us  [the longest x7 13.1 us: shards(): part = lax.ppermute(part, 'nets', perm)]
    dot_general x2 -> x16, matrix products: 15.8 us -> 33.8 us  [the longest x8 18.4 us: owner_terms(): jnp.einsum('tqe,te->tq', tiles, slot_grads, preferred_element_type=jnp.fl...]
    all_to_all x2 -> x0, waiting for transfers between devices: 16.2 us -> none  [the longest x1 8.88 us: shards(): lax.all_to_all(partial_value.reshape(groups, owned_blocks, block_size), '...]
    all_to_all x2 -> x0, starting transfers between devices: 10.8 us -> none  [the longest x1 7.25 us: shards(): lax.all_to_all(partial_value.reshape(groups, owned_blocks, block_size), '...]
    ppermute x0 -> x14, waiting for transfers between devices: none -> 6.56 us  [the longest x7 6.54 us: shards(): part = lax.ppermute(part, 'nets', perm)]
    dot_general x2 -> x16, matrix products: 1 us -> 3.77 us  [_take_rows(): jnp.dot(sel, table, preferred_element_type=jnp.float32).astype(table.dtype)]
    dot_general x2 -> x9, matrix products: 4.41 us -> 5.99 us  [_add_rows(): lax.dot_general(sel, parts, (((0,), (0,)), ((), ())), preferred_element_t...]
    convert_element_type x1, other arithmetic: 1.57 us -> 0.34 us  [shards(): probs_half = probs.astype(jnp.bfloat16).reshape(-1, block_size)]
  transfers between devices with their start and end apart: 2 -> 14, of which waited for: 2 -> 3; matrix products, arithmetic and copies ran while one was open for 0% -> 37% of each run, Pallas kernels for 0% -> 0%
where the time goes in v3:
time: 90.6 us; the launch traced here: 89.9 us
  matrix products  43.6 us (48%)
  starting transfers between devices  21 us (23%)
  blocking collectives  8.92 us (10%)
  other arithmetic  7.45 us (8%)
  waiting for transfers between devices  6.56 us (7%)
  between operations  1.37 us (2%)
  local copies, waits for them, and re-layouts  1.03 us (1%)
    dot_general x8, matrix products, owner_terms(): jnp.einsum('tqe,te->tq', tiles, slot_grads, preferred_element_type=jnp.fl...  18.4 us
    dot_general x8, matrix products, owner_partial(): jnp.einsum('tq,tqe->te', picked, tiles, preferred_element_type=jnp.float32)  15.4 us
    ppermute x7, starting transfers between devices, shards(): part = lax.ppermute(part, 'nets', perm)  13.1 us
    all_gather x1, blocking collectives, shards(): gathered = lax.all_gather(packed, 'region', axis=0, tiled=False)  8.92 us
    ppermute x7, starting transfers between devices, shards(): grads = lax.ppermute(edge_grad, 'nets', perm)  7.95 us
    ppermute x7, waiting for transfers between devices, shards(): part = lax.ppermute(part, 'nets', perm)  6.54 us
    dot_general x9, matrix products, _add_rows(): lax.dot_general(sel, parts, (((0,), (0,)), ((), ())), preferred_element_t...  5.99 us
    dot_general x16, matrix products, _take_rows(): jnp.dot(sel, table, preferred_element_type=jnp.float32).astype(table.dtype)  3.77 us
  transfers between devices with their start and end apart: 14, of which 3 were waited for; matrix products, arithmetic and copies ran while one was open for 37% of the time, Pallas kernels for 0%

profile of v3, /device:TPU:0, one launch (start us, length us, event | category | flops | bytes accessed | tf_op | source)
XLA Modules:
  0.0 89.9 jit_solution(8181911566318176022)
XLA Ops:
  5.5 1.9 %fusion.18 = f32[48,1,128]{2,1,0:T(1,128)S(1)} fusion(bf16[1,1,384,128,128]{4,3,2,1,0:T(8,128)(2,1)} %param.11, s32[]{:T(128)S(6)} %select_n.208, bf16[48,128,1]{1,0,2:T(8,128)(2,1)S(1)} %fusion.68), kind=kOutput, calls=%fused_computation.19 | convolution fusion | flops 1572864 | bytes 1609732 | tf_op jit(solution)/shard_map/tq,tqe->te/dot_general | solution.py:59
  7.5 1.9 %fusion.20 = f32[48,1,128]{2,1,0:T(1,128)S(1)} fusion(bf16[1,1,384,128,128]{4,3,2,1,0:T(8,128)(2,1)} %param.11, s32[]{:T(128)S(6)} %select_n.205, bf16[48,128,1]{1,0,2:T(8,128)(2,1)S(1)} %fusion.67), kind=kOutput, calls=%fused_computation.21 | convolution fusion | flops 1572864 | bytes 1609732 | tf_op jit(solution)/shard_map/tq,tqe->te/dot_general | solution.py:59
  9.8 5.1 %collective-permute-start.5 = (f32[64,128]{1,0:T(8,128)S(1)}, f32[64,128]{1,0:T(8,128)S(1)}, u32[]{:S(2)}, u32[]{:S(2)}) collective-permute-start(f32[64,128]{1,0:T(8,128)S(1)} %slice_add_fusion.6), channel_id=1, source_target_pairs={{0,24},{4,28},{8,0},{12,4},{16,8},{20,12},{24,16},{28,20},{1,25},{... | collective-permute-start | bytes 98312 | tf_op jit(solution)/shard_map/ppermute | solution.py:69
  15.2 1.9 %fusion.22 = f32[48,1,128]{2,1,0:T(1,128)S(1)} fusion(bf16[1,1,384,128,128]{4,3,2,1,0:T(8,128)(2,1)} %param.11, s32[]{:T(128)S(6)} %select_n.202, bf16[48,128,1]{1,0,2:T(8,128)(2,1)S(1)} %fusion.66), kind=kOutput, calls=%fused_computation.23 | convolution fusion | flops 1572864 | bytes 1609732 | tf_op jit(solution)/shard_map/tq,tqe->te/dot_general | solution.py:59
  17.4 1.9 %fusion.24 = f32[48,1,128]{2,1,0:T(1,128)S(1)} fusion(bf16[1,1,384,128,128]{4,3,2,1,0:T(8,128)(2,1)} %param.11, s32[]{:T(128)S(6)} %select_n.199, bf16[48,128,1]{1,0,2:T(8,128)(2,1)S(1)} %fusion.65), kind=kOutput, calls=%fused_computation.25 | convolution fusion | flops 1572864 | bytes 1609732 | tf_op jit(solution)/shard_map/tq,tqe->te/dot_general | solution.py:59
  20.3 1.9 %fusion.28 = f32[48,1,128]{2,1,0:T(1,128)S(1)} fusion(bf16[1,1,384,128,128]{4,3,2,1,0:T(8,128)(2,1)} %param.11, s32[]{:T(128)S(6)} %select_n.193, bf16[48,128,1]{1,0,2:T(8,128)(2,1)S(1)} %fusion.63), kind=kOutput, calls=%fused_computation.29 | convolution fusion | flops 1572864 | bytes 1609732 | tf_op jit(solution)/shard_map/tq,tqe->te/dot_general | solution.py:59
  22.3 1.9 %fusion.26 = f32[48,1,128]{2,1,0:T(1,128)S(1)} fusion(bf16[1,1,384,128,128]{4,3,2,1,0:T(8,128)(2,1)} %param.11, s32[]{:T(128)S(6)} %select_n.196, bf16[48,128,1]{1,0,2:T(8,128)(2,1)S(1)} %fusion.64), kind=kOutput, calls=%fused_computation.27 | convolution fusion | flops 1572864 | bytes 1609732 | tf_op jit(solution)/shard_map/tq,tqe->te/dot_general | solution.py:59
  26.2 1.9 %fusion.16 = f32[48,1,128]{2,1,0:T(1,128)S(1)} fusion(bf16[1,1,384,128,128]{4,3,2,1,0:T(8,128)(2,1)} %param.11, s32[]{:T(128)S(6)} %select_n.211, bf16[48,128,1]{1,0,2:T(8,128)(2,1)S(1)} %fusion.69), kind=kOutput, calls=%fused_computation.17 | convolution fusion | flops 1572864 | bytes 1609732 | tf_op jit(solution)/shard_map/tq,tqe->te/dot_general | solution.py:59
  28.1 1.9 %fusion.32 = f32[48,1,128]{2,1,0:T(1,128)S(1)} fusion(bf16[1,1,384,128,128]{4,3,2,1,0:T(8,128)(2,1)} %param.11, s32[]{:T(128)S(6)} %select_n.191, bf16[48,128,1]{1,0,2:T(8,128)(2,1)S(1)} %fusion.70), kind=kOutput, calls=%fused_computation.33 | convolution fusion | flops 1572864 | bytes 1609732 | tf_op jit(solution)/shard_map/tq,tqe->te/dot_general | solution.py:59
  30.4 3.8 %collective-permute-start.6 = (f32[64,128]{1,0:T(8,128)S(1)}, f32[64,128]{1,0:T(8,128)S(1)}, u32[]{:S(2)}, u32[]{:S(2)}) collective-permute-start(f32[64,128]{1,0:T(8,128)S(1)} %slice_add_fusion.4), channel_id=1, source_target_pairs={{0,28},{4,0},{8,4},{12,8},{16,12},{20,16},{24,20},{28,24},{1,29},{... | collective-permute-start | bytes 98312 | tf_op jit(solution)/shard_map/ppermute | solution.py:69
  35.5 3.0 %collective-permute-start.2 = (f32[64,128]{1,0:T(8,128)S(1)}, f32[64,128]{1,0:T(8,128)S(1)}, u32[]{:S(2)}, u32[]{:S(2)}) collective-permute-start(f32[64,128]{1,0:T(8,128)S(1)} %slice_add_fusion.12), channel_id=1, source_target_pairs={{0,12},{4,16},{8,20},{12,24},{16,28},{20,0},{24,4},{28,8},{1,13},{... | collective-permute-start | bytes 98312 | tf_op jit(solution)/shard_map/ppermute | solution.py:69
  39.7 1.6 %collective-permute-done.2 = f32[64,128]{1,0:T(8,128)S(1)} collective-permute-done((f32[64,128]{1,0:T(8,128)S(1)}, f32[64,128]{1,0:T(8,128)S(1)}, u32[]{:S(2)}, u32[]{:S(2)}) %collective-permute-start.2) | collective-permute-done | bytes 32800 | tf_op jit(solution)/shard_map/ppermute | solution.py:69
  41.3 3.8 %collective-permute-done = f32[64,128]{1,0:T(8,128)S(1)} collective-permute-done((f32[64,128]{1,0:T(8,128)S(1)}, f32[64,128]{1,0:T(8,128)S(1)}, u32[]{:S(2)}, u32[]{:S(2)}) %collective-permute-start) | collective-permute-done | bytes 32800 | tf_op jit(solution)/shard_map/ppermute | solution.py:69
  46.7 4.2 %collective-permute-start.10 = (bf16[64,128]{1,0:T(8,128)(2,1)S(1)}, bf16[64,128]{1,0:T(8,128)(2,1)S(1)}, u32[]{:S(2)}, u32[]{:S(2)}) collective-permute-start(bf16[64,128]{1,0:T(8,128)(2,1)S(1)} %get-tuple-element.22), channel_id=1, source_target_pairs={{0,16},{4,20},{8,24},{12,28},{16,0},{20,4},{24,8},{28,12},{1,17},{... | collective-permute-start | bytes 49160 | tf_op jit(solution)/shard_map/ppermute | solution.py:87
  50.9 2.3 %fusion.30 = f32[48,1,128]{2,1,0:T(1,128)S(1)} fusion(bf16[1,1,384,128,128]{4,3,2,1,0:T(8,128)(2,1)} %param.11, s32[]{:T(128)S(6)} %select_n.191, bf16[48,128,1]{1,0,2:T(8,128)(2,1)S(1)} %fusion.55), kind=kOutput, calls=%fused_computation.31 | convolution fusion | flops 1572864 | bytes 1609732 | tf_op jit(solution)/shard_map/tqe,te->tq/dot_general | solution.py:77
  55.0 2.3 %fusion.2 = f32[48,1,128]{2,1,0:T(1,128)S(1)} fusion(bf16[1,1,384,128,128]{4,3,2,1,0:T(8,128)(2,1)} %param.11, s32[]{:T(128)S(6)} %select_n.233, bf16[48,128,1]{1,0,2:T(8,128)(2,1)S(1)} %fusion.62), kind=kOutput, calls=%fused_computation.3 | convolution fusion | flops 1572864 | bytes 1609732 | tf_op jit(solution)/shard_map/tqe,te->tq/dot_general | solution.py:77
  59.0 2.3 %fusion.4 = f32[48,1,128]{2,1,0:T(1,128)S(1)} fusion(bf16[1,1,384,128,128]{4,3,2,1,0:T(8,128)(2,1)} %param.11, s32[]{:T(128)S(6)} %select_n.230, bf16[48,128,1]{1,0,2:T(8,128)(2,1)S(1)} %fusion.61), kind=kOutput, calls=%fused_computation.5 | convolution fusion | flops 1572864 | bytes 1609732 | tf_op jit(solution)/shard_map/tqe,te->tq/dot_general | solution.py:77
  61.5 2.3 %fusion.6 = f32[48,1,128]{2,1,0:T(1,128)S(1)} fusion(bf16[1,1,384,128,128]{4,3,2,1,0:T(8,128)(2,1)} %param.11, s32[]{:T(128)S(6)} %select_n.227, bf16[48,128,1]{1,0,2:T(8,128)(2,1)S(1)} %fusion.60), kind=kOutput, calls=%fused_computation.7 | convolution fusion | flops 1572864 | bytes 1609732 | tf_op jit(solution)/shard_map/tqe,te->tq/dot_general | solution.py:77
  64.0 2.3 %fusion.8 = f32[48,1,128]{2,1,0:T(1,128)S(1)} fusion(bf16[1,1,384,128,128]{4,3,2,1,0:T(8,128)(2,1)} %param.11, s32[]{:T(128)S(6)} %select_n.224, bf16[48,128,1]{1,0,2:T(8,128)(2,1)S(1)} %fusion.59), kind=kOutput, calls=%fused_computation.9 | convolution fusion | flops 1572864 | bytes 1609732 | tf_op jit(solution)/shard_map/tqe,te->tq/dot_general | solution.py:77
  66.5 2.3 %fusion.10 = f32[48,1,128]{2,1,0:T(1,128)S(1)} fusion(bf16[1,1,384,128,128]{4,3,2,1,0:T(8,128)(2,1)} %param.11, s32[]{:T(128)S(6)} %select_n.221, bf16[48,128,1]{1,0,2:T(8,128)(2,1)S(1)} %fusion.58), kind=kOutput, calls=%fused_computation.11 | convolution fusion | flops 1572864 | bytes 1609732 | tf_op jit(solution)/shard_map/tqe,te->tq/dot_general | solution.py:77
  69.1 2.3 %fusion.12 = f32[48,1,128]{2,1,0:T(1,128)S(1)} fusion(bf16[1,1,384,128,128]{4,3,2,1,0:T(8,128)(2,1)} %param.11, s32[]{:T(128)S(6)} %select_n.218, bf16[48,128,1]{1,0,2:T(8,128)(2,1)S(1)} %fusion.57), kind=kOutput, calls=%fused_computation.13 | convolution fusion | flops 1572864 | bytes 1609732 | tf_op jit(solution)/shard_map/tqe,te->tq/dot_general | solution.py:77
  71.6 2.3 %fusion.14 = f32[48,1,128]{2,1,0:T(1,128)S(1)} fusion(bf16[1,1,384,128,128]{4,3,2,1,0:T(8,128)(2,1)} %param.11, s32[]{:T(128)S(6)} %select_n.215, bf16[48,128,1]{1,0,2:T(8,128)(2,1)S(1)} %fusion.56), kind=kOutput, calls=%fused_computation.15 | convolution fusion | flops 1572864 | bytes 1609732 | tf_op jit(solution)/shard_map/tqe,te->tq/dot_general | solution.py:77
  74.4 8.9 %all-gather.1 = f32[4,387,128]{2,1,0:T(8,128)S(1)} all-gather(f32[1,387,128]{2,1,0:T(8,128)S(1)} %bitcast.232), channel_id=2, replica_groups=mesh['nets'=8,'region'=4] {'region'}, dimensions={0}, use_global_device_ids=true | all-gather | bytes 990720 | tf_op jit(solution)/shard_map/all_gather | solution.py:98
  83.6 3.9 %fusion = f32[2048,384]{1,0:T(8,128)S(1)} fusion(s32[1536]{0:T(1024)S(1)} %convert_element_type.141, bf16[1536,128]{1,0:T(8,128)(2,1)S(1)} %get-tuple-element.25, bf16[1536,128]{1,0:T(8,128)(2,1)S(1)} %get-tuple-element.26, bf16[1536,128]{1,0:T(8,128)(2,1)S(1)} %get-tuple-element.24), kind=kOutput, calls=%fused_computation.1 | convolution fusion | flops 2422603776 | bytes 4331520 | tf_op jit(solution)/shard_map/dot_general | solution.py:23
  (96 shorter events, 20.5 us)
Async XLA Ops:
  0.6 3.8 %copy-start = (f32[1024,256]{1,0:T(8,128)S(1)}, f32[1024,256]{1,0:T(8,128)}, u32[]{:S(2)}) copy-start(f32[1024,256]{1,0:T(8,128)} %param.10) | copy-start | bytes 3145732
  0.6 3.4 %copy-start.4 = (s32[1,1,8]{2,1,0:T(1,128)S(1)}, s32[1,1,8]{2,1,0:T(1,128)}, u32[]{:S(2)}) copy-start(s32[1,1,8]{2,1,0:T(1,128)} %param.14) | copy-start | bytes 100
  0.7 3.5 %copy-start.1 = (s32[1,1,384]{2,1,0:T(1,128)S(1)}, s32[1,1,384]{2,1,0:T(1,128)}, u32[]{:S(2)}) copy-start(s32[1,1,384]{2,1,0:T(1,128)} %param.13) | copy-start | bytes 4612
  0.7 3.6 %copy-start.2 = (s32[1,1,384]{2,1,0:T(1,128)S(1)}, s32[1,1,384]{2,1,0:T(1,128)}, u32[]{:S(2)}) copy-start(s32[1,1,384]{2,1,0:T(1,128)} %param.12) | copy-start | bytes 4612
  9.8 25.7 %collective-permute-start.5 = (f32[64,128]{1,0:T(8,128)S(1)}, f32[64,128]{1,0:T(8,128)S(1)}, u32[]{:S(2)}, u32[]{:S(2)}) collective-permute-start(f32[64,128]{1,0:T(8,128)S(1)} %slice_add_fusion.6), channel_id=1, source_target_pairs={{0,24},{4,28},{8,0},{12,4},{16,8},{20,12},{24,16},{28,20},{1,25},{... | collective-permute-start | bytes 98312 | tf_op jit(solution)/shard_map/ppermute | solution.py:69
  19.7 18.8 %collective-permute-start.3 = (f32[64,128]{1,0:T(8,128)S(1)}, f32[64,128]{1,0:T(8,128)S(1)}, u32[]{:S(2)}, u32[]{:S(2)}) collective-permute-start(f32[64,128]{1,0:T(8,128)S(1)} %slice_add_fusion.10), channel_id=1, source_target_pairs={{0,16},{4,20},{8,24},{12,28},{16,0},{20,4},{24,8},{28,12},{1,17},{... | collective-permute-start | bytes 98312 | tf_op jit(solution)/shard_map/ppermute | solution.py:69
  24.6 14.0 %collective-permute-start.1 = (f32[64,128]{1,0:T(8,128)S(1)}, f32[64,128]{1,0:T(8,128)S(1)}, u32[]{:S(2)}, u32[]{:S(2)}) collective-permute-start(f32[64,128]{1,0:T(8,128)S(1)} %slice_add_fusion.14), channel_id=1, source_target_pairs={{0,8},{4,12},{8,16},{12,20},{16,24},{20,28},{24,0},{28,4},{1,9},{5... | collective-permute-start | bytes 98312 | tf_op jit(solution)/shard_map/ppermute | solution.py:69
  26.2 12.3 %copy-start.3 = (s32[1,8192]{1,0:T(1,128)S(1)}, s32[1,8192]{1,0:T(1,128)}, u32[]{:S(2)}) copy-start(s32[1,8192]{1,0:T(1,128)} %param.15) | copy-start | bytes 98308
  30.4 8.1 %collective-permute-start.6 = (f32[64,128]{1,0:T(8,128)S(1)}, f32[64,128]{1,0:T(8,128)S(1)}, u32[]{:S(2)}, u32[]{:S(2)}) collective-permute-start(f32[64,128]{1,0:T(8,128)S(1)} %slice_add_fusion.4), channel_id=1, source_target_pairs={{0,28},{4,0},{8,4},{12,8},{16,12},{20,16},{24,20},{28,24},{1,29},{... | collective-permute-start | bytes 98312 | tf_op jit(solution)/shard_map/ppermute | solution.py:69
  34.5 5.2 %collective-permute-start.4 = (f32[64,128]{1,0:T(8,128)S(1)}, f32[64,128]{1,0:T(8,128)S(1)}, u32[]{:S(2)}, u32[]{:S(2)}) collective-permute-start(f32[64,128]{1,0:T(8,128)S(1)} %slice_add_fusion.8), channel_id=1, source_target_pairs={{0,20},{4,24},{8,28},{12,0},{16,4},{20,8},{24,12},{28,16},{1,21},{... | collective-permute-start | bytes 98312 | tf_op jit(solution)/shard_map/ppermute | solution.py:69
  35.5 5.8 %collective-permute-start.2 = (f32[64,128]{1,0:T(8,128)S(1)}, f32[64,128]{1,0:T(8,128)S(1)}, u32[]{:S(2)}, u32[]{:S(2)}) collective-permute-start(f32[64,128]{1,0:T(8,128)S(1)} %slice_add_fusion.12), channel_id=1, source_target_pairs={{0,12},{4,16},{8,20},{12,24},{16,28},{20,0},{24,4},{28,8},{1,13},{... | collective-permute-start | bytes 98312 | tf_op jit(solution)/shard_map/ppermute | solution.py:69
  38.5 6.6 %collective-permute-start = (f32[64,128]{1,0:T(8,128)S(1)}, f32[64,128]{1,0:T(8,128)S(1)}, u32[]{:S(2)}, u32[]{:S(2)}) collective-permute-start(f32[64,128]{1,0:T(8,128)S(1)} %slice_add_fusion.16), channel_id=1, source_target_pairs={{0,4},{4,8},{8,12},{12,16},{16,20},{20,24},{24,28},{28,0},{1,5},{5... | collective-permute-start | bytes 98312 | tf_op jit(solution)/shard_map/ppermute | solution.py:69
  46.0 7.3 %collective-permute-start.13 = (bf16[64,128]{1,0:T(8,128)(2,1)S(1)}, bf16[64,128]{1,0:T(8,128)(2,1)S(1)}, u32[]{:S(2)}, u32[]{:S(2)}) collective-permute-start(bf16[64,128]{1,0:T(8,128)(2,1)S(1)} %get-tuple-element.22), channel_id=1, source_target_pairs={{0,28},{4,0},{8,4},{12,8},{16,12},{20,16},{24,20},{28,24},{1,29},{... | collective-permute-start | bytes 49160 | tf_op jit(solution)/shard_map/ppermute | solution.py:87
  46.0 11.3 %collective-permute-start.12 = (bf16[64,128]{1,0:T(8,128)(2,1)S(1)}, bf16[64,128]{1,0:T(8,128)(2,1)S(1)}, u32[]{:S(2)}, u32[]{:S(2)}) collective-permute-start(bf16[64,128]{1,0:T(8,128)(2,1)S(1)} %get-tuple-element.22), channel_id=1, source_target_pairs={{0,24},{4,28},{8,0},{12,4},{16,8},{20,12},{24,16},{28,20},{1,25},{... | collective-permute-start | bytes 49160 | tf_op jit(solution)/shard_map/ppermute | solution.py:87
  46.5 14.7 %collective-permute-start.11 = (bf16[64,128]{1,0:T(8,128)(2,1)S(1)}, bf16[64,128]{1,0:T(8,128)(2,1)S(1)}, u32[]{:S(2)}, u32[]{:S(2)}) collective-permute-start(bf16[64,128]{1,0:T(8,128)(2,1)S(1)} %get-tuple-element.22), channel_id=1, source_target_pairs={{0,20},{4,24},{8,28},{12,0},{16,4},{20,8},{24,12},{28,16},{1,21},{... | collective-permute-start | bytes 49160 | tf_op jit(solution)/shard_map/ppermute | solution.py:87
  46.7 17.1 %collective-permute-start.10 = (bf16[64,128]{1,0:T(8,128)(2,1)S(1)}, bf16[64,128]{1,0:T(8,128)(2,1)S(1)}, u32[]{:S(2)}, u32[]{:S(2)}) collective-permute-start(bf16[64,128]{1,0:T(8,128)(2,1)S(1)} %get-tuple-element.22), channel_id=1, source_target_pairs={{0,16},{4,20},{8,24},{12,28},{16,0},{20,4},{24,8},{28,12},{1,17},{... | collective-permute-start | bytes 49160 | tf_op jit(solution)/shard_map/ppermute | solution.py:87
  50.9 15.4 %collective-permute-start.9 = (bf16[64,128]{1,0:T(8,128)(2,1)S(1)}, bf16[64,128]{1,0:T(8,128)(2,1)S(1)}, u32[]{:S(2)}, u32[]{:S(2)}) collective-permute-start(bf16[64,128]{1,0:T(8,128)(2,1)S(1)} %get-tuple-element.22), channel_id=1, source_target_pairs={{0,12},{4,16},{8,20},{12,24},{16,28},{20,0},{24,4},{28,8},{1,13},{... | collective-permute-start | bytes 49160 | tf_op jit(solution)/shard_map/ppermute | solution.py:87
  53.3 15.6 %collective-permute-start.8 = (bf16[64,128]{1,0:T(8,128)(2,1)S(1)}, bf16[64,128]{1,0:T(8,128)(2,1)S(1)}, u32[]{:S(2)}, u32[]{:S(2)}) collective-permute-start(bf16[64,128]{1,0:T(8,128)(2,1)S(1)} %get-tuple-element.22), channel_id=1, source_target_pairs={{0,8},{4,12},{8,16},{12,20},{16,24},{20,28},{24,0},{28,4},{1,9},{5... | collective-permute-start | bytes 49160 | tf_op jit(solution)/shard_map/ppermute | solution.py:87
  57.3 14.1 %collective-permute-start.7 = (bf16[64,128]{1,0:T(8,128)(2,1)S(1)}, bf16[64,128]{1,0:T(8,128)(2,1)S(1)}, u32[]{:S(2)}, u32[]{:S(2)}) collective-permute-start(bf16[64,128]{1,0:T(8,128)(2,1)S(1)} %get-tuple-element.22), channel_id=1, source_target_pairs={{0,4},{4,8},{8,12},{12,16},{16,20},{20,24},{24,28},{28,0},{1,5},{5... | collective-permute-start | bytes 49160 | tf_op jit(solution)/shard_map/ppermute | solution.py:87

commit v4 on v2

--- a/solution.py
+++ b/solution.py
@@ -1,6 +1,7 @@
 import jax
 import jax.numpy as jnp
 from jax import lax
+from jax.experimental import pallas as pl
 from jax.sharding import PartitionSpec as P
 
 
@@ -27,6 +28,39 @@
     return out[:, :width] + out[:, width : 2 * width] + out[:, 2 * width :]
 
 
+def _softmax_kernel(x_ref, p_ref, h_ref):
+    x = x_ref[...]
+    e = jnp.exp(x - jnp.max(x, axis=-1, keepdims=True))
+    p = e / jnp.sum(e, axis=-1, keepdims=True)
+    p_ref[...] = p
+    half = p.astype(jnp.bfloat16)
+    width = h_ref.shape[-1]
+    for h in range(h_ref.shape[0]):
+        h_ref[h] = half[:, h * width : (h + 1) * width]
+
+
+def _softmax(logits, block_size):
+    rows, width = logits.shape
+    halves = width // block_size
+    step = min(rows, 256)
+    return pl.pallas_call(
+        _softmax_kernel,
+        grid=(rows // step,),
+        in_specs=[pl.BlockSpec((step, width), lambda i: (i, 0))],
+        out_specs=[
+            pl.BlockSpec((step, width), lambda i: (i, 0)),
+            pl.BlockSpec((halves, step, block_size), lambda i: (0, i, 0)),
+        ],
+        out_shape=[
+            jax.ShapeDtypeStruct((rows, width), jnp.float32),
+            jax.ShapeDtypeStruct((halves, rows, block_size), jnp.bfloat16),
+        ],
+        cost_estimate=pl.CostEstimate(
+            flops=5 * rows * width, transcendentals=rows * width, bytes_accessed=10 * rows * width
+        ),
+    )(logits)
+
+
 def shards(logits, tile_values, tile_pattern, tile_edge, tile_counts, capacity):
     groups = lax.axis_size("nets")
     tile_block = tile_values[0, 0]
@@ -40,9 +74,11 @@
         tile_count
     )
     weight_live = live_slot.astype(jnp.float32)
-    probs = jax.nn.softmax(logits, axis=-1)
-    probs_half = probs.astype(jnp.bfloat16).reshape(-1, block_size)
-    picked = _take_rows(probs_half, pattern_idx)
+    probs, probs_split = _softmax(logits, block_size)
+    segments, halves = probs_split.shape[1], probs_split.shape[0]
+    probs_half = probs_split.reshape(-1, block_size)
+    split_idx = (pattern_idx % halves) * segments + pattern_idx // halves
+    picked = _take_rows(probs_half, split_idx)
     contrib = (
         jnp.einsum("tq,tqe->te", picked, tile_block, preferred_element_type=jnp.float32)
         * weight_live[:, None]
@@ -66,7 +102,7 @@
     )
     idx_rows = -(-tile_count // block_size)
     idx_f = jnp.zeros((idx_rows * block_size,), jnp.float32).at[:tile_count].set(
-        pattern_idx.astype(jnp.float32)
+        split_idx.astype(jnp.float32)
     )
     packed = jnp.concatenate([dp_tiles, idx_f.reshape(idx_rows, block_size)], axis=0)
     gathered = lax.all_gather(packed, "region", axis=0, tiled=False)
@@ -76,7 +112,8 @@
         .astype(jnp.int32)
         .reshape(-1)
     )
-    summed_grad = _add_rows(all_idx, all_dp, probs_half.shape[0]).reshape(logits.shape)
+    summed = _add_rows(all_idx, all_dp, probs_half.shape[0]).reshape(halves, segments, block_size)
+    summed_grad = jnp.concatenate([summed[h] for h in range(halves)], axis=1)
     logit_grad = probs * (summed_grad - jnp.sum(probs * summed_grad, axis=-1, keepdims=True))
     return (logit_grad, usage_edges.reshape(capacity.shape))
 

time: 70.7 us -> 70 us (0.990)
  other arithmetic: 10.1 us -> 4.99 us
  Pallas kernels: 0 us -> 3.79 us
  matrix products: 21.2 us -> 22.3 us
    pallas_call x0 -> x1, Pallas kernels: none -> 3.79 us  [_softmax(): pl.pallas_call(_softmax_kernel, grid=(rows // step,), in_specs=[pl.BlockS...]
    reduce_sum x1 -> x0, other arithmetic: 1.59 us -> none  [shards(): probs = jax.nn.softmax(logits, axis=-1)]
    convert_element_type x2 -> x1, other arithmetic: 1.59 us -> 0.01 us  [shards(): split_idx.astype(jnp.float32)]
    reduce_max x1 -> x0, other arithmetic: 1.43 us -> none  [shards(): probs = jax.nn.softmax(logits, axis=-1)]
    dot_general x2, matrix products: 1 us -> 2.04 us  [_take_rows(): jnp.dot(sel, table, preferred_element_type=jnp.float32).astype(table.dtype)]
where the time goes in v4:
time: 70 us; the launch traced here: 69.5 us
  matrix products  22.3 us (32%)
  waiting for transfers between devices  16.2 us (23%)
  starting transfers between devices  10.8 us (15%)
  blocking collectives  8.71 us (12%)
  other arithmetic  4.99 us (7%)
  Pallas kernels  3.79 us (5%)
  local copies, waits for them, and re-layouts  1.87 us (3%)
  between operations  0.76 us (1%)
    dot_general x1, matrix products, shards(): jnp.einsum('tqe,te->tq', tile_block, slot_grads, preferred_element_type=j...  9.46 us
    all_to_all x1, waiting for transfers between devices, shards(): lax.all_to_all(partial_value.reshape(groups, owned_blocks, block_size), '...  8.88 us
    all_gather x1, blocking collectives, shards(): gathered = lax.all_gather(packed, 'region', axis=0, tiled=False)  8.71 us
    all_to_all x1, waiting for transfers between devices, shards(): lax.all_to_all(spread, 'nets', 0, 0, tiled=False).reshape(-1, block_size)  7.33 us
    all_to_all x1, starting transfers between devices, shards(): lax.all_to_all(partial_value.reshape(groups, owned_blocks, block_size), '...  7.26 us
    dot_general x1, matrix products, shards(): jnp.einsum('tq,tqe->te', picked, tile_block, preferred_element_type=jnp.f...  6.36 us
    dot_general x2, matrix products, _add_rows(): lax.dot_general(sel, parts, (((0,), (0,)), ((), ())), preferred_element_t...  4.41 us
    pallas_call x1, Pallas kernels, _softmax(): pl.pallas_call(_softmax_kernel, grid=(rows // step,), in_specs=[pl.BlockS...  3.79 us
  transfers between devices with their start and end apart: 2, of which 2 were waited for; matrix products, arithmetic and copies ran while one was open for 0% of the time, Pallas kernels for 0%

profile of v4, /device:TPU:0, one launch (start us, length us, event | category | flops | bytes accessed | tf_op | source)
XLA Modules:
  0.0 69.5 jit_solution(7843317935574327160)
XLA Ops:
  0.6 0.7 %reduce.3 = s32[384]{0:T(512)S(1)} reduce(s32[1,1,384]{2,1,0:T(1,128)} %param.12, s32[]{:T(128)} %constant.68.clone.1), dimensions={0,1}, to_apply=%param.12.reduce_sub_computation | reduce | bytes 3076 | tf_op args[2]
  1.3 0.7 %reduce.2 = s32[384]{0:T(512)S(1)} reduce(s32[1,1,384]{2,1,0:T(1,128)} %param.13, s32[]{:T(128)} %constant.68.clone.1), dimensions={0,1}, to_apply=%param.13.reduce_sub_computation | reduce | bytes 3076 | tf_op args[3]
  2.1 0.7 %fusion.28 = f32[8,48]{1,0:T(8,128)S(1)} fusion(s32[8]{0:T(128)} %bitcast.51), kind=kLoop, calls=%fused_computation.55 | loop fusion | flops 768 | bytes 1568 | tf_op jit(solution)/shard_map/convert_element_type | solution.py:76
  2.9 3.8 %shard_map.82 = (f32[1024,256]{1,0:T(8,128)}, bf16[2,1024,128]{2,1,0:T(8,128)(2,1)}) custom-call(f32[1024,256]{1,0:T(8,128)} %x_ref.1), custom_call_target="tpu_custom_call" | custom-call | flops 1310720 | bytes 2621440 | tf_op jit(solution)/shard_map/pallas_call | solution.py:46
  6.7 1.7 %fusion.14 = bf16[384,128,1]{1,0,2:T(8,128)(2,1)S(1)} fusion(bf16[2048,128]{1,0:T(8,128)(2,1)} %bitcast.52, s32[384]{0:T(512)S(1)} %fusion.32), kind=kOutput, calls=%fused_computation.21 | convolution fusion | flops 202162176 | bytes 624128 | tf_op jit(solution)/shard_map/dot_general | solution.py:14
  8.4 6.4 %fusion.2 = f32[384,1,128]{2,1,0:T(1,128)S(1)} fusion(bf16[1,1,384,128,128]{4,3,2,1,0:T(8,128)(2,1)} %param.11, bf16[384,128,1]{1,0,2:T(8,128)(2,1)S(1)} %fusion.14), kind=kOutput, calls=%fused_computation.2 | convolution fusion | flops 12582912 | bytes 12877824 | tf_op jit(solution)/shard_map/tq,tqe->te/dot_general | solution.py:83
  14.7 0.1 reduce-precision_convert_fusion.3
  14.9 0.5 fusion.17
  15.4 0.7 %slice_add_fusion.2 = f32[512,128]{1,0:T(8,128)} fusion(f32[512,384]{1,0:T(8,128)S(1)} %fusion.17), kind=kLoop, calls=%fused_computation.42 | loop fusion | flops 131072 | bytes 1048576 | tf_op jit(solution)/shard_map/add | solution.py:28
  16.2 7.3 %all-to-all-start = ((f32[8,64,128]{2,1,0:T(8,128)}), f32[8,64,128]{2,1,0:T(8,128)S(1)}, u32[]{:S(2)}, u32[]{:S(2)}) async-start(f32[8,64,128]{2,1,0:T(8,128)} %bitcast.6), calls=%async_computation | async-start | bytes 524288 | tf_op jit(solution)/shard_map/all_to_all | solution.py:91
  23.5 8.9 %all-to-all-done = f32[8,64,128]{2,1,0:T(8,128)S(1)} async-done(((f32[8,64,128]{2,1,0:T(8,128)}), f32[8,64,128]{2,1,0:T(8,128)S(1)}, u32[]{:S(2)}, u32[]{:S(2)}) %all-to-all-start) | async-done | bytes 262176 | tf_op jit(solution)/shard_map/all_to_all | solution.py:91
  32.4 0.7 broadcast_in_dim.2
  33.1 3.6 %all-to-all-start.1 = ((bf16[8,64,128]{2,1,0:T(8,128)(2,1)}), bf16[8,64,128]{2,1,0:T(8,128)(2,1)S(1)}, u32[]{:S(2)}, u32[]{:S(2)}) async-start(bf16[8,64,128]{2,1,0:T(8,128)(2,1)} %broadcast_in_dim.2), calls=%async_computation.1 | async-start | bytes 262144 | tf_op jit(solution)/shard_map/all_to_all | solution.py:97
  36.7 7.3 %all-to-all-done.1 = bf16[8,64,128]{2,1,0:T(8,128)(2,1)S(1)} async-done(((bf16[8,64,128]{2,1,0:T(8,128)(2,1)}), bf16[8,64,128]{2,1,0:T(8,128)(2,1)S(1)}, u32[]{:S(2)}, u32[]{:S(2)}) %all-to-all-start.1) | async-done | bytes 131104 | tf_op jit(solution)/shard_map/all_to_all | solution.py:97
  44.0 0.3 fusion.15
  44.3 9.5 %fusion = f32[384,1,128]{2,1,0:T(1,128)S(1)} fusion(bf16[1,1,384,128,128]{4,3,2,1,0:T(8,128)(2,1)} %param.11, bf16[384,128,1]{1,0,2:T(8,128)(2,1)S(1)} %fusion.15), kind=kOutput, calls=%fused_computation | convolution fusion | flops 12582912 | bytes 12877824 | tf_op jit(solution)/shard_map/tqe,te->tq/dot_general | solution.py:100
  53.8 0.1 broadcast_multiply_fusion
  54.0 8.7 %all-gather.1 = f32[4,387,128]{2,1,0:T(8,128)S(1)} all-gather(f32[1,387,128]{2,1,0:T(8,128)S(1)} %maximum_bitcast_fusion), channel_id=2, replica_groups=mesh['nets'=8,'region'=4] {'region'}, dimensions={0}, use_global_device_ids=true | all-gather | bytes 990720 | tf_op jit(solution)/shard_map/all_gather | solution.py:108
  62.7 0.2 reduce-precision_convert_fusion.1
  63.0 3.9 %fusion.4 = f32[2048,384]{1,0:T(8,128)S(1)} fusion(s32[1536]{0:T(1024)S(1)} %convert_element_type.65, bf16[1536,128]{1,0:T(8,128)(2,1)S(1)} %get-tuple-element.29, bf16[1536,128]{1,0:T(8,128)(2,1)S(1)} %get-tuple-element.30, bf16[1536,128]{1,0:T(8,128)(2,1)S(1)} %get-tuple-element.28), kind=kOutput, calls=%fused_computation.5 | convolution fusion | flops 2422603776 | bytes 4331520 | tf_op jit(solution)/shard_map/dot_general | solution.py:24
  66.8 0.1 slice_add_fusion
  67.1 1.0 %copy-done = f32[1024,256]{1,0:T(8,128)S(1)} copy-done((f32[1024,256]{1,0:T(8,128)S(1)}, f32[1024,256]{1,0:T(8,128)}, u32[]{:S(2)}) %copy-start) | copy-done | bytes 1048600
  68.1 0.2 multiply_reduce_fusion
  68.3 1.2 %subtract_multiply_fusion = f32[1024,256]{1,0:T(8,128)} fusion(f32[1024,256]{1,0:T(8,128)S(1)} %copy-done, f32[1024,128]{1,0:T(8,128)S(1)} %get-tuple-element.27, f32[1024,128]{1,0:T(8,128)S(1)} %get-tuple-element.26, f32[1024]{0:T(1024)S(1)} %multiply_reduce_fusion), kind=kLoop, calls=%fused_computation.26 | loop fusion | flops 786432 | bytes 3149824 | tf_op jit(solution)/shard_map/mul | solution.py:117
  (17 shorter events, 0.4 us)
Async XLA Ops:
  14.7 8.7 %copy-start.2 = (s32[1,8192]{1,0:T(1,128)S(1)}, s32[1,8192]{1,0:T(1,128)}, u32[]{:S(2)}) copy-start(s32[1,8192]{1,0:T(1,128)} %param.15) | copy-start | bytes 98308
  16.2 16.2 %all-to-all-start = ((f32[8,64,128]{2,1,0:T(8,128)}), f32[8,64,128]{2,1,0:T(8,128)S(1)}, u32[]{:S(2)}, u32[]{:S(2)}) async-start(f32[8,64,128]{2,1,0:T(8,128)} %bitcast.6), calls=%async_computation | async-start | bytes 524288 | tf_op jit(solution)/shard_map/all_to_all | solution.py:91
  32.4 21.4 %copy-start.1 = (f32[64,128]{1,0:T(8,128)}, f32[64,128]{1,0:T(8,128)S(1)}, u32[]{:S(2)}) copy-start(f32[64,128]{1,0:T(8,128)S(1)} %reduce_sum.18) | copy-start | bytes 98308
  33.1 10.9 %all-to-all-start.1 = ((bf16[8,64,128]{2,1,0:T(8,128)(2,1)}), bf16[8,64,128]{2,1,0:T(8,128)(2,1)S(1)}, u32[]{:S(2)}, u32[]{:S(2)}) async-start(bf16[8,64,128]{2,1,0:T(8,128)(2,1)} %broadcast_in_dim.2), calls=%async_computation.1 | async-start | bytes 262144 | tf_op jit(solution)/shard_map/all_to_all | solution.py:97
  66.8 1.2 %copy-start = (f32[1024,256]{1,0:T(8,128)S(1)}, f32[1024,256]{1,0:T(8,128)}, u32[]{:S(2)}) copy-start(f32[1024,256]{1,0:T(8,128)} %get-tuple-element.24) | copy-start | bytes 3145732

commit v5 on v4

--- a/solution.py
+++ b/solution.py
@@ -31,7 +31,7 @@
 def _softmax_kernel(x_ref, p_ref, h_ref):
     x = x_ref[...]
     e = jnp.exp(x - jnp.max(x, axis=-1, keepdims=True))
-    p = e / jnp.sum(e, axis=-1, keepdims=True)
+    p = e * (1.0 / jnp.sum(e, axis=-1, keepdims=True))
     p_ref[...] = p
     half = p.astype(jnp.bfloat16)
     width = h_ref.shape[-1]
@@ -42,7 +42,7 @@
 def _softmax(logits, block_size):
     rows, width = logits.shape
     halves = width // block_size
-    step = min(rows, 256)
+    step = min(rows, 512)
     return pl.pallas_call(
         _softmax_kernel,
         grid=(rows // step,),
@@ -77,7 +77,7 @@
     probs, probs_split = _softmax(logits, block_size)
     segments, halves = probs_split.shape[1], probs_split.shape[0]
     probs_half = probs_split.reshape(-1, block_size)
-    split_idx = (pattern_idx % halves) * segments + pattern_idx // halves
+    split_idx = lax.optimization_barrier((pattern_idx % halves) * segments + pattern_idx // halves)
     picked = _take_rows(probs_half, split_idx)
     contrib = (
         jnp.einsum("tq,tqe->te", picked, tile_block, preferred_element_type=jnp.float32)

time: 70 us -> 68.6 us (0.980)
  Pallas kernels: 3.79 us -> 2.42 us
    pallas_call x1, Pallas kernels: 3.79 us -> 2.42 us  [_softmax(): pl.pallas_call(_softmax_kernel, grid=(rows // step,), in_specs=[pl.BlockS...]
where the time goes in v5:
time: 68.6 us; the launch traced here: 68.1 us
  matrix products  22.3 us (33%)
  waiting for transfers between devices  16.2 us (24%)
  starting transfers between devices  10.8 us (16%)
  blocking collectives  8.71 us (13%)
  other arithmetic  4.98 us (7%)
  Pallas kernels  2.42 us (4%)
  local copies, waits for them, and re-layouts  1.87 us (3%)
  between operations  0.77 us (1%)
    dot_general x1, matrix products, shards(): jnp.einsum('tqe,te->tq', tile_block, slot_grads, preferred_element_type=j...  9.46 us
    all_to_all x1, waiting for transfers between devices, shards(): lax.all_to_all(partial_value.reshape(groups, owned_blocks, block_size), '...  8.88 us
    all_gather x1, blocking collectives, shards(): gathered = lax.all_gather(packed, 'region', axis=0, tiled=False)  8.71 us
    all_to_all x1, waiting for transfers between devices, shards(): lax.all_to_all(spread, 'nets', 0, 0, tiled=False).reshape(-1, block_size)  7.34 us
    all_to_all x1, starting transfers between devices, shards(): lax.all_to_all(partial_value.reshape(groups, owned_blocks, block_size), '...  7.25 us
    dot_general x1, matrix products, shards(): jnp.einsum('tq,tqe->te', picked, tile_block, preferred_element_type=jnp.f...  6.36 us
    dot_general x2, matrix products, _add_rows(): lax.dot_general(sel, parts, (((0,), (0,)), ((), ())), preferred_element_t...  4.41 us
    all_to_all x1, starting transfers between devices, shards(): lax.all_to_all(spread, 'nets', 0, 0, tiled=False).reshape(-1, block_size)  3.59 us
  transfers between devices with their start and end apart: 2, of which 2 were waited for; matrix products, arithmetic and copies ran while one was open for 0% of the time, Pallas kernels for 0%

profile of v5, /device:TPU:0, one launch (start us, length us, event | category | flops | bytes accessed | tf_op | source)
XLA Modules:
  0.0 68.1 jit_solution(9227705540671900606)
XLA Ops:
  0.6 0.7 %reduce.3 = s32[384]{0:T(512)S(1)} reduce(s32[1,1,384]{2,1,0:T(1,128)} %param.12, s32[]{:T(128)} %constant.66.clone.1), dimensions={0,1}, to_apply=%param.12.reduce_sub_computation | reduce | bytes 3076 | tf_op args[2]
  1.3 0.7 %reduce.2 = s32[384]{0:T(512)S(1)} reduce(s32[1,1,384]{2,1,0:T(1,128)} %param.13, s32[]{:T(128)} %constant.66.clone.1), dimensions={0,1}, to_apply=%param.13.reduce_sub_computation | reduce | bytes 3076 | tf_op args[3]
  2.1 0.7 %fusion.28 = f32[8,48]{1,0:T(8,128)S(1)} fusion(s32[8]{0:T(128)} %bitcast.37), kind=kLoop, calls=%fused_computation.55 | loop fusion | flops 768 | bytes 1568 | tf_op jit(solution)/shard_map/convert_element_type | solution.py:76
  2.9 2.4 %shard_map.82 = (f32[1024,256]{1,0:T(8,128)}, bf16[2,1024,128]{2,1,0:T(8,128)(2,1)}) custom-call(f32[1024,256]{1,0:T(8,128)} %x_ref.1), custom_call_target="tpu_custom_call" | custom-call | flops 1310720 | bytes 2621440 | tf_op jit(solution)/shard_map/pallas_call | solution.py:46
  5.3 1.7 %fusion.14 = bf16[384,128,1]{1,0,2:T(8,128)(2,1)S(1)} fusion(bf16[2048,128]{1,0:T(8,128)(2,1)} %bitcast.38, s32[384]{0:T(512)S(1)} %fusion.32), kind=kOutput, calls=%fused_computation.21 | convolution fusion | flops 202162176 | bytes 624128 | tf_op jit(solution)/shard_map/dot_general | solution.py:14
  7.0 6.4 %fusion.2 = f32[384,1,128]{2,1,0:T(1,128)S(1)} fusion(bf16[1,1,384,128,128]{4,3,2,1,0:T(8,128)(2,1)} %param.11, bf16[384,128,1]{1,0,2:T(8,128)(2,1)S(1)} %fusion.14), kind=kOutput, calls=%fused_computation.2 | convolution fusion | flops 12582912 | bytes 12877824 | tf_op jit(solution)/shard_map/tq,tqe->te/dot_general | solution.py:83
  13.4 0.1 reduce-precision_convert_fusion.3
  13.5 0.5 fusion.17
  14.1 0.7 %slice_add_fusion.2 = f32[512,128]{1,0:T(8,128)} fusion(f32[512,384]{1,0:T(8,128)S(1)} %fusion.17), kind=kLoop, calls=%fused_computation.42 | loop fusion | flops 131072 | bytes 1048576 | tf_op jit(solution)/shard_map/add | solution.py:28
  14.8 7.3 %all-to-all-start = ((f32[8,64,128]{2,1,0:T(8,128)}), f32[8,64,128]{2,1,0:T(8,128)S(1)}, u32[]{:S(2)}, u32[]{:S(2)}) async-start(f32[8,64,128]{2,1,0:T(8,128)} %bitcast.6), calls=%async_computation | async-start | bytes 524288 | tf_op jit(solution)/shard_map/all_to_all | solution.py:91
  22.1 8.9 %all-to-all-done = f32[8,64,128]{2,1,0:T(8,128)S(1)} async-done(((f32[8,64,128]{2,1,0:T(8,128)}), f32[8,64,128]{2,1,0:T(8,128)S(1)}, u32[]{:S(2)}, u32[]{:S(2)}) %all-to-all-start) | async-done | bytes 262176 | tf_op jit(solution)/shard_map/all_to_all | solution.py:91
  31.0 0.7 broadcast_in_dim.2
  31.7 3.6 %all-to-all-start.1 = ((bf16[8,64,128]{2,1,0:T(8,128)(2,1)}), bf16[8,64,128]{2,1,0:T(8,128)(2,1)S(1)}, u32[]{:S(2)}, u32[]{:S(2)}) async-start(bf16[8,64,128]{2,1,0:T(8,128)(2,1)} %broadcast_in_dim.2), calls=%async_computation.1 | async-start | bytes 262144 | tf_op jit(solution)/shard_map/all_to_all | solution.py:97
  35.3 7.3 %all-to-all-done.1 = bf16[8,64,128]{2,1,0:T(8,128)(2,1)S(1)} async-done(((bf16[8,64,128]{2,1,0:T(8,128)(2,1)}), bf16[8,64,128]{2,1,0:T(8,128)(2,1)S(1)}, u32[]{:S(2)}, u32[]{:S(2)}) %all-to-all-start.1) | async-done | bytes 131104 | tf_op jit(solution)/shard_map/all_to_all | solution.py:97
  42.6 0.3 fusion.15
  42.9 9.5 %fusion = f32[384,1,128]{2,1,0:T(1,128)S(1)} fusion(bf16[1,1,384,128,128]{4,3,2,1,0:T(8,128)(2,1)} %param.11, bf16[384,128,1]{1,0,2:T(8,128)(2,1)S(1)} %fusion.15), kind=kOutput, calls=%fused_computation | convolution fusion | flops 12582912 | bytes 12877824 | tf_op jit(solution)/shard_map/tqe,te->tq/dot_general | solution.py:100
  52.4 0.1 broadcast_multiply_fusion
  52.6 8.7 %all-gather.1 = f32[4,387,128]{2,1,0:T(8,128)S(1)} all-gather(f32[1,387,128]{2,1,0:T(8,128)S(1)} %maximum_bitcast_fusion), channel_id=2, replica_groups=mesh['nets'=8,'region'=4] {'region'}, dimensions={0}, use_global_device_ids=true | all-gather | bytes 990720 | tf_op jit(solution)/shard_map/all_gather | solution.py:108
  61.4 0.2 reduce-precision_convert_fusion.1
  61.6 3.9 %fusion.4 = f32[2048,384]{1,0:T(8,128)S(1)} fusion(s32[1536]{0:T(1024)S(1)} %convert_element_type.61, bf16[1536,128]{1,0:T(8,128)(2,1)S(1)} %get-tuple-element.29, bf16[1536,128]{1,0:T(8,128)(2,1)S(1)} %get-tuple-element.30, bf16[1536,128]{1,0:T(8,128)(2,1)S(1)} %get-tuple-element.28), kind=kOutput, calls=%fused_computation.5 | convolution fusion | flops 2422603776 | bytes 4331520 | tf_op jit(solution)/shard_map/dot_general | solution.py:24
  65.5 0.1 slice_add_fusion
  65.7 1.0 %copy-done = f32[1024,256]{1,0:T(8,128)S(1)} copy-done((f32[1024,256]{1,0:T(8,128)S(1)}, f32[1024,256]{1,0:T(8,128)}, u32[]{:S(2)}) %copy-start) | copy-done | bytes 1048600
  66.7 0.2 multiply_reduce_fusion
  66.9 1.2 %subtract_multiply_fusion = f32[1024,256]{1,0:T(8,128)} fusion(f32[1024,256]{1,0:T(8,128)S(1)} %copy-done, f32[1024,128]{1,0:T(8,128)S(1)} %get-tuple-element.27, f32[1024,128]{1,0:T(8,128)S(1)} %get-tuple-element.26, f32[1024]{0:T(1024)S(1)} %multiply_reduce_fusion), kind=kLoop, calls=%fused_computation.26 | loop fusion | flops 786432 | bytes 3149824 | tf_op jit(solution)/shard_map/mul | solution.py:117
  (17 shorter events, 0.3 us)
Async XLA Ops:
  13.4 8.7 %copy-start.2 = (s32[1,8192]{1,0:T(1,128)S(1)}, s32[1,8192]{1,0:T(1,128)}, u32[]{:S(2)}) copy-start(s32[1,8192]{1,0:T(1,128)} %param.15) | copy-start | bytes 98308
  14.8 16.2 %all-to-all-start = ((f32[8,64,128]{2,1,0:T(8,128)}), f32[8,64,128]{2,1,0:T(8,128)S(1)}, u32[]{:S(2)}, u32[]{:S(2)}) async-start(f32[8,64,128]{2,1,0:T(8,128)} %bitcast.6), calls=%async_computation | async-start | bytes 524288 | tf_op jit(solution)/shard_map/all_to_all | solution.py:91
  31.0 21.4 %copy-start.1 = (f32[64,128]{1,0:T(8,128)}, f32[64,128]{1,0:T(8,128)S(1)}, u32[]{:S(2)}) copy-start(f32[64,128]{1,0:T(8,128)S(1)} %reduce_sum.18) | copy-start | bytes 98308
  31.7 10.9 %all-to-all-start.1 = ((bf16[8,64,128]{2,1,0:T(8,128)(2,1)}), bf16[8,64,128]{2,1,0:T(8,128)(2,1)S(1)}, u32[]{:S(2)}, u32[]{:S(2)}) async-start(bf16[8,64,128]{2,1,0:T(8,128)(2,1)} %broadcast_in_dim.2), calls=%async_computation.1 | async-start | bytes 262144 | tf_op jit(solution)/shard_map/all_to_all | solution.py:97
  65.5 1.2 %copy-start = (f32[1024,256]{1,0:T(8,128)S(1)}, f32[1024,256]{1,0:T(8,128)}, u32[]{:S(2)}) copy-start(f32[1024,256]{1,0:T(8,128)} %get-tuple-element.24) | copy-start | bytes 3145732

commit v6 on v5

--- a/solution.py
+++ b/solution.py
@@ -80,7 +80,7 @@
     split_idx = lax.optimization_barrier((pattern_idx % halves) * segments + pattern_idx // halves)
     picked = _take_rows(probs_half, split_idx)
     contrib = (
-        jnp.einsum("tq,tqe->te", picked, tile_block, preferred_element_type=jnp.float32)
+        jnp.sum(picked.astype(jnp.float32)[:, :, None] * tile_block.astype(jnp.float32), axis=1)
         * weight_live[:, None]
     )
     capacity_f = capacity.reshape(-1, block_size).astype(jnp.float32)
@@ -97,7 +97,7 @@
     all_grads = lax.all_to_all(spread, "nets", 0, 0, tiled=False).reshape(-1, block_size)
     slot_grads = _take_rows(all_grads, target)
     dp_tiles = (
-        jnp.einsum("tqe,te->tq", tile_block, slot_grads, preferred_element_type=jnp.float32)
+        jnp.sum(tile_block.astype(jnp.float32) * slot_grads.astype(jnp.float32)[:, None, :], axis=2)
         * weight_live[:, None]
     )
     idx_rows = -(-tile_count // block_size)

time: 68.6 us -> 71.3 us (1.039)
  other arithmetic: 4.98 us -> 23.4 us
  matrix products: 22.3 us -> 6.45 us
    reduce_sum x0 -> x2, other arithmetic: none -> 18.4 us  [the longest x1 9.63 us: shards(): jnp.sum(tile_block.astype(jnp.float32) * slot_grads.astype(jnp.float32)[:...]
    dot_general x2 -> x0, matrix products: 15.8 us -> none  [the longest x1 9.46 us: shards(): jnp.einsum('tqe,te->tq', tile_block, slot_grads, preferred_element_type=j...]
where the time goes in v6:
time: 71.3 us; the launch traced here: 70.7 us
  other arithmetic  23.4 us (33%)
  waiting for transfers between devices  16.2 us (23%)
  starting transfers between devices  10.8 us (15%)
  blocking collectives  8.71 us (12%)
  matrix products  6.45 us (9%)
  Pallas kernels  2.42 us (3%)
  local copies, waits for them, and re-layouts  1.88 us (3%)
  between operations  0.8 us (1%)
    reduce_sum x1, other arithmetic, shards(): jnp.sum(tile_block.astype(jnp.float32) * slot_grads.astype(jnp.float32)[:...  9.63 us
    all_to_all x1, waiting for transfers between devices, shards(): lax.all_to_all(partial_value.reshape(groups, owned_blocks, block_size), '...  8.88 us
    reduce_sum x1, other arithmetic, shards(): jnp.sum(picked.astype(jnp.float32)[:, :, None] * tile_block.astype(jnp.fl...  8.8 us
    all_gather x1, blocking collectives, shards(): gathered = lax.all_gather(packed, 'region', axis=0, tiled=False)  8.71 us
    all_to_all x1, waiting for transfers between devices, shards(): lax.all_to_all(spread, 'nets', 0, 0, tiled=False).reshape(-1, block_size)  7.34 us
    all_to_all x1, starting transfers between devices, shards(): lax.all_to_all(partial_value.reshape(groups, owned_blocks, block_size), '...  7.26 us
    dot_general x2, matrix products, _add_rows(): lax.dot_general(sel, parts, (((0,), (0,)), ((), ())), preferred_element_t...  4.41 us
    all_to_all x1, starting transfers between devices, shards(): lax.all_to_all(spread, 'nets', 0, 0, tiled=False).reshape(-1, block_size)  3.59 us
  transfers between devices with their start and end apart: 2, of which 2 were waited for; matrix products, arithmetic and copies ran while one was open for 0% of the time, Pallas kernels for 0%

profile of v6, /device:TPU:0, one launch (start us, length us, event | category | flops | bytes accessed | tf_op | source)
XLA Modules:
  0.0 70.7 jit_solution(10158611202660682134)
XLA Ops:
  0.6 0.7 reduce.3
  1.3 0.7 reduce.2
  2.1 0.7 %fusion.24 = f32[8,48]{1,0:T(8,128)S(1)} fusion(s32[8]{0:T(128)} %bitcast.26), kind=kLoop, calls=%fused_computation.53 | loop fusion | flops 768 | bytes 1568 | tf_op jit(solution)/shard_map/convert_element_type | solution.py:76
  2.9 2.4 %shard_map.82 = (f32[1024,256]{1,0:T(8,128)}, bf16[2,1024,128]{2,1,0:T(8,128)(2,1)}) custom-call(f32[1024,256]{1,0:T(8,128)} %x_ref.1), custom_call_target="tpu_custom_call" | custom-call | flops 1310720 | bytes 2621440 | tf_op jit(solution)/shard_map/pallas_call | solution.py:46
  5.3 1.7 %fusion.12 = f32[384,128]{1,0:T(8,128)S(1)} fusion(bf16[2048,128]{1,0:T(8,128)(2,1)} %bitcast.27, s32[384]{0:T(512)S(1)} %fusion.28), kind=kOutput, calls=%fused_computation.16 | convolution fusion | flops 202211328 | bytes 722432 | tf_op jit(solution)/shard_map/dot_general | solution.py:14
  7.0 8.8 %fusion = f32[384,128]{1,0:T(8,128)S(1)} fusion(bf16[1,1,384,128,128]{4,3,2,1,0:T(8,128)(2,1)} %param.11, f32[384,128]{1,0:T(8,128)S(1)} %fusion.12), kind=kLoop, calls=%fused_computation.2 | loop fusion | flops 18825216 | bytes 12976128 | tf_op jit(solution)/shard_map/reduce_sum | solution.py:83
  15.8 0.1 reduce-precision_convert_fusion.3
  16.0 0.5 fusion.15
  16.5 0.7 %slice_add_fusion.2 = f32[512,128]{1,0:T(8,128)} fusion(f32[512,384]{1,0:T(8,128)S(1)} %fusion.15), kind=kLoop, calls=%fused_computation.42 | loop fusion | flops 131072 | bytes 1048576 | tf_op jit(solution)/shard_map/add | solution.py:28
  17.3 7.3 %all-to-all-start = ((f32[8,64,128]{2,1,0:T(8,128)}), f32[8,64,128]{2,1,0:T(8,128)S(1)}, u32[]{:S(2)}, u32[]{:S(2)}) async-start(f32[8,64,128]{2,1,0:T(8,128)} %bitcast.4), calls=%async_computation | async-start | bytes 524288 | tf_op jit(solution)/shard_map/all_to_all | solution.py:91
  24.5 8.9 %all-to-all-done = f32[8,64,128]{2,1,0:T(8,128)S(1)} async-done(((f32[8,64,128]{2,1,0:T(8,128)}), f32[8,64,128]{2,1,0:T(8,128)S(1)}, u32[]{:S(2)}, u32[]{:S(2)}) %all-to-all-start) | async-done | bytes 262176 | tf_op jit(solution)/shard_map/all_to_all | solution.py:91
  33.5 0.7 broadcast_in_dim.2
  34.1 3.6 %all-to-all-start.1 = ((bf16[8,64,128]{2,1,0:T(8,128)(2,1)}), bf16[8,64,128]{2,1,0:T(8,128)(2,1)S(1)}, u32[]{:S(2)}, u32[]{:S(2)}) async-start(bf16[8,64,128]{2,1,0:T(8,128)(2,1)} %broadcast_in_dim.2), calls=%async_computation.1 | async-start | bytes 262144 | tf_op jit(solution)/shard_map/all_to_all | solution.py:97
  37.7 7.3 %all-to-all-done.1 = bf16[8,64,128]{2,1,0:T(8,128)(2,1)S(1)} async-done(((bf16[8,64,128]{2,1,0:T(8,128)(2,1)}), bf16[8,64,128]{2,1,0:T(8,128)(2,1)S(1)}, u32[]{:S(2)}, u32[]{:S(2)}) %all-to-all-start.1) | async-done | bytes 131104 | tf_op jit(solution)/shard_map/all_to_all | solution.py:97
  45.1 0.3 fusion.13
  45.4 9.6 %fusion.1 = f32[384,128]{1,0:T(8,128)S(1)} fusion(bf16[1,1,384,128,128]{4,3,2,1,0:T(8,128)(2,1)} %param.11, f32[384,128]{1,0:T(8,128)S(1)} %fusion.13), kind=kLoop, calls=%fused_computation.3 | loop fusion | flops 18825216 | bytes 12976128 | tf_op jit(solution)/shard_map/reduce_sum | solution.py:100
  55.0 0.1 broadcast_multiply_fusion
  55.2 8.7 %all-gather.1 = f32[4,387,128]{2,1,0:T(8,128)S(1)} all-gather(f32[1,387,128]{2,1,0:T(8,128)S(1)} %maximum_bitcast_fusion), channel_id=2, replica_groups=mesh['nets'=8,'region'=4] {'region'}, dimensions={0}, use_global_device_ids=true | all-gather | bytes 990720 | tf_op jit(solution)/shard_map/all_gather | solution.py:108
  64.0 0.2 reduce-precision_convert_fusion.1
  64.2 3.9 %fusion.2 = f32[2048,384]{1,0:T(8,128)S(1)} fusion(s32[1536]{0:T(1024)S(1)} %convert_element_type.78, bf16[1536,128]{1,0:T(8,128)(2,1)S(1)} %get-tuple-element.29, bf16[1536,128]{1,0:T(8,128)(2,1)S(1)} %get-tuple-element.30, bf16[1536,128]{1,0:T(8,128)(2,1)S(1)} %get-tuple-element.28), kind=kOutput, calls=%fused_computation.5 | convolution fusion | flops 2422603776 | bytes 4331520 | tf_op jit(solution)/shard_map/dot_general | solution.py:24
  68.1 0.1 slice_add_fusion
  68.3 1.0 %copy-done = f32[1024,256]{1,0:T(8,128)S(1)} copy-done((f32[1024,256]{1,0:T(8,128)S(1)}, f32[1024,256]{1,0:T(8,128)}, u32[]{:S(2)}) %copy-start) | copy-done | bytes 1048600
  69.3 0.2 multiply_reduce_fusion
  69.5 1.2 %subtract_multiply_fusion = f32[1024,256]{1,0:T(8,128)} fusion(f32[1024,256]{1,0:T(8,128)S(1)} %copy-done, f32[1024,128]{1,0:T(8,128)S(1)} %get-tuple-element.27, f32[1024,128]{1,0:T(8,128)S(1)} %get-tuple-element.26, f32[1024]{0:T(1024)S(1)} %multiply_reduce_fusion), kind=kLoop, calls=%fused_computation.26 | loop fusion | flops 786432 | bytes 3149824 | tf_op jit(solution)/shard_map/mul | solution.py:117
  (17 shorter events, 0.3 us)
Async XLA Ops:
  15.8 8.7 %copy-start.2 = (s32[1,8192]{1,0:T(1,128)S(1)}, s32[1,8192]{1,0:T(1,128)}, u32[]{:S(2)}) copy-start(s32[1,8192]{1,0:T(1,128)} %param.15) | copy-start | bytes 98308
  17.3 16.2 %all-to-all-start = ((f32[8,64,128]{2,1,0:T(8,128)}), f32[8,64,128]{2,1,0:T(8,128)S(1)}, u32[]{:S(2)}, u32[]{:S(2)}) async-start(f32[8,64,128]{2,1,0:T(8,128)} %bitcast.4), calls=%async_computation | async-start | bytes 524288 | tf_op jit(solution)/shard_map/all_to_all | solution.py:91
  33.4 21.6 %copy-start.1 = (f32[64,128]{1,0:T(8,128)}, f32[64,128]{1,0:T(8,128)S(1)}, u32[]{:S(2)}) copy-start(f32[64,128]{1,0:T(8,128)S(1)} %reduce_sum.37) | copy-start | bytes 98308
  34.1 10.9 %all-to-all-start.1 = ((bf16[8,64,128]{2,1,0:T(8,128)(2,1)}), bf16[8,64,128]{2,1,0:T(8,128)(2,1)S(1)}, u32[]{:S(2)}, u32[]{:S(2)}) async-start(bf16[8,64,128]{2,1,0:T(8,128)(2,1)} %broadcast_in_dim.2), calls=%async_computation.1 | async-start | bytes 262144 | tf_op jit(solution)/shard_map/all_to_all | solution.py:97
  68.1 1.2 %copy-start = (f32[1024,256]{1,0:T(8,128)S(1)}, f32[1024,256]{1,0:T(8,128)}, u32[]{:S(2)}) copy-start(f32[1024,256]{1,0:T(8,128)} %get-tuple-element.24) | copy-start | bytes 3145732

commit v7 on v5

--- a/solution.py
+++ b/solution.py
@@ -85,17 +85,32 @@
     )
     capacity_f = capacity.reshape(-1, block_size).astype(jnp.float32)
     owned_blocks = capacity_f.shape[0]
-    owner_idx = jnp.arange(tile_count, dtype=jnp.int32) // slot_count
-    target = owner_idx * owned_blocks + edge_idx
-    partial_value = _add_rows(target, contrib, groups * owned_blocks)
-    received = lax.all_to_all(
-        partial_value.reshape(groups, owned_blocks, block_size), "nets", 0, 0, tiled=False
+    idx_rows = -(-slot_count // block_size)
+    rows_out = -(-(slot_count + idx_rows) // 8) * 8
+    edge_f = jnp.zeros((groups, idx_rows * block_size), jnp.float32).at[:, :slot_count].set(
+        edge_idx.reshape(groups, slot_count).astype(jnp.float32)
     )
-    usage_edges = jnp.sum(received, axis=0)
+    payload = jnp.concatenate(
+        [
+            contrib.reshape(groups, slot_count, block_size),
+            edge_f.reshape(groups, idx_rows, block_size),
+            jnp.zeros((groups, rows_out - slot_count - idx_rows, block_size), jnp.float32),
+        ],
+        axis=1,
+    )
+    received = lax.all_to_all(payload, "nets", 0, 0, tiled=False)
+    asked = (
+        received[:, slot_count : slot_count + idx_rows]
+        .reshape(groups, -1)[:, :slot_count]
+        .astype(jnp.int32)
+        .reshape(-1)
+    )
+    usage_edges = _add_rows(
+        asked, received[:, :slot_count].reshape(-1, block_size), owned_blocks
+    )
     edge_grad = jax.nn.sigmoid(usage_edges - capacity_f).astype(jnp.bfloat16)
-    spread = jnp.broadcast_to(edge_grad[None], (groups, owned_blocks, block_size))
-    all_grads = lax.all_to_all(spread, "nets", 0, 0, tiled=False).reshape(-1, block_size)
-    slot_grads = _take_rows(all_grads, target)
+    answer = _take_rows(edge_grad, asked).reshape(groups, slot_count, block_size)
+    slot_grads = lax.all_to_all(answer, "nets", 0, 0, tiled=False).reshape(-1, block_size)
     dp_tiles = (
         jnp.einsum("tqe,te->tq", tile_block, slot_grads, preferred_element_type=jnp.float32)
         * weight_live[:, None]

time: 68.6 us -> 68.9 us (level)
  other arithmetic: 4.98 us -> 6.3 us
  waiting for transfers between devices: 16.2 us -> 15.5 us
    reshape x0 -> x1, other arithmetic: none -> 1.34 us  [shards(): edge_f.reshape(groups, idx_rows, block_size)]
    concatenate x0 -> x1, other arithmetic: none -> 0.76 us  [shards(): jnp.concatenate([contrib.reshape(groups, slot_count, block_size), edge_f....]
    add x2, other arithmetic: 0.87 us -> 0.15 us  [_add_rows(): return out[:, :width] + out[:, width:2 * width] + out[:, 2 * width:]]
    all_to_all x2, waiting for transfers between devices: 16.2 us -> 15.5 us  [the longest x1 8.4 us: shards(): received = lax.all_to_all(payload, 'nets', 0, 0, tiled=False)]
    unnamed x3 -> x2, other arithmetic: 1.41 us -> 0.72 us
where the time goes in v7:
time: 68.9 us; the launch traced here: 68.4 us
  matrix products  22.6 us (33%)
  waiting for transfers between devices  15.5 us (22%)
  starting transfers between devices  10.6 us (15%)
  blocking collectives  8.71 us (13%)
  other arithmetic  6.3 us (9%)
  Pallas kernels  2.42 us (4%)
  local copies, waits for them, and re-layouts  1.48 us (2%)
  between operations  0.79 us (1%)
    dot_general x1, matrix products, shards(): jnp.einsum('tqe,te->tq', tile_block, slot_grads, preferred_element_type=j...  9.45 us
    all_gather x1, blocking collectives, shards(): gathered = lax.all_gather(packed, 'region', axis=0, tiled=False)  8.71 us
    all_to_all x1, waiting for transfers between devices, shards(): received = lax.all_to_all(payload, 'nets', 0, 0, tiled=False)  8.4 us
    all_to_all x1, starting transfers between devices, shards(): received = lax.all_to_all(payload, 'nets', 0, 0, tiled=False)  7.25 us
    all_to_all x1, waiting for transfers between devices, shards(): lax.all_to_all(answer, 'nets', 0, 0, tiled=False).reshape(-1, block_size)  7.11 us
    dot_general x1, matrix products, shards(): jnp.einsum('tq,tqe->te', picked, tile_block, preferred_element_type=jnp.f...  6.36 us
    dot_general x2, matrix products, _add_rows(): lax.dot_general(sel, parts, (((0,), (0,)), ((), ())), preferred_element_t...  4.17 us
    all_to_all x1, starting transfers between devices, shards(): lax.all_to_all(answer, 'nets', 0, 0, tiled=False).reshape(-1, block_size)  3.37 us
  transfers between devices with their start and end apart: 2, of which 2 were waited for; matrix products, arithmetic and copies ran while one was open for 0% of the time, Pallas kernels for 0%

profile of v7, /device:TPU:0, one launch (start us, length us, event | category | flops | bytes accessed | tf_op | source)
XLA Modules:
  0.0 68.4 jit_solution(5400022914521498651)
XLA Ops:
  0.6 0.6 compare_reduce_fusion
  1.3 1.3 %fusion.35 = f32[384]{0:T(512)S(1)} fusion(pred[]{:T(512)} %compare_reduce_fusion, s32[1,1,384]{2,1,0:T(1,128)} %param.15), kind=kLoop, calls=%fused_computation.73 | loop fusion | flops 768 | bytes 3073 | tf_op jit(solution)/shard_map/reshape | solution.py:96
  2.7 0.7 %reduce.9 = s32[384]{0:T(512)S(1)} reduce(s32[1,1,384]{2,1,0:T(1,128)} %param.14, s32[]{:T(128)} %constant.87.clone.1), dimensions={0,1}, to_apply=%param.14.reduce_sub_computation | reduce | bytes 3076 | tf_op args[2]
  3.4 0.7 %fusion.30 = f32[8,48]{1,0:T(8,128)S(1)} fusion(s32[8]{0:T(128)} %bitcast.49), kind=kLoop, calls=%fused_computation.59 | loop fusion | flops 768 | bytes 1568 | tf_op jit(solution)/shard_map/convert_element_type | solution.py:76
  4.2 2.4 %shard_map.82 = (f32[1024,256]{1,0:T(8,128)}, bf16[2,1024,128]{2,1,0:T(8,128)(2,1)}) custom-call(f32[1024,256]{1,0:T(8,128)} %x_ref.1), custom_call_target="tpu_custom_call" | custom-call | flops 1310720 | bytes 2621440 | tf_op jit(solution)/shard_map/pallas_call | solution.py:46
  6.7 1.7 %fusion.14 = bf16[384,128,1]{1,0,2:T(8,128)(2,1)S(1)} fusion(bf16[2048,128]{1,0:T(8,128)(2,1)} %bitcast.50, s32[384]{0:T(512)S(1)} %fusion.32), kind=kOutput, calls=%fused_computation.21 | convolution fusion | flops 202162176 | bytes 624128 | tf_op jit(solution)/shard_map/dot_general | solution.py:14
  8.5 6.4 %fusion.2 = f32[384,1,128]{2,1,0:T(1,128)S(1)} fusion(bf16[1,1,384,128,128]{4,3,2,1,0:T(8,128)(2,1)} %param.13, bf16[384,128,1]{1,0,2:T(8,128)(2,1)S(1)} %fusion.14), kind=kOutput, calls=%fused_computation.2 | convolution fusion | flops 12582912 | bytes 12877824 | tf_op jit(solution)/shard_map/tq,tqe->te/dot_general | solution.py:83
  14.8 0.1 broadcast_multiply_fusion.1
  14.9 0.8 %fusion.22 = f32[8,56,128]{2,1,0:T(8,128)} fusion(f32[8,1,48]{2,1,0:T(1,128)S(1)} %bitcast.47, f32[8,48,128]{2,1,0:T(8,128)S(1)} %bitcast.43, f32[56]{0:T(128)S(1)} %pad.18.clone), kind=kLoop, calls=%fused_computation.41 | loop fusion | flops 344064 | bytes 427744 | tf_op jit(solution)/shard_map/concatenate | solution.py:93
  15.7 7.3 %all-to-all-start = ((f32[8,56,128]{2,1,0:T(8,128)}), f32[8,56,128]{2,1,0:T(8,128)S(1)}, u32[]{:S(2)}, u32[]{:S(2)}) async-start(f32[8,56,128]{2,1,0:T(8,128)} %fusion.22), calls=%async_computation | async-start | bytes 458752 | tf_op jit(solution)/shard_map/all_to_all | solution.py:101
  23.0 8.4 %all-to-all-done = f32[8,56,128]{2,1,0:T(8,128)S(1)} async-done(((f32[8,56,128]{2,1,0:T(8,128)}), f32[8,56,128]{2,1,0:T(8,128)S(1)}, u32[]{:S(2)}, u32[]{:S(2)}) %all-to-all-start) | async-done | bytes 229408 | tf_op jit(solution)/shard_map/all_to_all | solution.py:101
  31.6 0.3 fusion.16
  31.9 0.9 %convolution_convert_fusion = bf16[384,128]{1,0:T(8,128)(2,1)} fusion(s32[384]{0:T(512)S(1)} %eq.25, f32[64,128]{1,0:T(8,128)S(1)} %slice_add_fusion.2, f32[64,128]{1,0:T(8,128)S(1)} %bitcast.45), kind=kOutput, calls=%fused_computation.16 | convolution fusion | flops 6406144 | bytes 165376 | tf_op jit(solution)/shard_map/dot_general | solution.py:14
  32.8 3.4 %all-to-all-start.1 = ((bf16[8,48,128]{2,1,0:T(8,128)(2,1)}), bf16[8,48,128]{2,1,0:T(8,128)(2,1)S(1)}, u32[]{:S(2)}, u32[]{:S(2)}) async-start(bf16[8,48,128]{2,1,0:T(8,128)(2,1)} %bitcast.11), calls=%async_computation.1 | async-start | bytes 196608 | tf_op jit(solution)/shard_map/all_to_all | solution.py:113
  36.2 7.1 %all-to-all-done.1 = bf16[8,48,128]{2,1,0:T(8,128)(2,1)S(1)} async-done(((bf16[8,48,128]{2,1,0:T(8,128)(2,1)}), bf16[8,48,128]{2,1,0:T(8,128)(2,1)S(1)}, u32[]{:S(2)}, u32[]{:S(2)}) %all-to-all-start.1) | async-done | bytes 98336 | tf_op jit(solution)/shard_map/all_to_all | solution.py:113
  43.3 9.5 %fusion = f32[384,1,128]{2,1,0:T(1,128)S(1)} fusion(bf16[1,1,384,128,128]{4,3,2,1,0:T(8,128)(2,1)} %param.13, bf16[384,128,1]{1,0,2:T(8,128)(2,1)S(1)} %bitcast.42), kind=kOutput, calls=%fused_computation | convolution fusion | flops 12582912 | bytes 12877824 | tf_op jit(solution)/shard_map/tqe,te->tq/dot_general | solution.py:115
  52.7 0.1 broadcast_multiply_fusion
  52.9 8.7 %all-gather.1 = f32[4,387,128]{2,1,0:T(8,128)S(1)} all-gather(f32[1,387,128]{2,1,0:T(8,128)S(1)} %maximum_bitcast_fusion), channel_id=2, replica_groups=mesh['nets'=8,'region'=4] {'region'}, dimensions={0}, use_global_device_ids=true | all-gather | bytes 990720 | tf_op jit(solution)/shard_map/all_gather | solution.py:123
  61.7 0.2 reduce-precision_convert_fusion.1
  61.9 3.9 %fusion.4 = f32[2048,384]{1,0:T(8,128)S(1)} fusion(s32[1536]{0:T(1024)S(1)} %convert_element_type.67, bf16[1536,128]{1,0:T(8,128)(2,1)S(1)} %get-tuple-element.41, bf16[1536,128]{1,0:T(8,128)(2,1)S(1)} %get-tuple-element.42, bf16[1536,128]{1,0:T(8,128)(2,1)S(1)} %get-tuple-element.40), kind=kOutput, calls=%fused_computation.5 | convolution fusion | flops 2422603776 | bytes 4331520 | tf_op jit(solution)/shard_map/dot_general | solution.py:24
  65.8 0.1 slice_add_fusion
  66.0 1.0 %copy-done = f32[1024,256]{1,0:T(8,128)S(1)} copy-done((f32[1024,256]{1,0:T(8,128)S(1)}, f32[1024,256]{1,0:T(8,128)}, u32[]{:S(2)}) %copy-start) | copy-done | bytes 1048600
  67.0 0.2 multiply_reduce_fusion
  67.2 1.2 %subtract_multiply_fusion = f32[1024,256]{1,0:T(8,128)} fusion(f32[1024,256]{1,0:T(8,128)S(1)} %copy-done, f32[1024,128]{1,0:T(8,128)S(1)} %get-tuple-element.39, f32[1024,128]{1,0:T(8,128)S(1)} %get-tuple-element.38, f32[1024]{0:T(1024)S(1)} %multiply_reduce_fusion), kind=kLoop, calls=%fused_computation.25 | loop fusion | flops 786432 | bytes 3149824 | tf_op jit(solution)/shard_map/mul | solution.py:132
  (23 shorter events, 0.6 us)
Async XLA Ops:
  8.4 14.5 %copy-start.1 = (s32[1,8192]{1,0:T(1,128)S(1)}, s32[1,8192]{1,0:T(1,128)}, u32[]{:S(2)}) copy-start(s32[1,8192]{1,0:T(1,128)} %param.17) | copy-start | bytes 98308
  15.7 15.7 %all-to-all-start = ((f32[8,56,128]{2,1,0:T(8,128)}), f32[8,56,128]{2,1,0:T(8,128)S(1)}, u32[]{:S(2)}, u32[]{:S(2)}) async-start(f32[8,56,128]{2,1,0:T(8,128)} %fusion.22), calls=%async_computation | async-start | bytes 458752 | tf_op jit(solution)/shard_map/all_to_all | solution.py:101
  31.9 20.8 %copy-start.2 = (f32[64,128]{1,0:T(8,128)}, f32[64,128]{1,0:T(8,128)S(1)}, u32[]{:S(2)}) copy-start(f32[64,128]{1,0:T(8,128)S(1)} %slice_add_fusion.2) | copy-start | bytes 98308
  32.8 10.5 %all-to-all-start.1 = ((bf16[8,48,128]{2,1,0:T(8,128)(2,1)}), bf16[8,48,128]{2,1,0:T(8,128)(2,1)S(1)}, u32[]{:S(2)}, u32[]{:S(2)}) async-start(bf16[8,48,128]{2,1,0:T(8,128)(2,1)} %bitcast.11), calls=%async_computation.1 | async-start | bytes 196608 | tf_op jit(solution)/shard_map/all_to_all | solution.py:113
  65.8 1.2 %copy-start = (f32[1024,256]{1,0:T(8,128)S(1)}, f32[1024,256]{1,0:T(8,128)}, u32[]{:S(2)}) copy-start(f32[1024,256]{1,0:T(8,128)} %get-tuple-element.36) | copy-start | bytes 3145732

commit v8 on v5

--- a/solution.py
+++ b/solution.py
@@ -67,9 +67,12 @@
     tile_count = tile_block.shape[0]
     block_size = tile_block.shape[1]
     slot_count = tile_count // groups
-    pattern_idx = tile_pattern[0, 0]
-    edge_idx = tile_edge[0, 0]
-    counts = tile_counts[0, 0]
+    index_args = lax.optimization_barrier(
+        jnp.concatenate([tile_pattern.reshape(-1), tile_edge.reshape(-1), tile_counts.reshape(-1)])
+    )
+    pattern_idx = index_args[:tile_count]
+    edge_idx = index_args[tile_count : 2 * tile_count]
+    counts = index_args[2 * tile_count :]
     live_slot = (jnp.arange(slot_count, dtype=jnp.int32)[None, :] < counts[:, None]).reshape(
         tile_count
     )

time: 68.6 us -> 68.6 us (level)
  no operation moved by 1% of the time
where the time goes in v8:
time: 68.6 us; the launch traced here: 68.1 us
  matrix products  22.3 us (33%)
  waiting for transfers between devices  16.2 us (24%)
  starting transfers between devices  10.8 us (16%)
  blocking collectives  8.71 us (13%)
  other arithmetic  4.97 us (7%)
  Pallas kernels  2.42 us (4%)
  local copies, waits for them, and re-layouts  1.89 us (3%)
  between operations  0.77 us (1%)
    dot_general x1, matrix products, shards(): jnp.einsum('tqe,te->tq', tile_block, slot_grads, preferred_element_type=j...  9.46 us
    all_to_all x1, waiting for transfers between devices, shards(): lax.all_to_all(partial_value.reshape(groups, owned_blocks, block_size), '...  8.88 us
    all_gather x1, blocking collectives, shards(): gathered = lax.all_gather(packed, 'region', axis=0, tiled=False)  8.71 us
    all_to_all x1, waiting for transfers between devices, shards(): lax.all_to_all(spread, 'nets', 0, 0, tiled=False).reshape(-1, block_size)  7.34 us
    all_to_all x1, starting transfers between devices, shards(): lax.all_to_all(partial_value.reshape(groups, owned_blocks, block_size), '...  7.25 us
    dot_general x1, matrix products, shards(): jnp.einsum('tq,tqe->te', picked, tile_block, preferred_element_type=jnp.f...  6.36 us
    dot_general x2, matrix products, _add_rows(): lax.dot_general(sel, parts, (((0,), (0,)), ((), ())), preferred_element_t...  4.41 us
    all_to_all x1, starting transfers between devices, shards(): lax.all_to_all(spread, 'nets', 0, 0, tiled=False).reshape(-1, block_size)  3.59 us
  transfers between devices with their start and end apart: 2, of which 2 were waited for; matrix products, arithmetic and copies ran while one was open for 0% of the time, Pallas kernels for 0%

profile of v8, /device:TPU:0, one launch (start us, length us, event | category | flops | bytes accessed | tf_op | source)
XLA Modules:
  0.0 68.1 jit_solution(13252851943416201544)
XLA Ops:
  0.6 0.7 %reduce.2 = s32[384]{0:T(512)S(1)} reduce(s32[1,1,384]{2,1,0:T(1,128)} %param.12, s32[]{:T(128)} %constant.66.clone.1), dimensions={0,1}, to_apply=%param.12.reduce_sub_computation | reduce | bytes 3076 | tf_op args[2]
  1.3 0.7 %reduce.3 = s32[384]{0:T(512)S(1)} reduce(s32[1,1,384]{2,1,0:T(1,128)} %param.13, s32[]{:T(128)} %constant.66.clone.1), dimensions={0,1}, to_apply=%param.13.reduce_sub_computation | reduce | bytes 3076 | tf_op args[3]
  2.0 0.7 pad_add_fusion
  2.9 2.4 %shard_map.82 = (f32[1024,256]{1,0:T(8,128)}, bf16[2,1024,128]{2,1,0:T(8,128)(2,1)}) custom-call(f32[1024,256]{1,0:T(8,128)} %x_ref.1), custom_call_target="tpu_custom_call" | custom-call | flops 1310720 | bytes 2621440 | tf_op jit(solution)/shard_map/pallas_call | solution.py:46
  5.3 1.7 %fusion.14 = bf16[384,128,1]{1,0,2:T(8,128)(2,1)S(1)} fusion(bf16[2048,128]{1,0:T(8,128)(2,1)} %bitcast.38, s32[384]{0:T(512)S(1)} %get-tuple-element.35), kind=kOutput, calls=%fused_computation.21 | convolution fusion | flops 202162176 | bytes 624128 | tf_op jit(solution)/shard_map/dot_general | solution.py:14
  7.0 6.4 %fusion.2 = f32[384,1,128]{2,1,0:T(1,128)S(1)} fusion(bf16[1,1,384,128,128]{4,3,2,1,0:T(8,128)(2,1)} %param.11, bf16[384,128,1]{1,0,2:T(8,128)(2,1)S(1)} %fusion.14), kind=kOutput, calls=%fused_computation.2 | convolution fusion | flops 12582912 | bytes 12877824 | tf_op jit(solution)/shard_map/tq,tqe->te/dot_general | solution.py:86
  13.4 0.1 reduce-precision_convert_fusion.3
  13.5 0.5 fusion.17
  14.1 0.7 %slice_add_fusion.2 = f32[512,128]{1,0:T(8,128)} fusion(f32[512,384]{1,0:T(8,128)S(1)} %fusion.17), kind=kLoop, calls=%fused_computation.42 | loop fusion | flops 131072 | bytes 1048576 | tf_op jit(solution)/shard_map/add | solution.py:28
  14.8 7.3 %all-to-all-start = ((f32[8,64,128]{2,1,0:T(8,128)}), f32[8,64,128]{2,1,0:T(8,128)S(1)}, u32[]{:S(2)}, u32[]{:S(2)}) async-start(f32[8,64,128]{2,1,0:T(8,128)} %bitcast.6), calls=%async_computation | async-start | bytes 524288 | tf_op jit(solution)/shard_map/all_to_all | solution.py:94
  22.1 8.9 %all-to-all-done = f32[8,64,128]{2,1,0:T(8,128)S(1)} async-done(((f32[8,64,128]{2,1,0:T(8,128)}), f32[8,64,128]{2,1,0:T(8,128)S(1)}, u32[]{:S(2)}, u32[]{:S(2)}) %all-to-all-start) | async-done | bytes 262176 | tf_op jit(solution)/shard_map/all_to_all | solution.py:94
  31.0 0.7 broadcast_in_dim.2
  31.7 3.6 %all-to-all-start.1 = ((bf16[8,64,128]{2,1,0:T(8,128)(2,1)}), bf16[8,64,128]{2,1,0:T(8,128)(2,1)S(1)}, u32[]{:S(2)}, u32[]{:S(2)}) async-start(bf16[8,64,128]{2,1,0:T(8,128)(2,1)} %broadcast_in_dim.2), calls=%async_computation.1 | async-start | bytes 262144 | tf_op jit(solution)/shard_map/all_to_all | solution.py:100
  35.3 7.3 %all-to-all-done.1 = bf16[8,64,128]{2,1,0:T(8,128)(2,1)S(1)} async-done(((bf16[8,64,128]{2,1,0:T(8,128)(2,1)}), bf16[8,64,128]{2,1,0:T(8,128)(2,1)S(1)}, u32[]{:S(2)}, u32[]{:S(2)}) %all-to-all-start.1) | async-done | bytes 131104 | tf_op jit(solution)/shard_map/all_to_all | solution.py:100
  42.6 0.3 fusion.15
  43.0 9.5 %fusion = f32[384,1,128]{2,1,0:T(1,128)S(1)} fusion(bf16[1,1,384,128,128]{4,3,2,1,0:T(8,128)(2,1)} %param.11, bf16[384,128,1]{1,0,2:T(8,128)(2,1)S(1)} %fusion.15), kind=kOutput, calls=%fused_computation | convolution fusion | flops 12582912 | bytes 12877824 | tf_op jit(solution)/shard_map/tqe,te->tq/dot_general | solution.py:103
  52.4 0.1 broadcast_multiply_fusion
  52.6 8.7 %all-gather.1 = f32[4,387,128]{2,1,0:T(8,128)S(1)} all-gather(f32[1,387,128]{2,1,0:T(8,128)S(1)} %maximum_bitcast_fusion), channel_id=2, replica_groups=mesh['nets'=8,'region'=4] {'region'}, dimensions={0}, use_global_device_ids=true | all-gather | bytes 990720 | tf_op jit(solution)/shard_map/all_gather | solution.py:111
  61.4 0.2 reduce-precision_convert_fusion.1
  61.6 3.9 %fusion.4 = f32[2048,384]{1,0:T(8,128)S(1)} fusion(s32[1536]{0:T(1024)S(1)} %convert_element_type.61, bf16[1536,128]{1,0:T(8,128)(2,1)S(1)} %get-tuple-element.29, bf16[1536,128]{1,0:T(8,128)(2,1)S(1)} %get-tuple-element.30, bf16[1536,128]{1,0:T(8,128)(2,1)S(1)} %get-tuple-element.28), kind=kOutput, calls=%fused_computation.5 | convolution fusion | flops 2422603776 | bytes 4331520 | tf_op jit(solution)/shard_map/dot_general | solution.py:24
  65.5 0.1 slice_add_fusion
  65.7 1.0 %copy-done = f32[1024,256]{1,0:T(8,128)S(1)} copy-done((f32[1024,256]{1,0:T(8,128)S(1)}, f32[1024,256]{1,0:T(8,128)}, u32[]{:S(2)}) %copy-start) | copy-done | bytes 1048600
  66.7 0.2 multiply_reduce_fusion
  66.9 1.2 %subtract_multiply_fusion = f32[1024,256]{1,0:T(8,128)} fusion(f32[1024,256]{1,0:T(8,128)S(1)} %copy-done, f32[1024,128]{1,0:T(8,128)S(1)} %get-tuple-element.27, f32[1024,128]{1,0:T(8,128)S(1)} %get-tuple-element.26, f32[1024]{0:T(1024)S(1)} %multiply_reduce_fusion), kind=kLoop, calls=%fused_computation.26 | loop fusion | flops 786432 | bytes 3149824 | tf_op jit(solution)/shard_map/mul | solution.py:120
  (18 shorter events, 0.4 us)
Async XLA Ops:
  13.4 8.7 %copy-start.2 = (s32[1,8192]{1,0:T(1,128)S(1)}, s32[1,8192]{1,0:T(1,128)}, u32[]{:S(2)}) copy-start(s32[1,8192]{1,0:T(1,128)} %param.15) | copy-start | bytes 98308
  14.8 16.2 %all-to-all-start = ((f32[8,64,128]{2,1,0:T(8,128)}), f32[8,64,128]{2,1,0:T(8,128)S(1)}, u32[]{:S(2)}, u32[]{:S(2)}) async-start(f32[8,64,128]{2,1,0:T(8,128)} %bitcast.6), calls=%async_computation | async-start | bytes 524288 | tf_op jit(solution)/shard_map/all_to_all | solution.py:94
  31.0 21.4 %copy-start.1 = (f32[64,128]{1,0:T(8,128)}, f32[64,128]{1,0:T(8,128)S(1)}, u32[]{:S(2)}) copy-start(f32[64,128]{1,0:T(8,128)S(1)} %reduce_sum.18) | copy-start | bytes 98308
  31.7 10.9 %all-to-all-start.1 = ((bf16[8,64,128]{2,1,0:T(8,128)(2,1)}), bf16[8,64,128]{2,1,0:T(8,128)(2,1)S(1)}, u32[]{:S(2)}, u32[]{:S(2)}) async-start(bf16[8,64,128]{2,1,0:T(8,128)(2,1)} %broadcast_in_dim.2), calls=%async_computation.1 | async-start | bytes 262144 | tf_op jit(solution)/shard_map/all_to_all | solution.py:100
  65.5 1.2 %copy-start = (f32[1024,256]{1,0:T(8,128)S(1)}, f32[1024,256]{1,0:T(8,128)}, u32[]{:S(2)}) copy-start(f32[1024,256]{1,0:T(8,128)} %get-tuple-element.24) | copy-start | bytes 3145732

commit v9 on v6

--- a/solution.py
+++ b/solution.py
@@ -5,25 +5,24 @@
 from jax.sharding import PartitionSpec as P
 
 
-def _one_hot(idx, size, dtype):
-    return (idx[:, None] == jnp.arange(size, dtype=jnp.int32)[None, :]).astype(dtype)
+def _one_hot_t(idx_row, size, dtype):
+    return (jnp.arange(size, dtype=jnp.int32)[:, None] == idx_row).astype(dtype)
 
 
-def _take_rows(table, idx):
-    sel = _one_hot(idx, table.shape[0], table.dtype)
-    return jnp.dot(sel, table, preferred_element_type=jnp.float32).astype(table.dtype)
+def _take_rows(table, idx_row):
+    sel = _one_hot_t(idx_row, table.shape[0], table.dtype)
+    out = lax.dot_general(sel, table, (((0,), (0,)), ((), ())), preferred_element_type=jnp.float32)
+    return out.astype(table.dtype)
 
 
-def _add_rows(idx, rows, size):
+def _add_rows(idx_row, rows, size):
     hi = lax.reduce_precision(rows, exponent_bits=8, mantissa_bits=7)
     rest = rows - hi
     mid = lax.reduce_precision(rest, exponent_bits=8, mantissa_bits=7)
     lo = rest - mid
     parts = jnp.concatenate([hi, mid, lo], axis=1).astype(jnp.bfloat16)
-    sel = _one_hot(idx, size, jnp.bfloat16)
-    out = lax.dot_general(
-        sel, parts, (((0,), (0,)), ((), ())), preferred_element_type=jnp.float32
-    )
+    sel = _one_hot_t(idx_row, size, jnp.bfloat16)
+    out = jnp.dot(sel, parts, preferred_element_type=jnp.float32)
     width = rows.shape[1]
     return out[:, :width] + out[:, width : 2 * width] + out[:, 2 * width :]
 
@@ -67,27 +66,27 @@
     tile_count = tile_block.shape[0]
     block_size = tile_block.shape[1]
     slot_count = tile_count // groups
-    pattern_idx = tile_pattern[0, 0]
-    edge_idx = tile_edge[0, 0]
-    counts = tile_counts[0, 0]
-    live_slot = (jnp.arange(slot_count, dtype=jnp.int32)[None, :] < counts[:, None]).reshape(
-        tile_count
+    pattern_idx = tile_pattern[0]
+    edge_idx = tile_edge[0]
+    counts = tile_counts[0]
+    slot = jnp.arange(tile_count, dtype=jnp.int32)[None, :]
+    owner_idx = slot // slot_count
+    slot_limit = jnp.sum(
+        jnp.where(owner_idx == jnp.arange(groups, dtype=jnp.int32)[:, None], counts.T, 0),
+        axis=0,
+        keepdims=True,
     )
-    weight_live = live_slot.astype(jnp.float32)
+    live = slot % slot_count < slot_limit
     probs, probs_split = _softmax(logits, block_size)
     segments, halves = probs_split.shape[1], probs_split.shape[0]
     probs_half = probs_split.reshape(-1, block_size)
-    split_idx = lax.optimization_barrier((pattern_idx % halves) * segments + pattern_idx // halves)
+    split_idx = (pattern_idx % halves) * segments + pattern_idx // halves
     picked = _take_rows(probs_half, split_idx)
-    contrib = (
-        jnp.sum(picked.astype(jnp.float32)[:, :, None] * tile_block.astype(jnp.float32), axis=1)
-        * weight_live[:, None]
-    )
+    contrib = jnp.einsum("tq,tqe->te", picked, tile_block, preferred_element_type=jnp.float32)
     capacity_f = capacity.reshape(-1, block_size).astype(jnp.float32)
     owned_blocks = capacity_f.shape[0]
-    owner_idx = jnp.arange(tile_count, dtype=jnp.int32) // slot_count
     target = owner_idx * owned_blocks + edge_idx
-    partial_value = _add_rows(target, contrib, groups * owned_blocks)
+    partial_value = _add_rows(jnp.where(live, target, -1), contrib, groups * owned_blocks)
     received = lax.all_to_all(
         partial_value.reshape(groups, owned_blocks, block_size), "nets", 0, 0, tiled=False
     )
@@ -96,13 +95,10 @@
     spread = jnp.broadcast_to(edge_grad[None], (groups, owned_blocks, block_size))
     all_grads = lax.all_to_all(spread, "nets", 0, 0, tiled=False).reshape(-1, block_size)
     slot_grads = _take_rows(all_grads, target)
-    dp_tiles = (
-        jnp.sum(tile_block.astype(jnp.float32) * slot_grads.astype(jnp.float32)[:, None, :], axis=2)
-        * weight_live[:, None]
-    )
+    dp_tiles = jnp.einsum("tqe,te->tq", tile_block, slot_grads, preferred_element_type=jnp.float32)
     idx_rows = -(-tile_count // block_size)
-    idx_f = jnp.zeros((idx_rows * block_size,), jnp.float32).at[:tile_count].set(
-        split_idx.astype(jnp.float32)
+    idx_f = jnp.full((1, idx_rows * block_size), -1.0, jnp.float32).at[:, :tile_count].set(
+        jnp.where(live, split_idx, -1).astype(jnp.float32)
     )
     packed = jnp.concatenate([dp_tiles, idx_f.reshape(idx_rows, block_size)], axis=0)
     gathered = lax.all_gather(packed, "region", axis=0, tiled=False)
@@ -110,7 +106,7 @@
     all_idx = (
         gathered[:, tile_count:].reshape(gathered.shape[0], -1)[:, :tile_count]
         .astype(jnp.int32)
-        .reshape(-1)
+        .reshape(1, -1)
     )
     summed = _add_rows(all_idx, all_dp, probs_half.shape[0]).reshape(halves, segments, block_size)
     summed_grad = jnp.concatenate([summed[h] for h in range(halves)], axis=1)

time: 71.3 us -> 67.5 us (0.947)
  other arithmetic: 23.4 us -> 4.2 us
  matrix products: 6.45 us -> 22.1 us
    reduce_sum x2 -> x1, other arithmetic: 18.4 us -> 0.08 us  [shards(): jnp.sum(jnp.where(owner_idx == jnp.arange(groups, dtype=jnp.int32)[:, Non...]
    dot_general x4 -> x6, matrix products: 6.45 us -> 22.1 us  [the longest x1 9.46 us: shards(): jnp.einsum('tqe,te->tq', tile_block, slot_grads, preferred_element_type=j...]
where the time goes in v9:
time: 67.5 us; the launch traced here: 67.1 us
  matrix products  22.1 us (33%)
  waiting for transfers between devices  16.2 us (24%)
  starting transfers between devices  10.8 us (16%)
  blocking collectives  8.72 us (13%)
  other arithmetic  4.2 us (6%)
  Pallas kernels  2.42 us (4%)
  local copies, waits for them, and re-layouts  1.8 us (3%)
  between operations  0.78 us (1%)
    dot_general x1, matrix products, shards(): jnp.einsum('tqe,te->tq', tile_block, slot_grads, preferred_element_type=j...  9.46 us
    all_to_all x1, waiting for transfers between devices, shards(): lax.all_to_all(partial_value.reshape(groups, owned_blocks, block_size), '...  8.88 us
    all_gather x1, blocking collectives, shards(): gathered = lax.all_gather(packed, 'region', axis=0, tiled=False)  8.72 us
    all_to_all x1, waiting for transfers between devices, shards(): lax.all_to_all(spread, 'nets', 0, 0, tiled=False).reshape(-1, block_size)  7.3 us
    all_to_all x1, starting transfers between devices, shards(): lax.all_to_all(partial_value.reshape(groups, owned_blocks, block_size), '...  7.25 us
    dot_general x1, matrix products, shards(): jnp.einsum('tq,tqe->te', picked, tile_block, preferred_element_type=jnp.f...  6.36 us
    dot_general x2, matrix products, _add_rows(): out = jnp.dot(sel, parts, preferred_element_type=jnp.float32)  3.79 us
    all_to_all x1, starting transfers between devices, shards(): lax.all_to_all(spread, 'nets', 0, 0, tiled=False).reshape(-1, block_size)  3.59 us
  transfers between devices with their start and end apart: 2, of which 2 were waited for; matrix products, arithmetic and copies ran while one was open for 0% of the time, Pallas kernels for 0%

profile of v9, /device:TPU:0, one launch (start us, length us, event | category | flops | bytes accessed | tf_op | source)
XLA Modules:
  0.0 67.1 jit_solution(2072016691989268764)
XLA Ops:
  0.6 0.7 %reduce.3 = s32[384]{0:T(512)S(1)} reduce(s32[1,1,384]{2,1,0:T(1,128)} %param.13, s32[]{:T(128)} %constant.81.clone.1), dimensions={0,1}, to_apply=%param.13.reduce_sub_computation | reduce | bytes 3076 | tf_op args[3]
  1.3 0.7 %reduce.4 = s32[384]{0:T(512)S(1)} reduce(s32[1,1,384]{2,1,0:T(1,128)} %param.12, s32[]{:T(128)} %constant.81.clone.1), dimensions={0,1}, to_apply=%param.12.reduce_sub_computation | reduce | bytes 3076 | tf_op args[2]
  2.1 2.4 %shard_map.82 = (f32[1024,256]{1,0:T(8,128)}, bf16[2,1024,128]{2,1,0:T(8,128)(2,1)}) custom-call(f32[1024,256]{1,0:T(8,128)} %x_ref.1), custom_call_target="tpu_custom_call" | custom-call | flops 1310720 | bytes 2621440 | tf_op jit(solution)/shard_map/pallas_call | solution.py:45
  4.5 2.1 %fusion.14 = bf16[384,128,1]{1,0,2:T(8,128)(2,1)S(1)} fusion(bf16[2048,128]{1,0:T(8,128)(2,1)} %bitcast.38, s32[384]{0:T(512)S(1)} %fusion.33), kind=kOutput, calls=%fused_computation.21 | convolution fusion | flops 202162176 | bytes 624128 | tf_op jit(solution)/shard_map/dot_general | solution.py:14
  6.6 6.4 %fusion.2 = f32[384,1,128]{2,1,0:T(1,128)S(1)} fusion(bf16[1,1,384,128,128]{4,3,2,1,0:T(8,128)(2,1)} %param.11, bf16[384,128,1]{1,0,2:T(8,128)(2,1)S(1)} %fusion.14), kind=kOutput, calls=%fused_computation.2 | convolution fusion | flops 12582912 | bytes 12877824 | tf_op jit(solution)/shard_map/tq,tqe->te/dot_general | solution.py:85
  12.9 0.1 reduce-precision_convert_fusion.3
  13.0 0.1 select_reduce_fusion
  13.1 0.4 fusion.17
  13.5 0.7 %slice_add_fusion.2 = f32[512,128]{1,0:T(8,128)} fusion(f32[512,384]{1,0:T(8,128)S(1)} %fusion.17), kind=kLoop, calls=%fused_computation.43 | loop fusion | flops 131072 | bytes 1048576 | tf_op jit(solution)/shard_map/add | solution.py:27
  14.2 7.3 %all-to-all-start = ((f32[8,64,128]{2,1,0:T(8,128)}), f32[8,64,128]{2,1,0:T(8,128)S(1)}, u32[]{:S(2)}, u32[]{:S(2)}) async-start(f32[8,64,128]{2,1,0:T(8,128)} %bitcast.6), calls=%async_computation | async-start | bytes 524288 | tf_op jit(solution)/shard_map/all_to_all | solution.py:90
  21.5 8.9 %all-to-all-done = f32[8,64,128]{2,1,0:T(8,128)S(1)} async-done(((f32[8,64,128]{2,1,0:T(8,128)}), f32[8,64,128]{2,1,0:T(8,128)S(1)}, u32[]{:S(2)}, u32[]{:S(2)}) %all-to-all-start) | async-done | bytes 262176 | tf_op jit(solution)/shard_map/all_to_all | solution.py:90
  30.5 0.7 broadcast_in_dim.22
  31.1 3.6 %all-to-all-start.1 = ((bf16[8,64,128]{2,1,0:T(8,128)(2,1)}), bf16[8,64,128]{2,1,0:T(8,128)(2,1)S(1)}, u32[]{:S(2)}, u32[]{:S(2)}) async-start(bf16[8,64,128]{2,1,0:T(8,128)(2,1)} %broadcast_in_dim.22), calls=%async_computation.1 | async-start | bytes 262144 | tf_op jit(solution)/shard_map/all_to_all | solution.py:96
  34.8 7.3 %all-to-all-done.1 = bf16[8,64,128]{2,1,0:T(8,128)(2,1)S(1)} async-done(((bf16[8,64,128]{2,1,0:T(8,128)(2,1)}), bf16[8,64,128]{2,1,0:T(8,128)(2,1)S(1)}, u32[]{:S(2)}, u32[]{:S(2)}) %all-to-all-start.1) | async-done | bytes 131104 | tf_op jit(solution)/shard_map/all_to_all | solution.py:96
  42.1 0.4 fusion.15
  42.5 9.5 %fusion = f32[384,1,128]{2,1,0:T(1,128)S(1)} fusion(bf16[1,1,384,128,128]{4,3,2,1,0:T(8,128)(2,1)} %param.11, bf16[384,128,1]{1,0,2:T(8,128)(2,1)S(1)} %fusion.15), kind=kOutput, calls=%fused_computation | convolution fusion | flops 12582912 | bytes 12877824 | tf_op jit(solution)/shard_map/tqe,te->tq/dot_general | solution.py:98
  52.0 8.7 %all-gather.1 = f32[4,387,128]{2,1,0:T(8,128)S(1)} all-gather(f32[1,387,128]{2,1,0:T(8,128)S(1)} %maximum_bitcast_fusion), channel_id=2, replica_groups=mesh['nets'=8,'region'=4] {'region'}, dimensions={0}, use_global_device_ids=true | all-gather | bytes 990720 | tf_op jit(solution)/shard_map/all_gather | solution.py:104
  60.8 0.2 reduce-precision_convert_fusion.1
  61.0 3.4 %fusion.4 = f32[2048,384]{1,0:T(8,128)S(1)} fusion(s32[1536]{0:T(1024)S(1)} %convert_element_type.52, bf16[1536,128]{1,0:T(8,128)(2,1)S(1)} %get-tuple-element.29, bf16[1536,128]{1,0:T(8,128)(2,1)S(1)} %get-tuple-element.30, bf16[1536,128]{1,0:T(8,128)(2,1)S(1)} %get-tuple-element.28), kind=kOutput, calls=%fused_computation.5 | convolution fusion | flops 2422603776 | bytes 4331520 | tf_op jit(solution)/shard_map/dot_general | solution.py:25
  64.5 0.1 slice_add_fusion
  64.6 0.1 fusion.45
  64.7 1.0 %copy-done = f32[1024,256]{1,0:T(8,128)S(1)} copy-done((f32[1024,256]{1,0:T(8,128)S(1)}, f32[1024,256]{1,0:T(8,128)}, u32[]{:S(2)}) %copy-start) | copy-done | bytes 1048600
  65.7 0.2 multiply_reduce_fusion
  65.9 1.2 %subtract_multiply_fusion = f32[1024,256]{1,0:T(8,128)} fusion(f32[1024,256]{1,0:T(8,128)S(1)} %copy-done, f32[1024,128]{1,0:T(8,128)S(1)} %get-tuple-element.27, f32[1024,128]{1,0:T(8,128)S(1)} %get-tuple-element.26, f32[1024]{0:T(1024)S(1)} %multiply_reduce_fusion), kind=kLoop, calls=%fused_computation.26 | loop fusion | flops 786432 | bytes 3149824 | tf_op jit(solution)/shard_map/mul | solution.py:113
  (20 shorter events, 0.3 us)
Async XLA Ops:
  6.6 6.4 %copy-start.4 = (s32[1,1,8]{2,1,0:T(1,128)S(1)}, s32[1,1,8]{2,1,0:T(1,128)}, u32[]{:S(2)}) copy-start(s32[1,1,8]{2,1,0:T(1,128)} %param.14) | copy-start | bytes 100
  12.9 8.6 %copy-start.2 = (s32[1,8192]{1,0:T(1,128)S(1)}, s32[1,8192]{1,0:T(1,128)}, u32[]{:S(2)}) copy-start(s32[1,8192]{1,0:T(1,128)} %param.15) | copy-start | bytes 98308
  12.9 21.8 %copy-start.3 = (s32[1,1,384]{2,1,0:T(1,128)S(1)}, s32[1,1,384]{2,1,0:T(1,128)}, u32[]{:S(2)}) copy-start(s32[1,1,384]{2,1,0:T(1,128)} %param.12) | copy-start | bytes 4612
  14.2 16.2 %all-to-all-start = ((f32[8,64,128]{2,1,0:T(8,128)}), f32[8,64,128]{2,1,0:T(8,128)S(1)}, u32[]{:S(2)}, u32[]{:S(2)}) async-start(f32[8,64,128]{2,1,0:T(8,128)} %bitcast.6), calls=%async_computation | async-start | bytes 524288 | tf_op jit(solution)/shard_map/all_to_all | solution.py:90
  30.4 21.5 %copy-start.1 = (f32[64,128]{1,0:T(8,128)}, f32[64,128]{1,0:T(8,128)S(1)}, u32[]{:S(2)}) copy-start(f32[64,128]{1,0:T(8,128)S(1)} %reduce_sum.30) | copy-start | bytes 98308
  31.1 10.9 %all-to-all-start.1 = ((bf16[8,64,128]{2,1,0:T(8,128)(2,1)}), bf16[8,64,128]{2,1,0:T(8,128)(2,1)S(1)}, u32[]{:S(2)}, u32[]{:S(2)}) async-start(bf16[8,64,128]{2,1,0:T(8,128)(2,1)} %broadcast_in_dim.22), calls=%async_computation.1 | async-start | bytes 262144 | tf_op jit(solution)/shard_map/all_to_all | solution.py:96
  64.4 1.2 %copy-start = (f32[1024,256]{1,0:T(8,128)S(1)}, f32[1024,256]{1,0:T(8,128)}, u32[]{:S(2)}) copy-start(f32[1024,256]{1,0:T(8,128)} %get-tuple-element.24) | copy-start | bytes 3145732

commit v10 on v9

--- a/solution.py
+++ b/solution.py
@@ -27,37 +27,42 @@
     return out[:, :width] + out[:, width : 2 * width] + out[:, 2 * width :]
 
 
-def _softmax_kernel(x_ref, p_ref, h_ref):
+def _softmax_kernel(x_ref, idx_ref, p_ref, pick_ref):
     x = x_ref[...]
     e = jnp.exp(x - jnp.max(x, axis=-1, keepdims=True))
     p = e * (1.0 / jnp.sum(e, axis=-1, keepdims=True))
     p_ref[...] = p
     half = p.astype(jnp.bfloat16)
-    width = h_ref.shape[-1]
-    for h in range(h_ref.shape[0]):
-        h_ref[h] = half[:, h * width : (h + 1) * width]
+    rows, width = half.shape
+    block_size = pick_ref.shape[-1]
+    halves = width // block_size
+    idx = idx_ref[...]
+    seg = lax.broadcasted_iota(jnp.int32, (1, rows), 1) * halves
+    picked = None
+    for h in range(halves):
+        sel = (idx == seg + h).astype(jnp.bfloat16)
+        part = jnp.dot(
+            sel, half[:, h * block_size : (h + 1) * block_size], preferred_element_type=jnp.float32
+        )
+        picked = part if picked is None else picked + part
+    pick_ref[...] = picked.astype(jnp.bfloat16)
 
 
-def _softmax(logits, block_size):
+def _softmax(logits, idx_col, block_size):
     rows, width = logits.shape
-    halves = width // block_size
-    step = min(rows, 512)
+    tiles = idx_col.shape[0]
     return pl.pallas_call(
         _softmax_kernel,
-        grid=(rows // step,),
-        in_specs=[pl.BlockSpec((step, width), lambda i: (i, 0))],
-        out_specs=[
-            pl.BlockSpec((step, width), lambda i: (i, 0)),
-            pl.BlockSpec((halves, step, block_size), lambda i: (0, i, 0)),
-        ],
         out_shape=[
             jax.ShapeDtypeStruct((rows, width), jnp.float32),
-            jax.ShapeDtypeStruct((halves, rows, block_size), jnp.bfloat16),
+            jax.ShapeDtypeStruct((tiles, block_size), jnp.bfloat16),
         ],
         cost_estimate=pl.CostEstimate(
-            flops=5 * rows * width, transcendentals=rows * width, bytes_accessed=10 * rows * width
+            flops=5 * rows * width + 2 * tiles * rows * width,
+            transcendentals=rows * width,
+            bytes_accessed=8 * rows * width + 4 * tiles + 2 * tiles * block_size,
         ),
-    )(logits)
+    )(logits, idx_col)
 
 
 def shards(logits, tile_values, tile_pattern, tile_edge, tile_counts, capacity):
@@ -77,11 +82,9 @@
         keepdims=True,
     )
     live = slot % slot_count < slot_limit
-    probs, probs_split = _softmax(logits, block_size)
-    segments, halves = probs_split.shape[1], probs_split.shape[0]
-    probs_half = probs_split.reshape(-1, block_size)
+    probs, picked = _softmax(logits, tile_pattern.reshape(tile_count, 1), block_size)
+    segments, halves = logits.shape[0], logits.shape[1] // block_size
     split_idx = (pattern_idx % halves) * segments + pattern_idx // halves
-    picked = _take_rows(probs_half, split_idx)
     contrib = jnp.einsum("tq,tqe->te", picked, tile_block, preferred_element_type=jnp.float32)
     capacity_f = capacity.reshape(-1, block_size).astype(jnp.float32)
     owned_blocks = capacity_f.shape[0]
@@ -108,7 +111,7 @@
         .astype(jnp.int32)
         .reshape(1, -1)
     )
-    summed = _add_rows(all_idx, all_dp, probs_half.shape[0]).reshape(halves, segments, block_size)
+    summed = _add_rows(all_idx, all_dp, halves * segments).reshape(halves, segments, block_size)
     summed_grad = jnp.concatenate([summed[h] for h in range(halves)], axis=1)
     logit_grad = probs * (summed_grad - jnp.sum(probs * summed_grad, axis=-1, keepdims=True))
     return (logit_grad, usage_edges.reshape(capacity.shape))

time: 67.5 us -> 67.7 us (level)
  local copies, waits for them, and re-layouts: 1.8 us -> 3.31 us
  other arithmetic: 4.2 us -> 2.81 us
    dot_general x2 -> x1, matrix products: 2.51 us -> 0.43 us  [_take_rows(): lax.dot_general(sel, table, (((0,), (0,)), ((), ())), preferred_element_t...]
    dot_general x1, matrix products: 6.36 us -> 8.01 us  [shards(): jnp.einsum('tq,tqe->te', picked, tile_block, preferred_element_type=jnp.f...]
    reshape x0 -> x1, local copies, waits for them, and re-layouts: none -> 1.5 us  [shards(): tile_pattern.reshape(tile_count, 1)]
    unnamed x3 -> x2, other arithmetic: 1.44 us -> 0.06 us
where the time goes in v10:
time: 67.7 us; the launch traced here: 67.3 us
  matrix products  21.7 us (32%)
  waiting for transfers between devices  16.2 us (24%)
  starting transfers between devices  10.8 us (16%)
  blocking collectives  8.72 us (13%)
  local copies, waits for them, and re-layouts  3.31 us (5%)
  Pallas kernels  3 us (4%)
  other arithmetic  2.81 us (4%)
  between operations  0.78 us (1%)
    dot_general x1, matrix products, shards(): jnp.einsum('tqe,te->tq', tile_block, slot_grads, preferred_element_type=j...  9.46 us
    all_to_all x1, waiting for transfers between devices, shards(): lax.all_to_all(partial_value.reshape(groups, owned_blocks, block_size), '...  8.88 us
    all_gather x1, blocking collectives, shards(): gathered = lax.all_gather(packed, 'region', axis=0, tiled=False)  8.72 us
    dot_general x1, matrix products, shards(): jnp.einsum('tq,tqe->te', picked, tile_block, preferred_element_type=jnp.f...  8.01 us
    all_to_all x1, waiting for transfers between devices, shards(): lax.all_to_all(spread, 'nets', 0, 0, tiled=False).reshape(-1, block_size)  7.3 us
    all_to_all x1, starting transfers between devices, shards(): lax.all_to_all(partial_value.reshape(groups, owned_blocks, block_size), '...  7.25 us
    dot_general x2, matrix products, _add_rows(): out = jnp.dot(sel, parts, preferred_element_type=jnp.float32)  3.79 us
    all_to_all x1, starting transfers between devices, shards(): lax.all_to_all(spread, 'nets', 0, 0, tiled=False).reshape(-1, block_size)  3.59 us
  transfers between devices with their start and end apart: 2, of which 2 were waited for; matrix products, arithmetic and copies ran while one was open for 0% of the time, Pallas kernels for 0%

profile of v10, /device:TPU:0, one launch (start us, length us, event | category | flops | bytes accessed | tf_op | source)
XLA Modules:
  0.0 67.3 jit_solution(7062703578727467621)
XLA Ops:
  0.6 1.5 %copy.19.idx_ref = s32[384,1]{1,0:T(8,128)} copy(s32[384,1]{0,1:T(1,128)} %bitcast.36) | data formatting | bytes 3072 | tf_op jit(solution)/shard_map/reshape | solution.py:85
  2.1 3.0 %shard_map.82 = (f32[1024,256]{1,0:T(8,128)}, bf16[384,128]{1,0:T(8,128)(2,1)}) custom-call(f32[1024,256]{1,0:T(8,128)} %x_ref.1, s32[384,1]{1,0:T(8,128)} %copy.19.idx_ref), custom_call_target="tpu_custom_call" | custom-call | flops 202637312 | bytes 2196992 | tf_op jit(solution)/shard_map/pallas_call | solution.py:54
  5.1 8.0 %fusion.2 = f32[384,1,128]{2,1,0:T(1,128)S(1)} fusion(bf16[1,1,384,128,128]{4,3,2,1,0:T(8,128)(2,1)} %param.11, bf16[384,128,1]{1,0,2:T(8,128)(2,1)} %bitcast.30), kind=kOutput, calls=%fused_computation.2 | convolution fusion | flops 12582912 | bytes 12877824 | tf_op jit(solution)/shard_map/tq,tqe->te/dot_general | solution.py:88
  13.2 0.1 reduce-precision_convert_fusion.3
  13.3 0.1 select_reduce_fusion
  13.4 0.4 fusion.13
  13.8 0.7 %slice_add_fusion.2 = f32[512,128]{1,0:T(8,128)} fusion(f32[512,384]{1,0:T(8,128)S(1)} %fusion.13), kind=kLoop, calls=%fused_computation.38 | loop fusion | flops 131072 | bytes 1048576 | tf_op jit(solution)/shard_map/add | solution.py:27
  14.5 7.3 %all-to-all-start = ((f32[8,64,128]{2,1,0:T(8,128)}), f32[8,64,128]{2,1,0:T(8,128)S(1)}, u32[]{:S(2)}, u32[]{:S(2)}) async-start(f32[8,64,128]{2,1,0:T(8,128)} %bitcast.6), calls=%async_computation | async-start | bytes 524288 | tf_op jit(solution)/shard_map/all_to_all | solution.py:93
  21.8 8.9 %all-to-all-done = f32[8,64,128]{2,1,0:T(8,128)S(1)} async-done(((f32[8,64,128]{2,1,0:T(8,128)}), f32[8,64,128]{2,1,0:T(8,128)S(1)}, u32[]{:S(2)}, u32[]{:S(2)}) %all-to-all-start) | async-done | bytes 262176 | tf_op jit(solution)/shard_map/all_to_all | solution.py:93
  30.7 0.0 copy-start.1
  30.7 0.7 broadcast_in_dim.34
  31.4 3.6 %all-to-all-start.1 = ((bf16[8,64,128]{2,1,0:T(8,128)(2,1)}), bf16[8,64,128]{2,1,0:T(8,128)(2,1)S(1)}, u32[]{:S(2)}, u32[]{:S(2)}) async-start(bf16[8,64,128]{2,1,0:T(8,128)(2,1)} %broadcast_in_dim.34), calls=%async_computation.1 | async-start | bytes 262144 | tf_op jit(solution)/shard_map/all_to_all | solution.py:99
  35.0 7.3 %all-to-all-done.1 = bf16[8,64,128]{2,1,0:T(8,128)(2,1)S(1)} async-done(((bf16[8,64,128]{2,1,0:T(8,128)(2,1)}), bf16[8,64,128]{2,1,0:T(8,128)(2,1)S(1)}, u32[]{:S(2)}, u32[]{:S(2)}) %all-to-all-start.1) | async-done | bytes 131104 | tf_op jit(solution)/shard_map/all_to_all | solution.py:99
  42.3 0.4 fusion.11
  42.8 9.5 %fusion = f32[384,1,128]{2,1,0:T(1,128)S(1)} fusion(bf16[1,1,384,128,128]{4,3,2,1,0:T(8,128)(2,1)} %param.11, bf16[384,128,1]{1,0,2:T(8,128)(2,1)S(1)} %fusion.11), kind=kOutput, calls=%fused_computation | convolution fusion | flops 12582912 | bytes 12877824 | tf_op jit(solution)/shard_map/tqe,te->tq/dot_general | solution.py:101
  52.3 8.7 %all-gather.1 = f32[4,387,128]{2,1,0:T(8,128)S(1)} all-gather(f32[1,387,128]{2,1,0:T(8,128)S(1)} %maximum_bitcast_fusion), channel_id=2, replica_groups=mesh['nets'=8,'region'=4] {'region'}, dimensions={0}, use_global_device_ids=true | all-gather | bytes 990720 | tf_op jit(solution)/shard_map/all_gather | solution.py:107
  61.0 0.1 slice.60
  61.1 0.2 reduce-precision_convert_fusion.1
  61.3 3.4 %fusion.4 = f32[2048,384]{1,0:T(8,128)S(1)} fusion(s32[1536]{0:T(1024)S(1)} %convert_element_type.47, bf16[1536,128]{1,0:T(8,128)(2,1)S(1)} %get-tuple-element.29, bf16[1536,128]{1,0:T(8,128)(2,1)S(1)} %get-tuple-element.30, bf16[1536,128]{1,0:T(8,128)(2,1)S(1)} %get-tuple-element.28), kind=kOutput, calls=%fused_computation.5 | convolution fusion | flops 2422603776 | bytes 4331520 | tf_op jit(solution)/shard_map/dot_general | solution.py:25
  64.7 0.1 slice_add_fusion
  64.9 0.1 fusion.37
  64.9 1.0 %copy-done = f32[1024,256]{1,0:T(8,128)S(1)} copy-done((f32[1024,256]{1,0:T(8,128)S(1)}, f32[1024,256]{1,0:T(8,128)}, u32[]{:S(2)}) %copy-start) | copy-done | bytes 1048600
  65.9 0.2 multiply_reduce_fusion
  66.1 1.2 %subtract_multiply_fusion = f32[1024,256]{1,0:T(8,128)} fusion(f32[1024,256]{1,0:T(8,128)S(1)} %copy-done, f32[1024,128]{1,0:T(8,128)S(1)} %get-tuple-element.27, f32[1024,128]{1,0:T(8,128)S(1)} %get-tuple-element.26, f32[1024]{0:T(1024)S(1)} %multiply_reduce_fusion), kind=kLoop, calls=%fused_computation.21 | loop fusion | flops 786432 | bytes 3149824 | tf_op jit(solution)/shard_map/mul | solution.py:116
  (20 shorter events, 0.2 us)
Async XLA Ops:
  5.1 8.1 %copy-start.4 = (s32[1,1,384]{2,1,0:T(1,128)S(1)}, s32[1,1,384]{2,1,0:T(1,128)}, u32[]{:S(2)}) copy-start(s32[1,1,384]{2,1,0:T(1,128)} %param.13) | copy-start | bytes 4612
  5.1 8.1 %copy-start.5 = (s32[1,1,8]{2,1,0:T(1,128)S(1)}, s32[1,1,8]{2,1,0:T(1,128)}, u32[]{:S(2)}) copy-start(s32[1,1,8]{2,1,0:T(1,128)} %param.14) | copy-start | bytes 100
  13.1 8.6 %copy-start.2 = (s32[1,8192]{1,0:T(1,128)S(1)}, s32[1,8192]{1,0:T(1,128)}, u32[]{:S(2)}) copy-start(s32[1,8192]{1,0:T(1,128)} %param.15) | copy-start | bytes 98308
  13.2 21.8 %copy-start.3 = (s32[1,1,384]{2,1,0:T(1,128)S(1)}, s32[1,1,384]{2,1,0:T(1,128)}, u32[]{:S(2)}) copy-start(s32[1,1,384]{2,1,0:T(1,128)} %param.12) | copy-start | bytes 4612
  14.5 16.2 %all-to-all-start = ((f32[8,64,128]{2,1,0:T(8,128)}), f32[8,64,128]{2,1,0:T(8,128)S(1)}, u32[]{:S(2)}, u32[]{:S(2)}) async-start(f32[8,64,128]{2,1,0:T(8,128)} %bitcast.6), calls=%async_computation | async-start | bytes 524288 | tf_op jit(solution)/shard_map/all_to_all | solution.py:93
  30.7 21.5 %copy-start.1 = (f32[64,128]{1,0:T(8,128)}, f32[64,128]{1,0:T(8,128)S(1)}, u32[]{:S(2)}) copy-start(f32[64,128]{1,0:T(8,128)S(1)} %reduce_sum.30) | copy-start | bytes 98308
  31.4 10.9 %all-to-all-start.1 = ((bf16[8,64,128]{2,1,0:T(8,128)(2,1)}), bf16[8,64,128]{2,1,0:T(8,128)(2,1)S(1)}, u32[]{:S(2)}, u32[]{:S(2)}) async-start(bf16[8,64,128]{2,1,0:T(8,128)(2,1)} %broadcast_in_dim.34), calls=%async_computation.1 | async-start | bytes 262144 | tf_op jit(solution)/shard_map/all_to_all | solution.py:99
  64.7 1.2 %copy-start = (f32[1024,256]{1,0:T(8,128)S(1)}, f32[1024,256]{1,0:T(8,128)}, u32[]{:S(2)}) copy-start(f32[1024,256]{1,0:T(8,128)} %get-tuple-element.24) | copy-start | bytes 3145732

commit v11 on v9

--- a/solution.py
+++ b/solution.py
@@ -20,11 +20,9 @@
     rest = rows - hi
     mid = lax.reduce_precision(rest, exponent_bits=8, mantissa_bits=7)
     lo = rest - mid
-    parts = jnp.concatenate([hi, mid, lo], axis=1).astype(jnp.bfloat16)
-    sel = _one_hot_t(idx_row, size, jnp.bfloat16)
-    out = jnp.dot(sel, parts, preferred_element_type=jnp.float32)
-    width = rows.shape[1]
-    return out[:, :width] + out[:, width : 2 * width] + out[:, 2 * width :]
+    parts = jnp.concatenate([hi, mid, lo], axis=0).astype(jnp.bfloat16)
+    sel = _one_hot_t(jnp.concatenate([idx_row] * 3, axis=1), size, jnp.bfloat16)
+    return jnp.dot(sel, parts, preferred_element_type=jnp.float32)
 
 
 def _softmax_kernel(x_ref, p_ref, h_ref):

time: 67.5 us -> 70.7 us (1.047)
  matrix products: 22.1 us -> 26.3 us
  local copies, waits for them, and re-layouts: 1.8 us -> 0.82 us
    dot_general x2, matrix products: 3.79 us -> 7.99 us  [_add_rows(): return jnp.dot(sel, parts, preferred_element_type=jnp.float32)]
    unnamed x10, local copies, waits for them, and re-layouts: 1.02 us -> 0.03 us
    add x2 -> x0, other arithmetic: 0.87 us -> none  [_add_rows(): return out[:, :width] + out[:, width:2 * width] + out[:, 2 * width:]]
where the time goes in v11:
time: 70.7 us; the launch traced here: 70.3 us
  matrix products  26.3 us (37%)
  waiting for transfers between devices  16.1 us (23%)
  starting transfers between devices  10.8 us (15%)
  blocking collectives  8.9 us (13%)
  other arithmetic  4.09 us (6%)
  Pallas kernels  2.42 us (3%)
  local copies, waits for them, and re-layouts  0.82 us (1%)
  between operations  0.78 us (1%)
    dot_general x1, matrix products, shards(): jnp.einsum('tqe,te->tq', tile_block, slot_grads, preferred_element_type=j...  9.46 us
    all_gather x1, blocking collectives, shards(): gathered = lax.all_gather(packed, 'region', axis=0, tiled=False)  8.9 us
    all_to_all x1, waiting for transfers between devices, shards(): lax.all_to_all(partial_value.reshape(groups, owned_blocks, block_size), '...  8.88 us
    dot_general x2, matrix products, _add_rows(): return jnp.dot(sel, parts, preferred_element_type=jnp.float32)  7.99 us
    all_to_all x1, starting transfers between devices, shards(): lax.all_to_all(partial_value.reshape(groups, owned_blocks, block_size), '...  7.26 us
    all_to_all x1, waiting for transfers between devices, shards(): lax.all_to_all(spread, 'nets', 0, 0, tiled=False).reshape(-1, block_size)  7.25 us
    dot_general x1, matrix products, shards(): jnp.einsum('tq,tqe->te', picked, tile_block, preferred_element_type=jnp.f...  6.36 us
    all_to_all x1, starting transfers between devices, shards(): lax.all_to_all(spread, 'nets', 0, 0, tiled=False).reshape(-1, block_size)  3.59 us
  transfers between devices with their start and end apart: 2, of which 2 were waited for; matrix products, arithmetic and copies ran while one was open for 0% of the time, Pallas kernels for 0%

profile of v11, /device:TPU:0, one launch (start us, length us, event | category | flops | bytes accessed | tf_op | source)
XLA Modules:
  0.0 70.3 jit_solution(5632038231198545519)
XLA Ops:
  0.6 0.7 reduce.5
  1.4 0.7 %select_reduce_fusion = s32[384]{0:T(512)S(1)} fusion(s32[8]{0:T(128)} %bitcast.39, s32[384]{0:T(512)S(1)} %add_select_fusion.2), kind=kLoop, calls=%fused_computation.47 | loop fusion | flops 8832 | bytes 3104 | tf_op jit(solution)/shard_map/reduce_sum | solution.py:72
  2.1 0.7 compare_select_fusion.1
  2.8 2.4 %shard_map.82 = (f32[1024,256]{1,0:T(8,128)}, bf16[2,1024,128]{2,1,0:T(8,128)(2,1)}) custom-call(f32[1024,256]{1,0:T(8,128)} %x_ref.1), custom_call_target="tpu_custom_call" | custom-call | flops 1310720 | bytes 2621440 | tf_op jit(solution)/shard_map/pallas_call | solution.py:43
  5.2 2.1 %fusion.16 = bf16[384,128,1]{1,0,2:T(8,128)(2,1)S(1)} fusion(bf16[2048,128]{1,0:T(8,128)(2,1)} %bitcast.40, s32[384]{0:T(512)S(1)} %fusion.29), kind=kOutput, calls=%fused_computation.24 | convolution fusion | flops 202162176 | bytes 624128 | tf_op jit(solution)/shard_map/dot_general | solution.py:14
  7.3 0.0 copy-start.2
  7.3 6.4 %fusion.4 = f32[384,1,128]{2,1,0:T(1,128)S(1)} fusion(bf16[1,1,384,128,128]{4,3,2,1,0:T(8,128)(2,1)} %param.11, bf16[384,128,1]{1,0,2:T(8,128)(2,1)S(1)} %fusion.16), kind=kOutput, calls=%fused_computation.5 | convolution fusion | flops 12582912 | bytes 12877824 | tf_op jit(solution)/shard_map/tq,tqe->te/dot_general | solution.py:83
  13.7 0.1 reduce-precision_convert_fusion.3
  13.8 1.2 %fusion.7 = f32[512,128]{1,0:T(8,128)} fusion(s32[1152]{0:T(1024)S(1)} %add_reduce_fusion.1, bf16[384,128]{1,0:T(8,128)(2,1)S(1)} %get-tuple-element.32, bf16[384,128]{1,0:T(8,128)(2,1)S(1)} %get-tuple-element.33, bf16[384,128]{1,0:T(8,128)(2,1)S(1)} %get-tuple-element.31), kind=kOutput, calls=%fused_computation.10 | convolution fusion | flops 152469504 | bytes 561664 | tf_op jit(solution)/shard_map/dot_general | solution.py:25
  15.0 7.3 %all-to-all-start = ((f32[8,64,128]{2,1,0:T(8,128)}), f32[8,64,128]{2,1,0:T(8,128)S(1)}, u32[]{:S(2)}, u32[]{:S(2)}) async-start(f32[8,64,128]{2,1,0:T(8,128)} %bitcast.7), calls=%async_computation | async-start | bytes 524288 | tf_op jit(solution)/shard_map/all_to_all | solution.py:88
  22.3 8.9 %all-to-all-done = f32[8,64,128]{2,1,0:T(8,128)S(1)} async-done(((f32[8,64,128]{2,1,0:T(8,128)}), f32[8,64,128]{2,1,0:T(8,128)S(1)}, u32[]{:S(2)}, u32[]{:S(2)}) %all-to-all-start) | async-done | bytes 262176 | tf_op jit(solution)/shard_map/all_to_all | solution.py:88
  31.2 0.0 copy-start.1
  31.2 0.7 broadcast_in_dim.22
  31.9 3.6 %all-to-all-start.1 = ((bf16[8,64,128]{2,1,0:T(8,128)(2,1)}), bf16[8,64,128]{2,1,0:T(8,128)(2,1)S(1)}, u32[]{:S(2)}, u32[]{:S(2)}) async-start(bf16[8,64,128]{2,1,0:T(8,128)(2,1)} %broadcast_in_dim.22), calls=%async_computation.1 | async-start | bytes 262144 | tf_op jit(solution)/shard_map/all_to_all | solution.py:94
  35.5 7.3 %all-to-all-done.1 = bf16[8,64,128]{2,1,0:T(8,128)(2,1)S(1)} async-done(((bf16[8,64,128]{2,1,0:T(8,128)(2,1)}), bf16[8,64,128]{2,1,0:T(8,128)(2,1)S(1)}, u32[]{:S(2)}, u32[]{:S(2)}) %all-to-all-start.1) | async-done | bytes 131104 | tf_op jit(solution)/shard_map/all_to_all | solution.py:94
  42.8 0.4 fusion.17
  43.2 9.5 %fusion.2 = f32[384,1,128]{2,1,0:T(1,128)S(1)} fusion(bf16[1,1,384,128,128]{4,3,2,1,0:T(8,128)(2,1)} %param.11, bf16[384,128,1]{1,0,2:T(8,128)(2,1)S(1)} %fusion.17), kind=kOutput, calls=%fused_computation.3 | convolution fusion | flops 12582912 | bytes 12877824 | tf_op jit(solution)/shard_map/tqe,te->tq/dot_general | solution.py:96
  52.7 8.9 %all-gather.1 = f32[4,387,128]{2,1,0:T(8,128)S(1)} all-gather(f32[1,387,128]{2,1,0:T(8,128)S(1)} %maximum_bitcast_fusion), channel_id=2, replica_groups=mesh['nets'=8,'region'=4] {'region'}, dimensions={0}, use_global_device_ids=true | all-gather | bytes 990720 | tf_op jit(solution)/shard_map/all_gather | solution.py:102
  61.6 0.1 slice.33
  61.7 0.2 reduce-precision_convert_fusion.1
  62.0 6.8 %fusion = f32[2048,128]{1,0:T(8,128)S(1)} fusion(s32[4608]{0:T(1024)S(1)} %add_reduce_fusion, bf16[1536,128]{1,0:T(8,128)(2,1)S(1)} %get-tuple-element.29, bf16[1536,128]{1,0:T(8,128)(2,1)S(1)} %get-tuple-element.30, bf16[1536,128]{1,0:T(8,128)(2,1)S(1)} %get-tuple-element.28), kind=kOutput, calls=%fused_computation.1 | convolution fusion | flops 2428895232 | bytes 2246656 | tf_op jit(solution)/shard_map/dot_general | solution.py:25
  68.8 0.1 fusion.41
  68.9 0.3 multiply_reduce_fusion
  69.1 1.2 %subtract_multiply_fusion = f32[1024,256]{1,0:T(8,128)} fusion(f32[1024,256]{1,0:T(8,128)S(1)} %copy-done, f32[1024,128]{1,0:T(8,128)S(1)} %get-tuple-element.27, f32[1024,128]{1,0:T(8,128)S(1)} %get-tuple-element.26, f32[1024]{0:T(1024)S(1)} %multiply_reduce_fusion), kind=kLoop, calls=%fused_computation.27 | loop fusion | flops 786432 | bytes 3149824 | tf_op jit(solution)/shard_map/mul | solution.py:111
  (21 shorter events, 0.3 us)
Async XLA Ops:
  7.3 14.9 %copy-start.2 = (s32[1,8192]{1,0:T(1,128)S(1)}, s32[1,8192]{1,0:T(1,128)}, u32[]{:S(2)}) copy-start(s32[1,8192]{1,0:T(1,128)} %param.15) | copy-start | bytes 98308
  13.7 21.8 %copy-start.3 = (s32[1,1,384]{2,1,0:T(1,128)S(1)}, s32[1,1,384]{2,1,0:T(1,128)}, u32[]{:S(2)}) copy-start(s32[1,1,384]{2,1,0:T(1,128)} %param.12) | copy-start | bytes 4612
  13.7 21.8 %copy-start.4 = (s32[1,1,384]{2,1,0:T(1,128)S(1)}, s32[1,1,384]{2,1,0:T(1,128)}, u32[]{:S(2)}) copy-start(s32[1,1,384]{2,1,0:T(1,128)} %param.13) | copy-start | bytes 4612
  15.0 16.2 %all-to-all-start = ((f32[8,64,128]{2,1,0:T(8,128)}), f32[8,64,128]{2,1,0:T(8,128)S(1)}, u32[]{:S(2)}, u32[]{:S(2)}) async-start(f32[8,64,128]{2,1,0:T(8,128)} %bitcast.7), calls=%async_computation | async-start | bytes 524288 | tf_op jit(solution)/shard_map/all_to_all | solution.py:88
  31.2 21.5 %copy-start.1 = (f32[64,128]{1,0:T(8,128)}, f32[64,128]{1,0:T(8,128)S(1)}, u32[]{:S(2)}) copy-start(f32[64,128]{1,0:T(8,128)S(1)} %reduce_sum.33) | copy-start | bytes 98308
  31.9 10.9 %all-to-all-start.1 = ((bf16[8,64,128]{2,1,0:T(8,128)(2,1)}), bf16[8,64,128]{2,1,0:T(8,128)(2,1)S(1)}, u32[]{:S(2)}, u32[]{:S(2)}) async-start(bf16[8,64,128]{2,1,0:T(8,128)(2,1)} %broadcast_in_dim.22), calls=%async_computation.1 | async-start | bytes 262144 | tf_op jit(solution)/shard_map/all_to_all | solution.py:94
  62.0 6.9 %copy-start = (f32[1024,256]{1,0:T(8,128)S(1)}, f32[1024,256]{1,0:T(8,128)}, u32[]{:S(2)}) copy-start(f32[1024,256]{1,0:T(8,128)} %get-tuple-element.24) | copy-start | bytes 3145732

commit v12 on v9

--- a/solution.py
+++ b/solution.py
@@ -60,6 +60,35 @@
     )(logits)
 
 
+def _vjp_kernel(p_ref, g_ref, o_ref):
+    p = p_ref[...]
+    block_size = g_ref.shape[-1]
+    halves = g_ref.shape[0]
+    cols = [slice(h * block_size, (h + 1) * block_size) for h in range(halves)]
+    dot = sum(jnp.sum(p[:, c] * g_ref[h], axis=-1, keepdims=True) for h, c in enumerate(cols))
+    for h, c in enumerate(cols):
+        o_ref[:, c] = p[:, c] * (g_ref[h] - dot)
+
+
+def _softmax_vjp(probs, grads):
+    rows, width = probs.shape
+    halves, _, block_size = grads.shape
+    step = min(rows, 256)
+    return pl.pallas_call(
+        _vjp_kernel,
+        grid=(rows // step,),
+        in_specs=[
+            pl.BlockSpec((step, width), lambda i: (i, 0)),
+            pl.BlockSpec((halves, step, block_size), lambda i: (0, i, 0)),
+        ],
+        out_specs=pl.BlockSpec((step, width), lambda i: (i, 0)),
+        out_shape=jax.ShapeDtypeStruct((rows, width), jnp.float32),
+        cost_estimate=pl.CostEstimate(
+            flops=4 * rows * width, transcendentals=0, bytes_accessed=12 * rows * width
+        ),
+    )(probs, grads)
+
+
 def shards(logits, tile_values, tile_pattern, tile_edge, tile_counts, capacity):
     groups = lax.axis_size("nets")
     tile_block = tile_values[0, 0]
@@ -109,8 +138,7 @@
         .reshape(1, -1)
     )
     summed = _add_rows(all_idx, all_dp, probs_half.shape[0]).reshape(halves, segments, block_size)
-    summed_grad = jnp.concatenate([summed[h] for h in range(halves)], axis=1)
-    logit_grad = probs * (summed_grad - jnp.sum(probs * summed_grad, axis=-1, keepdims=True))
+    logit_grad = _softmax_vjp(probs, summed)
     return (logit_grad, usage_edges.reshape(capacity.shape))
 
 

time: 67.5 us -> 69.9 us (1.036)
  Pallas kernels: 2.42 us -> 6.21 us
  local copies, waits for them, and re-layouts: 1.8 us -> 0.75 us
    pallas_call x0 -> x1, Pallas kernels: none -> 3.79 us  [_softmax_vjp(): pl.pallas_call(_vjp_kernel, grid=(rows // step,), in_specs=[pl.BlockSpec(...]
    mul x1 -> x0, other arithmetic: 1.18 us -> none  [shards(): probs * (summed_grad - jnp.sum(probs * summed_grad, axis=-1, keepdims=True))]
    add x2, other arithmetic: 0.87 us -> 1.91 us  [_add_rows(): return out[:, :width] + out[:, width:2 * width] + out[:, 2 * width:]]
    unnamed x10 -> x8, local copies, waits for them, and re-layouts: 1.02 us -> 0.02 us
where the time goes in v12:
time: 69.9 us; the launch traced here: 69.4 us
  matrix products  22.1 us (32%)
  waiting for transfers between devices  16.2 us (23%)
  starting transfers between devices  10.8 us (15%)
  blocking collectives  8.72 us (12%)
  Pallas kernels  6.21 us (9%)
  other arithmetic  3.86 us (6%)
  local copies, waits for them, and re-layouts  0.75 us (1%)
  between operations  0.75 us (1%)
    dot_general x1, matrix products, shards(): jnp.einsum('tqe,te->tq', tile_block, slot_grads, preferred_element_type=j...  9.46 us
    all_to_all x1, waiting for transfers between devices, shards(): lax.all_to_all(partial_value.reshape(groups, owned_blocks, block_size), '...  8.88 us
    all_gather x1, blocking collectives, shards(): gathered = lax.all_gather(packed, 'region', axis=0, tiled=False)  8.72 us
    all_to_all x1, waiting for transfers between devices, shards(): lax.all_to_all(spread, 'nets', 0, 0, tiled=False).reshape(-1, block_size)  7.3 us
    all_to_all x1, starting transfers between devices, shards(): lax.all_to_all(partial_value.reshape(groups, owned_blocks, block_size), '...  7.25 us
    dot_general x1, matrix products, shards(): jnp.einsum('tq,tqe->te', picked, tile_block, preferred_element_type=jnp.f...  6.36 us
    dot_general x2, matrix products, _add_rows(): out = jnp.dot(sel, parts, preferred_element_type=jnp.float32)  3.79 us
    pallas_call x1, Pallas kernels, _softmax_vjp(): pl.pallas_call(_vjp_kernel, grid=(rows // step,), in_specs=[pl.BlockSpec(...  3.79 us
  transfers between devices with their start and end apart: 2, of which 2 were waited for; matrix products, arithmetic and copies ran while one was open for 0% of the time, Pallas kernels for 0%

profile of v12, /device:TPU:0, one launch (start us, length us, event | category | flops | bytes accessed | tf_op | source)
XLA Modules:
  0.0 69.4 jit_solution(13824040399578170161)
XLA Ops:
  0.6 0.7 %reduce.3 = s32[384]{0:T(512)S(1)} reduce(s32[1,1,384]{2,1,0:T(1,128)} %param.13, s32[]{:T(128)} %constant.81.clone.1), dimensions={0,1}, to_apply=%param.13.reduce_sub_computation | reduce | bytes 3076 | tf_op args[3]
  1.3 0.7 %reduce.4 = s32[384]{0:T(512)S(1)} reduce(s32[1,1,384]{2,1,0:T(1,128)} %param.12, s32[]{:T(128)} %constant.81.clone.1), dimensions={0,1}, to_apply=%param.12.reduce_sub_computation | reduce | bytes 3076 | tf_op args[2]
  2.1 2.4 %shard_map.82 = (f32[1024,256]{1,0:T(8,128)}, bf16[2,1024,128]{2,1,0:T(8,128)(2,1)}) custom-call(f32[1024,256]{1,0:T(8,128)} %x_ref.1), custom_call_target="tpu_custom_call" | custom-call | flops 1310720 | bytes 2621440 | tf_op jit(solution)/shard_map/pallas_call | solution.py:45
  4.5 2.1 %fusion.14 = bf16[384,128,1]{1,0,2:T(8,128)(2,1)S(1)} fusion(bf16[2048,128]{1,0:T(8,128)(2,1)} %bitcast.40, s32[384]{0:T(512)S(1)} %fusion.33), kind=kOutput, calls=%fused_computation.21 | convolution fusion | flops 202162176 | bytes 624128 | tf_op jit(solution)/shard_map/dot_general | solution.py:14
  6.6 0.0 copy-start.3
  6.6 6.4 %fusion.2 = f32[384,1,128]{2,1,0:T(1,128)S(1)} fusion(bf16[1,1,384,128,128]{4,3,2,1,0:T(8,128)(2,1)} %param.11, bf16[384,128,1]{1,0,2:T(8,128)(2,1)S(1)} %fusion.14), kind=kOutput, calls=%fused_computation.2 | convolution fusion | flops 12582912 | bytes 12877824 | tf_op jit(solution)/shard_map/tq,tqe->te/dot_general | solution.py:114
  12.9 0.1 reduce-precision_convert_fusion.3
  13.0 0.1 select_reduce_fusion
  13.1 0.4 fusion.17
  13.5 0.7 %slice_add_fusion.2 = f32[512,128]{1,0:T(8,128)} fusion(f32[512,384]{1,0:T(8,128)S(1)} %fusion.17), kind=kLoop, calls=%fused_computation.40 | loop fusion | flops 131072 | bytes 1048576 | tf_op jit(solution)/shard_map/add | solution.py:27
  14.3 7.3 %all-to-all-start = ((f32[8,64,128]{2,1,0:T(8,128)}), f32[8,64,128]{2,1,0:T(8,128)S(1)}, u32[]{:S(2)}, u32[]{:S(2)}) async-start(f32[8,64,128]{2,1,0:T(8,128)} %bitcast.6), calls=%async_computation | async-start | bytes 524288 | tf_op jit(solution)/shard_map/all_to_all | solution.py:119
  21.5 8.9 %all-to-all-done = f32[8,64,128]{2,1,0:T(8,128)S(1)} async-done(((f32[8,64,128]{2,1,0:T(8,128)}), f32[8,64,128]{2,1,0:T(8,128)S(1)}, u32[]{:S(2)}, u32[]{:S(2)}) %all-to-all-start) | async-done | bytes 262176 | tf_op jit(solution)/shard_map/all_to_all | solution.py:119
  30.4 0.0 copy-start
  30.5 0.7 broadcast_in_dim.34
  31.2 3.6 %all-to-all-start.1 = ((bf16[8,64,128]{2,1,0:T(8,128)(2,1)}), bf16[8,64,128]{2,1,0:T(8,128)(2,1)S(1)}, u32[]{:S(2)}, u32[]{:S(2)}) async-start(bf16[8,64,128]{2,1,0:T(8,128)(2,1)} %broadcast_in_dim.34), calls=%async_computation.1 | async-start | bytes 262144 | tf_op jit(solution)/shard_map/all_to_all | solution.py:125
  34.8 7.3 %all-to-all-done.1 = bf16[8,64,128]{2,1,0:T(8,128)(2,1)S(1)} async-done(((bf16[8,64,128]{2,1,0:T(8,128)(2,1)}), bf16[8,64,128]{2,1,0:T(8,128)(2,1)S(1)}, u32[]{:S(2)}, u32[]{:S(2)}) %all-to-all-start.1) | async-done | bytes 131104 | tf_op jit(solution)/shard_map/all_to_all | solution.py:125
  42.1 0.4 fusion.15
  42.5 9.5 %fusion = f32[384,1,128]{2,1,0:T(1,128)S(1)} fusion(bf16[1,1,384,128,128]{4,3,2,1,0:T(8,128)(2,1)} %param.11, bf16[384,128,1]{1,0,2:T(8,128)(2,1)S(1)} %fusion.15), kind=kOutput, calls=%fused_computation | convolution fusion | flops 12582912 | bytes 12877824 | tf_op jit(solution)/shard_map/tqe,te->tq/dot_general | solution.py:127
  52.0 8.7 %all-gather.1 = f32[4,387,128]{2,1,0:T(8,128)S(1)} all-gather(f32[1,387,128]{2,1,0:T(8,128)S(1)} %maximum_bitcast_fusion), channel_id=2, replica_groups=mesh['nets'=8,'region'=4] {'region'}, dimensions={0}, use_global_device_ids=true | all-gather | bytes 990720 | tf_op jit(solution)/shard_map/all_gather | solution.py:133
  60.8 0.1 slice.50
  60.8 0.2 reduce-precision_convert_fusion.1
  61.0 3.4 %fusion.4 = f32[2048,384]{1,0:T(8,128)S(1)} fusion(s32[1536]{0:T(1024)S(1)} %convert_element_type.52, bf16[1536,128]{1,0:T(8,128)(2,1)S(1)} %get-tuple-element.27, bf16[1536,128]{1,0:T(8,128)(2,1)S(1)} %get-tuple-element.28, bf16[1536,128]{1,0:T(8,128)(2,1)S(1)} %get-tuple-element.26), kind=kOutput, calls=%fused_computation.5 | convolution fusion | flops 2422603776 | bytes 4331520 | tf_op jit(solution)/shard_map/dot_general | solution.py:25
  64.5 1.2 %slice_add_fusion = f32[2048,128]{1,0:T(8,128)} fusion(f32[2048,384]{1,0:T(8,128)S(1)} %fusion.4), kind=kLoop, calls=%fused_computation.23 | loop fusion | flops 524288 | bytes 4194304 | tf_op jit(solution)/shard_map/add | solution.py:27
  65.6 3.8 %shard_map.83 = f32[1024,256]{1,0:T(8,128)} custom-call(f32[1024,256]{1,0:T(8,128)} %get-tuple-element.24.p_ref, f32[2,1024,128]{2,1,0:T(8,128)} %bitcast.32), custom_call_target="tpu_custom_call" | custom-call | flops 1048576 | bytes 3145728 | tf_op jit(solution)/shard_map/pallas_call | solution.py:77
  (16 shorter events, 0.2 us)
Async XLA Ops:
  6.6 6.4 %copy-start.3 = (s32[1,1,8]{2,1,0:T(1,128)S(1)}, s32[1,1,8]{2,1,0:T(1,128)}, u32[]{:S(2)}) copy-start(s32[1,1,8]{2,1,0:T(1,128)} %param.14) | copy-start | bytes 100
  12.9 8.6 %copy-start.1 = (s32[1,8192]{1,0:T(1,128)S(1)}, s32[1,8192]{1,0:T(1,128)}, u32[]{:S(2)}) copy-start(s32[1,8192]{1,0:T(1,128)} %param.15) | copy-start | bytes 98308
  12.9 21.8 %copy-start.2 = (s32[1,1,384]{2,1,0:T(1,128)S(1)}, s32[1,1,384]{2,1,0:T(1,128)}, u32[]{:S(2)}) copy-start(s32[1,1,384]{2,1,0:T(1,128)} %param.12) | copy-start | bytes 4612
  14.3 16.2 %all-to-all-start = ((f32[8,64,128]{2,1,0:T(8,128)}), f32[8,64,128]{2,1,0:T(8,128)S(1)}, u32[]{:S(2)}, u32[]{:S(2)}) async-start(f32[8,64,128]{2,1,0:T(8,128)} %bitcast.6), calls=%async_computation | async-start | bytes 524288 | tf_op jit(solution)/shard_map/all_to_all | solution.py:119
  30.4 21.5 %copy-start = (f32[64,128]{1,0:T(8,128)}, f32[64,128]{1,0:T(8,128)S(1)}, u32[]{:S(2)}) copy-start(f32[64,128]{1,0:T(8,128)S(1)} %reduce_sum.21) | copy-start | bytes 98308
  31.2 10.9 %all-to-all-start.1 = ((bf16[8,64,128]{2,1,0:T(8,128)(2,1)}), bf16[8,64,128]{2,1,0:T(8,128)(2,1)S(1)}, u32[]{:S(2)}, u32[]{:S(2)}) async-start(bf16[8,64,128]{2,1,0:T(8,128)(2,1)} %broadcast_in_dim.34), calls=%async_computation.1 | async-start | bytes 262144 | tf_op jit(solution)/shard_map/all_to_all | solution.py:125

commit v13 on v9

--- a/solution.py
+++ b/solution.py
@@ -81,7 +81,7 @@
     segments, halves = probs_split.shape[1], probs_split.shape[0]
     probs_half = probs_split.reshape(-1, block_size)
     split_idx = (pattern_idx % halves) * segments + pattern_idx // halves
-    picked = _take_rows(probs_half, split_idx)
+    picked = jnp.take(probs_half, split_idx[0], axis=0, mode="clip")
     contrib = jnp.einsum("tq,tqe->te", picked, tile_block, preferred_element_type=jnp.float32)
     capacity_f = capacity.reshape(-1, block_size).astype(jnp.float32)
     owned_blocks = capacity_f.shape[0]

time: 67.5 us -> 67.1 us (level)
  local copies, waits for them, and re-layouts: 1.8 us -> 4.08 us
  matrix products: 22.1 us -> 20 us
    gather x0 -> x1, local copies, waits for them, and re-layouts: none -> 2.27 us  [shards(): picked = jnp.take(probs_half, split_idx[0], axis=0, mode='clip')]
    dot_general x2 -> x1, matrix products: 2.51 us -> 0.43 us  [_take_rows(): lax.dot_general(sel, table, (((0,), (0,)), ((), ())), preferred_element_t...]
    unnamed x3 -> x2, other arithmetic: 1.44 us -> 0.06 us
    add x1, other arithmetic: 0.02 us -> 0.71 us  [shards(): split_idx = pattern_idx % halves * segments + pattern_idx // halves]
where the time goes in v13:
time: 67.1 us; the launch traced here: 66.6 us
  matrix products  20 us (30%)
  waiting for transfers between devices  16.2 us (24%)
  starting transfers between devices  10.8 us (16%)
  blocking collectives  8.72 us (13%)
  local copies, waits for them, and re-layouts  4.08 us (6%)
  other arithmetic  3.53 us (5%)
  Pallas kernels  2.42 us (4%)
  between operations  0.8 us (1%)
    dot_general x1, matrix products, shards(): jnp.einsum('tqe,te->tq', tile_block, slot_grads, preferred_element_type=j...  9.46 us
    all_to_all x1, waiting for transfers between devices, shards(): lax.all_to_all(partial_value.reshape(groups, owned_blocks, block_size), '...  8.88 us
    all_gather x1, blocking collectives, shards(): gathered = lax.all_gather(packed, 'region', axis=0, tiled=False)  8.72 us
    all_to_all x1, waiting for transfers between devices, shards(): lax.all_to_all(spread, 'nets', 0, 0, tiled=False).reshape(-1, block_size)  7.3 us
    all_to_all x1, starting transfers between devices, shards(): lax.all_to_all(partial_value.reshape(groups, owned_blocks, block_size), '...  7.26 us
    dot_general x1, matrix products, shards(): jnp.einsum('tq,tqe->te', picked, tile_block, preferred_element_type=jnp.f...  6.36 us
    dot_general x2, matrix products, _add_rows(): out = jnp.dot(sel, parts, preferred_element_type=jnp.float32)  3.79 us
    all_to_all x1, starting transfers between devices, shards(): lax.all_to_all(spread, 'nets', 0, 0, tiled=False).reshape(-1, block_size)  3.59 us
  transfers between devices with their start and end apart: 2, of which 2 were waited for; matrix products, arithmetic and copies ran while one was open for 0% of the time, Pallas kernels for 0%

profile of v13, /device:TPU:0, one launch (start us, length us, event | category | flops | bytes accessed | tf_op | source)
XLA Modules:
  0.0 66.6 jit_solution(15308118296484923753)
XLA Ops:
  0.6 0.7 %fusion.37 = s32[384]{0:T(512)S(1)} fusion(s32[1,1,384]{2,1,0:T(1,128)} %param.12), kind=kLoop, calls=%fused_computation.82 | loop fusion | flops 8064 | bytes 3072 | tf_op jit(solution)/shard_map/add | solution.py:83
  1.4 2.4 %shard_map.82 = (f32[1024,256]{1,0:T(8,128)}, bf16[2,1024,128]{2,1,0:T(8,128)(2,1)}) custom-call(f32[1024,256]{1,0:T(8,128)} %x_ref.1), custom_call_target="tpu_custom_call" | custom-call | flops 1310720 | bytes 2621440 | tf_op jit(solution)/shard_map/pallas_call | solution.py:45
  3.8 2.3 %gather_fusion = bf16[384,128]{1,0:T(8,128)(2,1)S(1)} fusion(bf16[2048,128]{1,0:T(8,128)(2,1)} %bitcast.46, s32[1024]{0:T(1024)S(1)} %pad_clamp_fusion), kind=kCustom, calls=%fused_computation | custom fusion | bytes 198144 | tf_op jit(solution)/shard_map/jit(_take)/gather | solution.py:84
  6.1 6.4 %fusion.2 = f32[384,1,128]{2,1,0:T(1,128)S(1)} fusion(bf16[1,1,384,128,128]{4,3,2,1,0:T(8,128)(2,1)} %param.11, bf16[384,128,1]{1,0,2:T(8,128)(2,1)S(1)} %bitcast.44), kind=kOutput, calls=%fused_computation.3 | convolution fusion | flops 12582912 | bytes 12877824 | tf_op jit(solution)/shard_map/tq,tqe->te/dot_general | solution.py:85
  12.5 0.1 reduce-precision_convert_fusion.3
  12.6 0.1 select_reduce_fusion
  12.7 0.4 fusion.13
  13.1 0.7 %slice_add_fusion.2 = f32[512,128]{1,0:T(8,128)} fusion(f32[512,384]{1,0:T(8,128)S(1)} %fusion.13), kind=kLoop, calls=%fused_computation.39 | loop fusion | flops 131072 | bytes 1048576 | tf_op jit(solution)/shard_map/add | solution.py:27
  13.8 7.3 %all-to-all-start = ((f32[8,64,128]{2,1,0:T(8,128)}), f32[8,64,128]{2,1,0:T(8,128)S(1)}, u32[]{:S(2)}, u32[]{:S(2)}) async-start(f32[8,64,128]{2,1,0:T(8,128)} %bitcast.7), calls=%async_computation | async-start | bytes 524288 | tf_op jit(solution)/shard_map/all_to_all | solution.py:90
  21.1 8.9 %all-to-all-done = f32[8,64,128]{2,1,0:T(8,128)S(1)} async-done(((f32[8,64,128]{2,1,0:T(8,128)}), f32[8,64,128]{2,1,0:T(8,128)S(1)}, u32[]{:S(2)}, u32[]{:S(2)}) %all-to-all-start) | async-done | bytes 262176 | tf_op jit(solution)/shard_map/all_to_all | solution.py:90
  30.0 0.7 broadcast_in_dim.36
  30.7 3.6 %all-to-all-start.1 = ((bf16[8,64,128]{2,1,0:T(8,128)(2,1)}), bf16[8,64,128]{2,1,0:T(8,128)(2,1)S(1)}, u32[]{:S(2)}, u32[]{:S(2)}) async-start(bf16[8,64,128]{2,1,0:T(8,128)(2,1)} %broadcast_in_dim.36), calls=%async_computation.1 | async-start | bytes 262144 | tf_op jit(solution)/shard_map/all_to_all | solution.py:96
  34.3 7.3 %all-to-all-done.1 = bf16[8,64,128]{2,1,0:T(8,128)(2,1)S(1)} async-done(((bf16[8,64,128]{2,1,0:T(8,128)(2,1)}), bf16[8,64,128]{2,1,0:T(8,128)(2,1)S(1)}, u32[]{:S(2)}, u32[]{:S(2)}) %all-to-all-start.1) | async-done | bytes 131104 | tf_op jit(solution)/shard_map/all_to_all | solution.py:96
  41.6 0.4 fusion.11
  42.0 9.5 %fusion = f32[384,1,128]{2,1,0:T(1,128)S(1)} fusion(bf16[1,1,384,128,128]{4,3,2,1,0:T(8,128)(2,1)} %param.11, bf16[384,128,1]{1,0,2:T(8,128)(2,1)S(1)} %fusion.11), kind=kOutput, calls=%fused_computation.1 | convolution fusion | flops 12582912 | bytes 12877824 | tf_op jit(solution)/shard_map/tqe,te->tq/dot_general | solution.py:98
  51.6 8.7 %all-gather.1 = f32[4,387,128]{2,1,0:T(8,128)S(1)} all-gather(f32[1,387,128]{2,1,0:T(8,128)S(1)} %maximum_bitcast_fusion), channel_id=2, replica_groups=mesh['nets'=8,'region'=4] {'region'}, dimensions={0}, use_global_device_ids=true | all-gather | bytes 990720 | tf_op jit(solution)/shard_map/all_gather | solution.py:104
  60.3 0.1 slice.62
  60.3 0.2 reduce-precision_convert_fusion.1
  60.6 3.4 %fusion.4 = f32[2048,384]{1,0:T(8,128)S(1)} fusion(s32[1536]{0:T(1024)S(1)} %convert_element_type.47, bf16[1536,128]{1,0:T(8,128)(2,1)S(1)} %get-tuple-element.29, bf16[1536,128]{1,0:T(8,128)(2,1)S(1)} %get-tuple-element.30, bf16[1536,128]{1,0:T(8,128)(2,1)S(1)} %get-tuple-element.28), kind=kOutput, calls=%fused_computation.6 | convolution fusion | flops 2422603776 | bytes 4331520 | tf_op jit(solution)/shard_map/dot_general | solution.py:25
  64.0 0.1 slice_add_fusion
  64.1 0.1 fusion.40
  64.2 1.0 %copy-done = f32[1024,256]{1,0:T(8,128)S(1)} copy-done((f32[1024,256]{1,0:T(8,128)S(1)}, f32[1024,256]{1,0:T(8,128)}, u32[]{:S(2)}) %copy-start) | copy-done | bytes 1048600
  65.2 0.2 multiply_reduce_fusion
  65.4 1.2 %subtract_multiply_fusion = f32[1024,256]{1,0:T(8,128)} fusion(f32[1024,256]{1,0:T(8,128)S(1)} %copy-done, f32[1024,128]{1,0:T(8,128)S(1)} %get-tuple-element.27, f32[1024,128]{1,0:T(8,128)S(1)} %get-tuple-element.26, f32[1024]{0:T(1024)S(1)} %multiply_reduce_fusion), kind=kLoop, calls=%fused_computation.22 | loop fusion | flops 786432 | bytes 3149824 | tf_op jit(solution)/shard_map/mul | solution.py:113
  (22 shorter events, 0.2 us)
Async XLA Ops:
  6.1 6.5 %copy-start.4 = (s32[1,1,384]{2,1,0:T(1,128)S(1)}, s32[1,1,384]{2,1,0:T(1,128)}, u32[]{:S(2)}) copy-start(s32[1,1,384]{2,1,0:T(1,128)} %param.13) | copy-start | bytes 4612
  6.1 6.5 %copy-start.5 = (s32[1,1,8]{2,1,0:T(1,128)S(1)}, s32[1,1,8]{2,1,0:T(1,128)}, u32[]{:S(2)}) copy-start(s32[1,1,8]{2,1,0:T(1,128)} %param.14) | copy-start | bytes 100
  12.5 8.6 %copy-start.2 = (s32[1,8192]{1,0:T(1,128)S(1)}, s32[1,8192]{1,0:T(1,128)}, u32[]{:S(2)}) copy-start(s32[1,8192]{1,0:T(1,128)} %param.15) | copy-start | bytes 98308
  12.5 21.8 %copy-start.3 = (s32[1,1,384]{2,1,0:T(1,128)S(1)}, s32[1,1,384]{2,1,0:T(1,128)}, u32[]{:S(2)}) copy-start(s32[1,1,384]{2,1,0:T(1,128)} %param.12) | copy-start | bytes 4612
  13.8 16.2 %all-to-all-start = ((f32[8,64,128]{2,1,0:T(8,128)}), f32[8,64,128]{2,1,0:T(8,128)S(1)}, u32[]{:S(2)}, u32[]{:S(2)}) async-start(f32[8,64,128]{2,1,0:T(8,128)} %bitcast.7), calls=%async_computation | async-start | bytes 524288 | tf_op jit(solution)/shard_map/all_to_all | solution.py:90
  30.0 21.5 %copy-start.1 = (f32[64,128]{1,0:T(8,128)}, f32[64,128]{1,0:T(8,128)S(1)}, u32[]{:S(2)}) copy-start(f32[64,128]{1,0:T(8,128)S(1)} %reduce_sum.30) | copy-start | bytes 98308
  30.7 10.9 %all-to-all-start.1 = ((bf16[8,64,128]{2,1,0:T(8,128)(2,1)}), bf16[8,64,128]{2,1,0:T(8,128)(2,1)S(1)}, u32[]{:S(2)}, u32[]{:S(2)}) async-start(bf16[8,64,128]{2,1,0:T(8,128)(2,1)} %broadcast_in_dim.36), calls=%async_computation.1 | async-start | bytes 262144 | tf_op jit(solution)/shard_map/all_to_all | solution.py:96
  64.0 1.2 %copy-start = (f32[1024,256]{1,0:T(8,128)S(1)}, f32[1024,256]{1,0:T(8,128)}, u32[]{:S(2)}) copy-start(f32[1024,256]{1,0:T(8,128)} %get-tuple-element.24) | copy-start | bytes 3145732

commit v14 on v13

--- a/solution.py
+++ b/solution.py
@@ -41,7 +41,7 @@
 def _softmax(logits, block_size):
     rows, width = logits.shape
     halves = width // block_size
-    step = min(rows, 512)
+    step = rows
     return pl.pallas_call(
         _softmax_kernel,
         grid=(rows // step,),

time: 67.1 us -> 67.4 us (level)
  no operation moved by 1% of the time
where the time goes in v14:
time: 67.4 us; the launch traced here: 66.9 us
  matrix products  20 us (30%)
  waiting for transfers between devices  16.2 us (24%)
  starting transfers between devices  10.8 us (16%)
  blocking collectives  8.71 us (13%)
  local copies, waits for them, and re-layouts  4.08 us (6%)
  other arithmetic  3.53 us (5%)
  Pallas kernels  2.71 us (4%)
  between operations  0.8 us (1%)
    dot_general x1, matrix products, shards(): jnp.einsum('tqe,te->tq', tile_block, slot_grads, preferred_element_type=j...  9.46 us
    all_to_all x1, waiting for transfers between devices, shards(): lax.all_to_all(partial_value.reshape(groups, owned_blocks, block_size), '...  8.88 us
    all_gather x1, blocking collectives, shards(): gathered = lax.all_gather(packed, 'region', axis=0, tiled=False)  8.71 us
    all_to_all x1, waiting for transfers between devices, shards(): lax.all_to_all(spread, 'nets', 0, 0, tiled=False).reshape(-1, block_size)  7.3 us
    all_to_all x1, starting transfers between devices, shards(): lax.all_to_all(partial_value.reshape(groups, owned_blocks, block_size), '...  7.25 us
    dot_general x1, matrix products, shards(): jnp.einsum('tq,tqe->te', picked, tile_block, preferred_element_type=jnp.f...  6.36 us
    dot_general x2, matrix products, _add_rows(): out = jnp.dot(sel, parts, preferred_element_type=jnp.float32)  3.79 us
    all_to_all x1, starting transfers between devices, shards(): lax.all_to_all(spread, 'nets', 0, 0, tiled=False).reshape(-1, block_size)  3.59 us
  transfers between devices with their start and end apart: 2, of which 2 were waited for; matrix products, arithmetic and copies ran while one was open for 0% of the time, Pallas kernels for 0%

profile of v14, /device:TPU:0, one launch (start us, length us, event | category | flops | bytes accessed | tf_op | source)
XLA Modules:
  0.0 66.9 jit_solution(5222587928022501323)
XLA Ops:
  0.6 0.7 %fusion.37 = s32[384]{0:T(512)S(1)} fusion(s32[1,1,384]{2,1,0:T(1,128)} %param.12), kind=kLoop, calls=%fused_computation.82 | loop fusion | flops 8064 | bytes 3072 | tf_op jit(solution)/shard_map/add | solution.py:83
  1.4 2.7 %shard_map.82 = (f32[1024,256]{1,0:T(8,128)}, bf16[2,1024,128]{2,1,0:T(8,128)(2,1)}) custom-call(f32[1024,256]{1,0:T(8,128)} %x_ref.1), custom_call_target="tpu_custom_call" | custom-call | flops 1310720 | bytes 2621440 | tf_op jit(solution)/shard_map/pallas_call | solution.py:45
  4.1 2.3 %gather_fusion = bf16[384,128]{1,0:T(8,128)(2,1)S(1)} fusion(bf16[2048,128]{1,0:T(8,128)(2,1)} %bitcast.46, s32[1024]{0:T(1024)S(1)} %pad_clamp_fusion), kind=kCustom, calls=%fused_computation | custom fusion | bytes 198144 | tf_op jit(solution)/shard_map/jit(_take)/gather | solution.py:84
  6.4 6.4 %fusion.2 = f32[384,1,128]{2,1,0:T(1,128)S(1)} fusion(bf16[1,1,384,128,128]{4,3,2,1,0:T(8,128)(2,1)} %param.11, bf16[384,128,1]{1,0,2:T(8,128)(2,1)S(1)} %bitcast.44), kind=kOutput, calls=%fused_computation.3 | convolution fusion | flops 12582912 | bytes 12877824 | tf_op jit(solution)/shard_map/tq,tqe->te/dot_general | solution.py:85
  12.7 0.1 reduce-precision_convert_fusion.3
  12.9 0.1 select_reduce_fusion
  13.0 0.4 fusion.13
  13.3 0.7 %slice_add_fusion.2 = f32[512,128]{1,0:T(8,128)} fusion(f32[512,384]{1,0:T(8,128)S(1)} %fusion.13), kind=kLoop, calls=%fused_computation.39 | loop fusion | flops 131072 | bytes 1048576 | tf_op jit(solution)/shard_map/add | solution.py:27
  14.1 7.3 %all-to-all-start = ((f32[8,64,128]{2,1,0:T(8,128)}), f32[8,64,128]{2,1,0:T(8,128)S(1)}, u32[]{:S(2)}, u32[]{:S(2)}) async-start(f32[8,64,128]{2,1,0:T(8,128)} %bitcast.7), calls=%async_computation | async-start | bytes 524288 | tf_op jit(solution)/shard_map/all_to_all | solution.py:90
  21.4 8.9 %all-to-all-done = f32[8,64,128]{2,1,0:T(8,128)S(1)} async-done(((f32[8,64,128]{2,1,0:T(8,128)}), f32[8,64,128]{2,1,0:T(8,128)S(1)}, u32[]{:S(2)}, u32[]{:S(2)}) %all-to-all-start) | async-done | bytes 262176 | tf_op jit(solution)/shard_map/all_to_all | solution.py:90
  30.3 0.7 broadcast_in_dim.36
  31.0 3.6 %all-to-all-start.1 = ((bf16[8,64,128]{2,1,0:T(8,128)(2,1)}), bf16[8,64,128]{2,1,0:T(8,128)(2,1)S(1)}, u32[]{:S(2)}, u32[]{:S(2)}) async-start(bf16[8,64,128]{2,1,0:T(8,128)(2,1)} %broadcast_in_dim.36), calls=%async_computation.1 | async-start | bytes 262144 | tf_op jit(solution)/shard_map/all_to_all | solution.py:96
  34.6 7.3 %all-to-all-done.1 = bf16[8,64,128]{2,1,0:T(8,128)(2,1)S(1)} async-done(((bf16[8,64,128]{2,1,0:T(8,128)(2,1)}), bf16[8,64,128]{2,1,0:T(8,128)(2,1)S(1)}, u32[]{:S(2)}, u32[]{:S(2)}) %all-to-all-start.1) | async-done | bytes 131104 | tf_op jit(solution)/shard_map/all_to_all | solution.py:96
  41.9 0.4 fusion.11
  42.3 9.5 %fusion = f32[384,1,128]{2,1,0:T(1,128)S(1)} fusion(bf16[1,1,384,128,128]{4,3,2,1,0:T(8,128)(2,1)} %param.11, bf16[384,128,1]{1,0,2:T(8,128)(2,1)S(1)} %fusion.11), kind=kOutput, calls=%fused_computation.1 | convolution fusion | flops 12582912 | bytes 12877824 | tf_op jit(solution)/shard_map/tqe,te->tq/dot_general | solution.py:98
  51.8 8.7 %all-gather.1 = f32[4,387,128]{2,1,0:T(8,128)S(1)} all-gather(f32[1,387,128]{2,1,0:T(8,128)S(1)} %maximum_bitcast_fusion), channel_id=2, replica_groups=mesh['nets'=8,'region'=4] {'region'}, dimensions={0}, use_global_device_ids=true | all-gather | bytes 990720 | tf_op jit(solution)/shard_map/all_gather | solution.py:104
  60.6 0.1 slice.62
  60.6 0.2 reduce-precision_convert_fusion.1
  60.9 3.4 %fusion.4 = f32[2048,384]{1,0:T(8,128)S(1)} fusion(s32[1536]{0:T(1024)S(1)} %convert_element_type.47, bf16[1536,128]{1,0:T(8,128)(2,1)S(1)} %get-tuple-element.29, bf16[1536,128]{1,0:T(8,128)(2,1)S(1)} %get-tuple-element.30, bf16[1536,128]{1,0:T(8,128)(2,1)S(1)} %get-tuple-element.28), kind=kOutput, calls=%fused_computation.6 | convolution fusion | flops 2422603776 | bytes 4331520 | tf_op jit(solution)/shard_map/dot_general | solution.py:25
  64.3 0.1 slice_add_fusion
  64.4 0.1 fusion.40
  64.5 1.0 %copy-done = f32[1024,256]{1,0:T(8,128)S(1)} copy-done((f32[1024,256]{1,0:T(8,128)S(1)}, f32[1024,256]{1,0:T(8,128)}, u32[]{:S(2)}) %copy-start) | copy-done | bytes 1048600
  65.5 0.2 multiply_reduce_fusion
  65.7 1.2 %subtract_multiply_fusion = f32[1024,256]{1,0:T(8,128)} fusion(f32[1024,256]{1,0:T(8,128)S(1)} %copy-done, f32[1024,128]{1,0:T(8,128)S(1)} %get-tuple-element.27, f32[1024,128]{1,0:T(8,128)S(1)} %get-tuple-element.26, f32[1024]{0:T(1024)S(1)} %multiply_reduce_fusion), kind=kLoop, calls=%fused_computation.22 | loop fusion | flops 786432 | bytes 3149824 | tf_op jit(solution)/shard_map/mul | solution.py:113
  (22 shorter events, 0.2 us)
Async XLA Ops:
  6.4 6.5 %copy-start.4 = (s32[1,1,384]{2,1,0:T(1,128)S(1)}, s32[1,1,384]{2,1,0:T(1,128)}, u32[]{:S(2)}) copy-start(s32[1,1,384]{2,1,0:T(1,128)} %param.13) | copy-start | bytes 4612
  6.4 6.5 %copy-start.5 = (s32[1,1,8]{2,1,0:T(1,128)S(1)}, s32[1,1,8]{2,1,0:T(1,128)}, u32[]{:S(2)}) copy-start(s32[1,1,8]{2,1,0:T(1,128)} %param.14) | copy-start | bytes 100
  12.7 8.6 %copy-start.2 = (s32[1,8192]{1,0:T(1,128)S(1)}, s32[1,8192]{1,0:T(1,128)}, u32[]{:S(2)}) copy-start(s32[1,8192]{1,0:T(1,128)} %param.15) | copy-start | bytes 98308
  12.7 21.8 %copy-start.3 = (s32[1,1,384]{2,1,0:T(1,128)S(1)}, s32[1,1,384]{2,1,0:T(1,128)}, u32[]{:S(2)}) copy-start(s32[1,1,384]{2,1,0:T(1,128)} %param.12) | copy-start | bytes 4612
  14.1 16.2 %all-to-all-start = ((f32[8,64,128]{2,1,0:T(8,128)}), f32[8,64,128]{2,1,0:T(8,128)S(1)}, u32[]{:S(2)}, u32[]{:S(2)}) async-start(f32[8,64,128]{2,1,0:T(8,128)} %bitcast.7), calls=%async_computation | async-start | bytes 524288 | tf_op jit(solution)/shard_map/all_to_all | solution.py:90
  30.3 21.5 %copy-start.1 = (f32[64,128]{1,0:T(8,128)}, f32[64,128]{1,0:T(8,128)S(1)}, u32[]{:S(2)}) copy-start(f32[64,128]{1,0:T(8,128)S(1)} %reduce_sum.30) | copy-start | bytes 98308
  31.0 10.9 %all-to-all-start.1 = ((bf16[8,64,128]{2,1,0:T(8,128)(2,1)}), bf16[8,64,128]{2,1,0:T(8,128)(2,1)S(1)}, u32[]{:S(2)}, u32[]{:S(2)}) async-start(bf16[8,64,128]{2,1,0:T(8,128)(2,1)} %broadcast_in_dim.36), calls=%async_computation.1 | async-start | bytes 262144 | tf_op jit(solution)/shard_map/all_to_all | solution.py:96
  64.3 1.2 %copy-start = (f32[1024,256]{1,0:T(8,128)S(1)}, f32[1024,256]{1,0:T(8,128)}, u32[]{:S(2)}) copy-start(f32[1024,256]{1,0:T(8,128)} %get-tuple-element.24) | copy-start | bytes 3145732

commit v15 on v13

--- a/solution.py
+++ b/solution.py
@@ -85,16 +85,31 @@
     contrib = jnp.einsum("tq,tqe->te", picked, tile_block, preferred_element_type=jnp.float32)
     capacity_f = capacity.reshape(-1, block_size).astype(jnp.float32)
     owned_blocks = capacity_f.shape[0]
-    target = owner_idx * owned_blocks + edge_idx
-    partial_value = _add_rows(jnp.where(live, target, -1), contrib, groups * owned_blocks)
-    received = lax.all_to_all(
-        partial_value.reshape(groups, owned_blocks, block_size), "nets", 0, 0, tiled=False
+    idx_rows = -(-tile_count // block_size)
+    rows_out = -(-(slot_count + idx_rows) // 8) * 8
+    edge_f = jnp.full((1, idx_rows * block_size), -1.0, jnp.float32).at[:, :tile_count].set(
+        jnp.where(live, edge_idx, -1).astype(jnp.float32)
     )
-    usage_edges = jnp.sum(received, axis=0)
+    payload = jnp.concatenate(
+        [
+            contrib.reshape(groups, slot_count, block_size),
+            jnp.broadcast_to(edge_f.reshape(1, idx_rows, block_size), (groups, idx_rows, block_size)),
+            jnp.zeros((groups, rows_out - slot_count - idx_rows, block_size), jnp.float32),
+        ],
+        axis=1,
+    )
+    received = lax.all_to_all(payload, "nets", 0, 0, tiled=False)
+    every_edge = received[:, slot_count : slot_count + idx_rows].reshape(groups, -1)
+    me = lax.axis_index("nets")
+    asked = (
+        lax.dynamic_slice_in_dim(every_edge, me * slot_count, slot_count, axis=1)
+        .astype(jnp.int32)
+        .reshape(1, -1)
+    )
+    usage_edges = _add_rows(asked, received[:, :slot_count].reshape(-1, block_size), owned_blocks)
     edge_grad = jax.nn.sigmoid(usage_edges - capacity_f).astype(jnp.bfloat16)
-    spread = jnp.broadcast_to(edge_grad[None], (groups, owned_blocks, block_size))
-    all_grads = lax.all_to_all(spread, "nets", 0, 0, tiled=False).reshape(-1, block_size)
-    slot_grads = _take_rows(all_grads, target)
+    answer = _take_rows(edge_grad, asked).reshape(groups, slot_count, block_size)
+    slot_grads = lax.all_to_all(answer, "nets", 0, 0, tiled=False).reshape(-1, block_size)
     dp_tiles = jnp.einsum("tqe,te->tq", tile_block, slot_grads, preferred_element_type=jnp.float32)
     idx_rows = -(-tile_count // block_size)
     idx_f = jnp.full((1, idx_rows * block_size), -1.0, jnp.float32).at[:, :tile_count].set(

time: 67.1 us -> 66.4 us (0.990)
  blocking collectives: 8.72 us -> 19 us
  waiting for transfers between devices: 16.2 us -> 8.4 us
  starting transfers between devices: 10.8 us -> 7.25 us
  other arithmetic: 3.53 us -> 4.92 us
    all_to_all x0 -> x1, blocking collectives: none -> 10.3 us  [shards(): lax.all_to_all(answer, 'nets', 0, 0, tiled=False).reshape(-1, block_size)]
    all_to_all x2 -> x1, waiting for transfers between devices: 16.2 us -> 8.4 us  [shards(): received = lax.all_to_all(payload, 'nets', 0, 0, tiled=False)]
    all_to_all x2 -> x1, starting transfers between devices: 10.8 us -> 7.25 us  [shards(): received = lax.all_to_all(payload, 'nets', 0, 0, tiled=False)]
    concatenate x0 -> x1, other arithmetic: none -> 0.77 us  [shards(): jnp.concatenate([contrib.reshape(groups, slot_count, block_size), jnp.bro...]
    convert_element_type x2, other arithmetic: 0.06 us -> 0.81 us  [the longest x1 0.74 us: shards(): jnp.where(live, edge_idx, -1).astype(jnp.float32)]
    add x2, other arithmetic: 0.87 us -> 0.15 us  [_add_rows(): return out[:, :width] + out[:, width:2 * width] + out[:, 2 * width:]]
  transfers between devices with their start and end apart: 2 -> 1, of which waited for: 2 -> 1; matrix products, arithmetic and copies ran while one was open for 0% -> 0% of each run, Pallas kernels for 0% -> 0%
where the time goes in v15:
time: 66.4 us; the launch traced here: 66 us
  matrix products  19.6 us (30%)
  blocking collectives  19 us (29%)
  waiting for transfers between devices  8.4 us (13%)
  starting transfers between devices  7.25 us (11%)
  other arithmetic  4.92 us (7%)
  local copies, waits for them, and re-layouts  3.6 us (5%)
  Pallas kernels  2.42 us (4%)
  between operations  0.77 us (1%)
    all_to_all x1, blocking collectives, shards(): lax.all_to_all(answer, 'nets', 0, 0, tiled=False).reshape(-1, block_size)  10.3 us
    dot_general x1, matrix products, shards(): jnp.einsum('tqe,te->tq', tile_block, slot_grads, preferred_element_type=j...  9.45 us
    all_gather x1, blocking collectives, shards(): gathered = lax.all_gather(packed, 'region', axis=0, tiled=False)  8.72 us
    all_to_all x1, waiting for transfers between devices, shards(): received = lax.all_to_all(payload, 'nets', 0, 0, tiled=False)  8.4 us
    all_to_all x1, starting transfers between devices, shards(): received = lax.all_to_all(payload, 'nets', 0, 0, tiled=False)  7.25 us
    dot_general x1, matrix products, shards(): jnp.einsum('tq,tqe->te', picked, tile_block, preferred_element_type=jnp.f...  6.35 us
    dot_general x2, matrix products, _add_rows(): out = jnp.dot(sel, parts, preferred_element_type=jnp.float32)  3.59 us
    pallas_call x1, Pallas kernels, _softmax(): pl.pallas_call(_softmax_kernel, grid=(rows // step,), in_specs=[pl.BlockS...  2.42 us
  transfers between devices with their start and end apart: 1, of which 1 were waited for; matrix products, arithmetic and copies ran while one was open for 0% of the time, Pallas kernels for 0%

profile of v15, /device:TPU:0, one launch (start us, length us, event | category | flops | bytes accessed | tf_op | source)
XLA Modules:
  0.0 66.0 jit_solution(13585496087274558401)
XLA Ops:
  0.6 0.7 %fusion.33 = s32[384]{0:T(512)S(1)} fusion(s32[1,1,384]{2,1,0:T(1,128)} %param.16), kind=kLoop, calls=%fused_computation.80 | loop fusion | flops 8064 | bytes 3072 | tf_op jit(solution)/shard_map/add | solution.py:83
  1.4 2.4 %shard_map.87 = (f32[1024,256]{1,0:T(8,128)}, bf16[2,1024,128]{2,1,0:T(8,128)(2,1)}) custom-call(f32[1024,256]{1,0:T(8,128)} %x_ref.1), custom_call_target="tpu_custom_call" | custom-call | flops 1310720 | bytes 2621440 | tf_op jit(solution)/shard_map/pallas_call | solution.py:45
  3.8 0.1 pad.18.clone
  3.9 0.7 %select_reduce_fusion = s32[384]{0:T(512)S(1)} fusion(s32[8]{0:T(128)} %bitcast.69, s32[384]{0:T(512)S(1)} %add_select_fusion), kind=kLoop, calls=%fused_computation.48 | loop fusion | flops 8832 | bytes 3104 | tf_op jit(solution)/shard_map/reduce_sum | solution.py:74
  4.6 0.7 %convert_reduce_fusion.1 = (f32[384]{0:T(512)S(1)}, f32[384]{0:T(512)S(1)}) fusion(s32[1,1,384]{2,1,0:T(1,128)} %param.17, s32[384]{0:T(512)S(1)} %select_reduce_fusion, s32[1,1,384]{2,1,0:T(1,128)} %param.16), kind=kLoop, calls=%fused_computation.79 | loop fusion | flops 12288 | bytes 7680 | tf_op jit(solution)/shard_map/convert_element_type | solution.py:91
  5.3 2.3 %gather_fusion = bf16[384,128]{1,0:T(8,128)(2,1)S(1)} fusion(bf16[2048,128]{1,0:T(8,128)(2,1)} %bitcast.60, s32[1024]{0:T(1024)S(1)} %pad_clamp_fusion), kind=kCustom, calls=%fused_computation | custom fusion | bytes 198144 | tf_op jit(solution)/shard_map/jit(_take)/gather | solution.py:84
  7.6 6.4 %fusion.2 = f32[384,1,128]{2,1,0:T(1,128)S(1)} fusion(bf16[1,1,384,128,128]{4,3,2,1,0:T(8,128)(2,1)} %param.15, bf16[384,128,1]{1,0,2:T(8,128)(2,1)S(1)} %bitcast.58), kind=kOutput, calls=%fused_computation.3 | convolution fusion | flops 12582912 | bytes 12877824 | tf_op jit(solution)/shard_map/tq,tqe->te/dot_general | solution.py:85
  14.0 0.8 %maximum_maximum_fusion = f32[8,56,128]{2,1,0:T(8,128)} fusion(f32[8,3,128]{2,1,0:T(4,128)S(1)} %broadcast_in_dim.43, f32[8,48,128]{2,1,0:T(8,128)S(1)} %bitcast.59, f32[56]{0:T(128)S(1)} %pad.18.clone), kind=kLoop, calls=%fused_computation.34 | loop fusion | flops 114688 | bytes 438496 | tf_op jit(solution)/shard_map/concatenate | solution.py:93
  14.8 7.3 %all-to-all-start = ((f32[8,56,128]{2,1,0:T(8,128)}), f32[8,56,128]{2,1,0:T(8,128)S(1)}, u32[]{:S(2)}, u32[]{:S(2)}) async-start(f32[8,56,128]{2,1,0:T(8,128)} %maximum_maximum_fusion), calls=%async_computation | async-start | bytes 458752 | tf_op jit(solution)/shard_map/all_to_all | solution.py:101
  22.1 8.4 %all-to-all-done = f32[8,56,128]{2,1,0:T(8,128)S(1)} async-done(((f32[8,56,128]{2,1,0:T(8,128)}), f32[8,56,128]{2,1,0:T(8,128)S(1)}, u32[]{:S(2)}, u32[]{:S(2)}) %all-to-all-start) | async-done | bytes 229408 | tf_op jit(solution)/shard_map/all_to_all | solution.py:101
  30.5 0.1 dynamic-slice_convert_fusion
  30.5 0.1 eq.28
  30.7 0.2 fusion.12
  30.9 0.2 convolution_convert_fusion
  31.2 10.3 %all_to_all.10 = bf16[8,48,128]{2,1,0:T(8,128)(2,1)S(1)} all-to-all(bf16[8,48,128]{2,1,0:T(8,128)(2,1)S(1)} %bitcast.63), channel_id=1, replica_groups=mesh['nets'=8,'region'=4] {'nets'}, dimensions={0} | all-to-all | bytes 196608 | tf_op jit(solution)/shard_map/all_to_all | solution.py:112
  41.5 9.5 %fusion = f32[384,1,128]{2,1,0:T(1,128)S(1)} fusion(bf16[1,1,384,128,128]{4,3,2,1,0:T(8,128)(2,1)} %param.15, bf16[384,128,1]{1,0,2:T(8,128)(2,1)S(1)} %bitcast.61), kind=kOutput, calls=%fused_computation.1 | convolution fusion | flops 12582912 | bytes 12877824 | tf_op jit(solution)/shard_map/tqe,te->tq/dot_general | solution.py:113
  51.0 8.7 %all-gather.1 = f32[4,387,128]{2,1,0:T(8,128)S(1)} all-gather(f32[1,387,128]{2,1,0:T(8,128)S(1)} %maximum_bitcast_fusion), channel_id=2, replica_groups=mesh['nets'=8,'region'=4] {'region'}, dimensions={0}, use_global_device_ids=true | all-gather | bytes 990720 | tf_op jit(solution)/shard_map/all_gather | solution.py:119
  59.8 0.2 reduce-precision_convert_fusion.1
  60.0 3.4 %fusion.4 = f32[2048,384]{1,0:T(8,128)S(1)} fusion(s32[1536]{0:T(1024)S(1)} %convert_element_type.50, bf16[1536,128]{1,0:T(8,128)(2,1)S(1)} %get-tuple-element.51, bf16[1536,128]{1,0:T(8,128)(2,1)S(1)} %get-tuple-element.52, bf16[1536,128]{1,0:T(8,128)(2,1)S(1)} %get-tuple-element.50), kind=kOutput, calls=%fused_computation.6 | convolution fusion | flops 2422603776 | bytes 4331520 | tf_op jit(solution)/shard_map/dot_general | solution.py:25
  63.4 0.1 slice_add_fusion
  63.6 0.1 fusion.37
  63.6 1.0 %copy-done = f32[1024,256]{1,0:T(8,128)S(1)} copy-done((f32[1024,256]{1,0:T(8,128)S(1)}, f32[1024,256]{1,0:T(8,128)}, u32[]{:S(2)}) %copy-start) | copy-done | bytes 1048600
  64.6 0.2 multiply_reduce_fusion
  64.8 1.2 %subtract_multiply_fusion = f32[1024,256]{1,0:T(8,128)} fusion(f32[1024,256]{1,0:T(8,128)S(1)} %copy-done, f32[1024,128]{1,0:T(8,128)S(1)} %get-tuple-element.49, f32[1024,128]{1,0:T(8,128)S(1)} %get-tuple-element.48, f32[1024]{0:T(1024)S(1)} %multiply_reduce_fusion), kind=kLoop, calls=%fused_computation.21 | loop fusion | flops 786432 | bytes 3149824 | tf_op jit(solution)/shard_map/mul | solution.py:128
  (19 shorter events, 0.3 us)
Async XLA Ops:
  7.6 14.4 %copy-start.1 = (s32[1,8192]{1,0:T(1,128)S(1)}, s32[1,8192]{1,0:T(1,128)}, u32[]{:S(2)}) copy-start(s32[1,8192]{1,0:T(1,128)} %param.19) | copy-start | bytes 98308
  14.8 15.7 %all-to-all-start = ((f32[8,56,128]{2,1,0:T(8,128)}), f32[8,56,128]{2,1,0:T(8,128)S(1)}, u32[]{:S(2)}, u32[]{:S(2)}) async-start(f32[8,56,128]{2,1,0:T(8,128)} %maximum_maximum_fusion), calls=%async_computation | async-start | bytes 458752 | tf_op jit(solution)/shard_map/all_to_all | solution.py:101
  30.9 20.0 %copy-start.2 = (f32[64,128]{1,0:T(8,128)}, f32[64,128]{1,0:T(8,128)S(1)}, u32[]{:S(2)}) copy-start(f32[64,128]{1,0:T(8,128)S(1)} %slice_add_fusion.2) | copy-start | bytes 98308
  63.4 1.2 %copy-start = (f32[1024,256]{1,0:T(8,128)S(1)}, f32[1024,256]{1,0:T(8,128)}, u32[]{:S(2)}) copy-start(f32[1024,256]{1,0:T(8,128)} %get-tuple-element.44) | copy-start | bytes 3145732

commit v16 on v15

--- a/solution.py
+++ b/solution.py
@@ -70,12 +70,7 @@
     edge_idx = tile_edge[0]
     counts = tile_counts[0]
     slot = jnp.arange(tile_count, dtype=jnp.int32)[None, :]
-    owner_idx = slot // slot_count
-    slot_limit = jnp.sum(
-        jnp.where(owner_idx == jnp.arange(groups, dtype=jnp.int32)[:, None], counts.T, 0),
-        axis=0,
-        keepdims=True,
-    )
+    slot_limit = jnp.broadcast_to(counts[0][:, None], (groups, slot_count)).reshape(1, tile_count)
     live = slot % slot_count < slot_limit
     probs, probs_split = _softmax(logits, block_size)
     segments, halves = probs_split.shape[1], probs_split.shape[0]

time: 66.4 us -> 66.5 us (level)
  local copies, waits for them, and re-layouts: 3.6 us -> 4.41 us
  other arithmetic: 4.92 us -> 4.17 us
    reduce_sum x1 -> x0, other arithmetic: 0.74 us -> none  [shards(): jnp.sum(jnp.where(owner_idx == jnp.arange(groups, dtype=jnp.int32)[:, Non...]
    broadcast_in_dim x0 -> x1, local copies, waits for them, and re-layouts: none -> 0.73 us  [shards(): jnp.broadcast_to(counts[0][:, None], (groups, slot_count))]
where the time goes in v16:
time: 66.5 us; the launch traced here: 66.1 us
  matrix products  19.6 us (29%)
  blocking collectives  19 us (29%)
  waiting for transfers between devices  8.4 us (13%)
  starting transfers between devices  7.25 us (11%)
  local copies, waits for them, and re-layouts  4.41 us (7%)
  other arithmetic  4.17 us (6%)
  Pallas kernels  2.42 us (4%)
  between operations  0.77 us (1%)
    all_to_all x1, blocking collectives, shards(): lax.all_to_all(answer, 'nets', 0, 0, tiled=False).reshape(-1, block_size)  10.3 us
    dot_general x1, matrix products, shards(): jnp.einsum('tqe,te->tq', tile_block, slot_grads, preferred_element_type=j...  9.45 us
    all_gather x1, blocking collectives, shards(): gathered = lax.all_gather(packed, 'region', axis=0, tiled=False)  8.71 us
    all_to_all x1, waiting for transfers between devices, shards(): received = lax.all_to_all(payload, 'nets', 0, 0, tiled=False)  8.4 us
    all_to_all x1, starting transfers between devices, shards(): received = lax.all_to_all(payload, 'nets', 0, 0, tiled=False)  7.25 us
    dot_general x1, matrix products, shards(): jnp.einsum('tq,tqe->te', picked, tile_block, preferred_element_type=jnp.f...  6.35 us
    dot_general x2, matrix products, _add_rows(): out = jnp.dot(sel, parts, preferred_element_type=jnp.float32)  3.59 us
    pallas_call x1, Pallas kernels, _softmax(): pl.pallas_call(_softmax_kernel, grid=(rows // step,), in_specs=[pl.BlockS...  2.42 us
  transfers between devices with their start and end apart: 1, of which 1 were waited for; matrix products, arithmetic and copies ran while one was open for 0% of the time, Pallas kernels for 0%

profile of v16, /device:TPU:0, one launch (start us, length us, event | category | flops | bytes accessed | tf_op | source)
XLA Modules:
  0.0 66.1 jit_solution(7265316444785501753)
XLA Ops:
  0.6 0.7 %fusion.30 = s32[384]{0:T(512)S(1)} fusion(s32[1,1,384]{2,1,0:T(1,128)} %param.16), kind=kLoop, calls=%fused_computation.71 | loop fusion | flops 8064 | bytes 3072 | tf_op jit(solution)/shard_map/add | solution.py:78
  1.4 0.7 %broadcast_in_dim.30 = s32[8,48]{1,0:T(8,128)S(1)} broadcast(s32[8]{0:T(128)} %bitcast.69), dimensions={0} | broadcast | bytes 1568 | tf_op jit(solution)/shard_map/broadcast_in_dim | solution.py:73
  2.1 0.1 reshape.317
  2.2 2.4 %shard_map.87 = (f32[1024,256]{1,0:T(8,128)}, bf16[2,1024,128]{2,1,0:T(8,128)(2,1)}) custom-call(f32[1024,256]{1,0:T(8,128)} %x_ref.1), custom_call_target="tpu_custom_call" | custom-call | flops 1310720 | bytes 2621440 | tf_op jit(solution)/shard_map/pallas_call | solution.py:45
  4.6 0.1 pad.18.clone
  4.7 0.7 %convert_reduce_fusion.1 = (f32[384]{0:T(512)S(1)}, f32[384]{0:T(512)S(1)}) fusion(s32[1,1,384]{2,1,0:T(1,128)} %param.17, s32[1,1,384]{2,1,0:T(1,128)S(1)} %reshape.317, s32[1,1,384]{2,1,0:T(1,128)} %param.16), kind=kLoop, calls=%fused_computation.70 | loop fusion | flops 12288 | bytes 7680 | tf_op jit(solution)/shard_map/convert_element_type | solution.py:86
  5.4 2.3 %gather_fusion = bf16[384,128]{1,0:T(8,128)(2,1)S(1)} fusion(bf16[2048,128]{1,0:T(8,128)(2,1)} %bitcast.60, s32[1024]{0:T(1024)S(1)} %pad_clamp_fusion), kind=kCustom, calls=%fused_computation | custom fusion | bytes 198144 | tf_op jit(solution)/shard_map/jit(_take)/gather | solution.py:79
  7.7 6.4 %fusion.2 = f32[384,1,128]{2,1,0:T(1,128)S(1)} fusion(bf16[1,1,384,128,128]{4,3,2,1,0:T(8,128)(2,1)} %param.15, bf16[384,128,1]{1,0,2:T(8,128)(2,1)S(1)} %bitcast.58), kind=kOutput, calls=%fused_computation.3 | convolution fusion | flops 12582912 | bytes 12877824 | tf_op jit(solution)/shard_map/tq,tqe->te/dot_general | solution.py:80
  14.0 0.8 %maximum_maximum_fusion = f32[8,56,128]{2,1,0:T(8,128)} fusion(f32[8,3,128]{2,1,0:T(4,128)S(1)} %broadcast_in_dim.33, f32[8,48,128]{2,1,0:T(8,128)S(1)} %bitcast.59, f32[56]{0:T(128)S(1)} %pad.18.clone), kind=kLoop, calls=%fused_computation.34 | loop fusion | flops 114688 | bytes 438496 | tf_op jit(solution)/shard_map/concatenate | solution.py:88
  14.8 7.3 %all-to-all-start = ((f32[8,56,128]{2,1,0:T(8,128)}), f32[8,56,128]{2,1,0:T(8,128)S(1)}, u32[]{:S(2)}, u32[]{:S(2)}) async-start(f32[8,56,128]{2,1,0:T(8,128)} %maximum_maximum_fusion), calls=%async_computation | async-start | bytes 458752 | tf_op jit(solution)/shard_map/all_to_all | solution.py:96
  22.1 8.4 %all-to-all-done = f32[8,56,128]{2,1,0:T(8,128)S(1)} async-done(((f32[8,56,128]{2,1,0:T(8,128)}), f32[8,56,128]{2,1,0:T(8,128)S(1)}, u32[]{:S(2)}, u32[]{:S(2)}) %all-to-all-start) | async-done | bytes 229408 | tf_op jit(solution)/shard_map/all_to_all | solution.py:96
  30.5 0.1 dynamic-slice_convert_fusion
  30.6 0.1 eq.19
  30.8 0.2 fusion.12
  31.0 0.2 convolution_convert_fusion
  31.2 10.3 %all_to_all.10 = bf16[8,48,128]{2,1,0:T(8,128)(2,1)S(1)} all-to-all(bf16[8,48,128]{2,1,0:T(8,128)(2,1)S(1)} %bitcast.63), channel_id=1, replica_groups=mesh['nets'=8,'region'=4] {'nets'}, dimensions={0} | all-to-all | bytes 196608 | tf_op jit(solution)/shard_map/all_to_all | solution.py:107
  41.5 9.5 %fusion = f32[384,1,128]{2,1,0:T(1,128)S(1)} fusion(bf16[1,1,384,128,128]{4,3,2,1,0:T(8,128)(2,1)} %param.15, bf16[384,128,1]{1,0,2:T(8,128)(2,1)S(1)} %bitcast.61), kind=kOutput, calls=%fused_computation.1 | convolution fusion | flops 12582912 | bytes 12877824 | tf_op jit(solution)/shard_map/tqe,te->tq/dot_general | solution.py:108
  51.0 8.7 %all-gather.1 = f32[4,387,128]{2,1,0:T(8,128)S(1)} all-gather(f32[1,387,128]{2,1,0:T(8,128)S(1)} %maximum_bitcast_fusion), channel_id=2, replica_groups=mesh['nets'=8,'region'=4] {'region'}, dimensions={0}, use_global_device_ids=true | all-gather | bytes 990720 | tf_op jit(solution)/shard_map/all_gather | solution.py:114
  59.8 0.2 reduce-precision_convert_fusion.1
  60.0 3.4 %fusion.4 = f32[2048,384]{1,0:T(8,128)S(1)} fusion(s32[1536]{0:T(1024)S(1)} %convert_element_type.50, bf16[1536,128]{1,0:T(8,128)(2,1)S(1)} %get-tuple-element.51, bf16[1536,128]{1,0:T(8,128)(2,1)S(1)} %get-tuple-element.52, bf16[1536,128]{1,0:T(8,128)(2,1)S(1)} %get-tuple-element.50), kind=kOutput, calls=%fused_computation.6 | convolution fusion | flops 2422603776 | bytes 4331520 | tf_op jit(solution)/shard_map/dot_general | solution.py:25
  63.5 0.1 slice_add_fusion
  63.7 1.0 %copy-done = f32[1024,256]{1,0:T(8,128)S(1)} copy-done((f32[1024,256]{1,0:T(8,128)S(1)}, f32[1024,256]{1,0:T(8,128)}, u32[]{:S(2)}) %copy-start) | copy-done | bytes 1048600
  64.7 0.2 multiply_reduce_fusion
  64.9 1.2 %subtract_multiply_fusion = f32[1024,256]{1,0:T(8,128)} fusion(f32[1024,256]{1,0:T(8,128)S(1)} %copy-done, f32[1024,128]{1,0:T(8,128)S(1)} %get-tuple-element.49, f32[1024,128]{1,0:T(8,128)S(1)} %get-tuple-element.48, f32[1024]{0:T(1024)S(1)} %multiply_reduce_fusion), kind=kLoop, calls=%fused_computation.21 | loop fusion | flops 786432 | bytes 3149824 | tf_op jit(solution)/shard_map/mul | solution.py:123
  (19 shorter events, 0.3 us)
Async XLA Ops:
  7.7 14.4 %copy-start.1 = (s32[1,8192]{1,0:T(1,128)S(1)}, s32[1,8192]{1,0:T(1,128)}, u32[]{:S(2)}) copy-start(s32[1,8192]{1,0:T(1,128)} %param.19) | copy-start | bytes 98308
  14.8 15.7 %all-to-all-start = ((f32[8,56,128]{2,1,0:T(8,128)}), f32[8,56,128]{2,1,0:T(8,128)S(1)}, u32[]{:S(2)}, u32[]{:S(2)}) async-start(f32[8,56,128]{2,1,0:T(8,128)} %maximum_maximum_fusion), calls=%async_computation | async-start | bytes 458752 | tf_op jit(solution)/shard_map/all_to_all | solution.py:96
  31.0 20.0 %copy-start.2 = (f32[64,128]{1,0:T(8,128)}, f32[64,128]{1,0:T(8,128)S(1)}, u32[]{:S(2)}) copy-start(f32[64,128]{1,0:T(8,128)S(1)} %slice_add_fusion.2) | copy-start | bytes 98308
  63.4 1.2 %copy-start = (f32[1024,256]{1,0:T(8,128)S(1)}, f32[1024,256]{1,0:T(8,128)}, u32[]{:S(2)}) copy-start(f32[1024,256]{1,0:T(8,128)} %get-tuple-element.44) | copy-start | bytes 3145732

commit v17 on v15

--- a/solution.py
+++ b/solution.py
@@ -27,35 +27,23 @@
     return out[:, :width] + out[:, width : 2 * width] + out[:, 2 * width :]
 
 
-def _softmax_kernel(x_ref, p_ref, h_ref):
+def _softmax_kernel(x_ref, p_ref):
     x = x_ref[...]
     e = jnp.exp(x - jnp.max(x, axis=-1, keepdims=True))
-    p = e * (1.0 / jnp.sum(e, axis=-1, keepdims=True))
-    p_ref[...] = p
-    half = p.astype(jnp.bfloat16)
-    width = h_ref.shape[-1]
-    for h in range(h_ref.shape[0]):
-        h_ref[h] = half[:, h * width : (h + 1) * width]
+    p_ref[...] = e * (1.0 / jnp.sum(e, axis=-1, keepdims=True))
 
 
-def _softmax(logits, block_size):
+def _softmax(logits):
     rows, width = logits.shape
-    halves = width // block_size
     step = min(rows, 512)
     return pl.pallas_call(
         _softmax_kernel,
         grid=(rows // step,),
         in_specs=[pl.BlockSpec((step, width), lambda i: (i, 0))],
-        out_specs=[
-            pl.BlockSpec((step, width), lambda i: (i, 0)),
-            pl.BlockSpec((halves, step, block_size), lambda i: (0, i, 0)),
-        ],
-        out_shape=[
-            jax.ShapeDtypeStruct((rows, width), jnp.float32),
-            jax.ShapeDtypeStruct((halves, rows, block_size), jnp.bfloat16),
-        ],
+        out_specs=pl.BlockSpec((step, width), lambda i: (i, 0)),
+        out_shape=jax.ShapeDtypeStruct((rows, width), jnp.float32),
         cost_estimate=pl.CostEstimate(
-            flops=5 * rows * width, transcendentals=rows * width, bytes_accessed=10 * rows * width
+            flops=5 * rows * width, transcendentals=rows * width, bytes_accessed=8 * rows * width
         ),
     )(logits)
 
@@ -77,11 +65,13 @@
         keepdims=True,
     )
     live = slot % slot_count < slot_limit
-    probs, probs_split = _softmax(logits, block_size)
-    segments, halves = probs_split.shape[1], probs_split.shape[0]
-    probs_half = probs_split.reshape(-1, block_size)
+    probs = _softmax(logits)
+    segments, halves = logits.shape[0], logits.shape[1] // block_size
+    rows_sel = jnp.take(probs, pattern_idx[0] // halves, axis=0, mode="clip")
+    rows_sel = rows_sel.reshape(tile_count, halves, block_size)
+    which = (pattern_idx[0] % halves)[:, None, None] == jnp.arange(halves)[None, :, None]
+    picked = jnp.sum(jnp.where(which, rows_sel, 0.0), axis=1).astype(jnp.bfloat16)
     split_idx = (pattern_idx % halves) * segments + pattern_idx // halves
-    picked = jnp.take(probs_half, split_idx[0], axis=0, mode="clip")
     contrib = jnp.einsum("tq,tqe->te", picked, tile_block, preferred_element_type=jnp.float32)
     capacity_f = capacity.reshape(-1, block_size).astype(jnp.float32)
     owned_blocks = capacity_f.shape[0]
@@ -123,7 +113,7 @@
         .astype(jnp.int32)
         .reshape(1, -1)
     )
-    summed = _add_rows(all_idx, all_dp, probs_half.shape[0]).reshape(halves, segments, block_size)
+    summed = _add_rows(all_idx, all_dp, halves * segments).reshape(halves, segments, block_size)
     summed_grad = jnp.concatenate([summed[h] for h in range(halves)], axis=1)
     logit_grad = probs * (summed_grad - jnp.sum(probs * summed_grad, axis=-1, keepdims=True))
     return (logit_grad, usage_edges.reshape(capacity.shape))

time: 66.4 us -> 68.5 us (1.032)
  other arithmetic: 4.92 us -> 6.22 us
  local copies, waits for them, and re-layouts: 3.6 us -> 4.43 us
    reduce_sum x0 -> x1, other arithmetic: none -> 1.84 us  [shards(): jnp.sum(jnp.where(which, rows_sel, 0.0), axis=1).astype(jnp.bfloat16)]
    select_n x0 -> x2, other arithmetic: none -> 0.72 us  [the longest x1 0.71 us: shards(): rows_sel = jnp.take(probs, pattern_idx[0] // halves, axis=0, mode='clip')]
    add x1 -> x0, other arithmetic: 0.71 us -> none  [shards(): split_idx = pattern_idx % halves * segments + pattern_idx // halves]
    unnamed x1 -> x2, other arithmetic: 0.04 us -> 0.74 us
    convert_element_type x1, other arithmetic: 0.74 us -> 0.04 us  [shards(): jnp.where(live, edge_idx, -1).astype(jnp.float32)]
where the time goes in v17:
time: 68.5 us; the launch traced here: 68.1 us
  matrix products  19.7 us (29%)
  blocking collectives  19 us (28%)
  waiting for transfers between devices  8.4 us (12%)
  starting transfers between devices  7.25 us (11%)
  other arithmetic  6.22 us (9%)
  local copies, waits for them, and re-layouts  4.43 us (6%)
  Pallas kernels  2.33 us (3%)
  between operations  0.83 us (1%)
    all_to_all x1, blocking collectives, shards(): lax.all_to_all(answer, 'nets', 0, 0, tiled=False).reshape(-1, block_size)  10.3 us
    dot_general x1, matrix products, shards(): jnp.einsum('tqe,te->tq', tile_block, slot_grads, preferred_element_type=j...  9.45 us
    all_gather x1, blocking collectives, shards(): gathered = lax.all_gather(packed, 'region', axis=0, tiled=False)  8.72 us
    all_to_all x1, waiting for transfers between devices, shards(): received = lax.all_to_all(payload, 'nets', 0, 0, tiled=False)  8.4 us
    all_to_all x1, starting transfers between devices, shards(): received = lax.all_to_all(payload, 'nets', 0, 0, tiled=False)  7.25 us
    dot_general x1, matrix products, shards(): jnp.einsum('tq,tqe->te', picked, tile_block, preferred_element_type=jnp.f...  6.36 us
    dot_general x2, matrix products, _add_rows(): out = jnp.dot(sel, parts, preferred_element_type=jnp.float32)  3.6 us
    gather x1, local copies, waits for them, and re-layouts, shards(): rows_sel = jnp.take(probs, pattern_idx[0] // halves, axis=0, mode='clip')  2.89 us
  transfers between devices with their start and end apart: 1, of which 1 were waited for; matrix products, arithmetic and copies ran while one was open for 0% of the time, Pallas kernels for 0%

profile of v17, /device:TPU:0, one launch (start us, length us, event | category | flops | bytes accessed | tf_op | source)
XLA Modules:
  0.0 68.1 jit_solution(6751919071158342535)
XLA Ops:
  0.6 0.7 %fusion.32 = s32[384]{0:T(512)S(1)} fusion(s32[1,1,384]{2,1,0:T(1,128)} %param.16), kind=kLoop, calls=%fused_computation.84 | loop fusion | flops 5760 | bytes 3072 | tf_op jit(solution)/shard_map/jit(floor_divide)/jit(_where)/select_n | solution.py:70
  1.4 0.7 %reduce.6 = s32[384]{0:T(512)S(1)} reduce(s32[1,1,384]{2,1,0:T(1,128)} %param.16, s32[]{:T(128)} %constant.132.clone.1), dimensions={0,1}, to_apply=%param.16.reduce_sub_computation | reduce | bytes 3076 | tf_op args[2]
  2.1 0.1 iota_compare_fusion.2
  2.2 2.3 %shard_map.87 = f32[1024,256]{1,0:T(8,128)} custom-call(f32[1024,256]{1,0:T(8,128)} %x_ref.1), custom_call_target="tpu_custom_call" | custom-call | flops 1310720 | bytes 2097152 | tf_op jit(solution)/shard_map/pallas_call | solution.py:39
  4.6 2.9 %gather_fusion = f32[384,256]{1,0:T(8,128)S(1)} fusion(f32[1024,256]{1,0:T(8,128)} %shard_map.87, s32[1024]{0:T(1024)S(1)} %pad_clamp_fusion), kind=kCustom, calls=%fused_computation | custom fusion | bytes 787968 | tf_op jit(solution)/shard_map/jit(_take)/gather | solution.py:70
  7.5 0.2 reshape.329
  7.8 0.1 select_reduce_fusion.1
  7.9 1.8 %select_reduce_fusion = bf16[384,128]{1,0:T(8,128)(2,1)S(1)} fusion(f32[384,2,128]{2,1,0:T(2,128)S(1)} %reshape.329, pred[384,2]{1,0:T(8,128)(4,1)S(1)} %iota_compare_fusion.2), kind=kLoop, calls=%fused_computation.24 | loop fusion | flops 147456 | bytes 492288 | tf_op jit(solution)/shard_map/reduce_sum | solution.py:73
  9.7 6.4 %fusion.2 = f32[384,1,128]{2,1,0:T(1,128)S(1)} fusion(bf16[1,1,384,128,128]{4,3,2,1,0:T(8,128)(2,1)} %param.15, bf16[384,128,1]{1,0,2:T(8,128)(2,1)S(1)} %bitcast.54), kind=kOutput, calls=%fused_computation.3 | convolution fusion | flops 12582912 | bytes 12877824 | tf_op jit(solution)/shard_map/tq,tqe->te/dot_general | solution.py:75
  16.1 0.8 %maximum_maximum_fusion = f32[8,56,128]{2,1,0:T(8,128)} fusion(f32[8,3,128]{2,1,0:T(4,128)S(1)} %broadcast_in_dim.59, f32[8,48,128]{2,1,0:T(8,128)S(1)} %bitcast.55, f32[56]{0:T(128)S(1)} %pad.18.clone), kind=kLoop, calls=%fused_computation.35 | loop fusion | flops 114688 | bytes 438496 | tf_op jit(solution)/shard_map/concatenate | solution.py:83
  16.9 7.3 %all-to-all-start = ((f32[8,56,128]{2,1,0:T(8,128)}), f32[8,56,128]{2,1,0:T(8,128)S(1)}, u32[]{:S(2)}, u32[]{:S(2)}) async-start(f32[8,56,128]{2,1,0:T(8,128)} %maximum_maximum_fusion), calls=%async_computation | async-start | bytes 458752 | tf_op jit(solution)/shard_map/all_to_all | solution.py:91
  24.2 8.4 %all-to-all-done = f32[8,56,128]{2,1,0:T(8,128)S(1)} async-done(((f32[8,56,128]{2,1,0:T(8,128)}), f32[8,56,128]{2,1,0:T(8,128)S(1)}, u32[]{:S(2)}, u32[]{:S(2)}) %all-to-all-start) | async-done | bytes 229408 | tf_op jit(solution)/shard_map/all_to_all | solution.py:91
  32.7 0.1 eq.79
  32.8 0.2 fusion.12
  33.0 0.2 convolution_convert_fusion
  33.3 10.3 %all_to_all.10 = bf16[8,48,128]{2,1,0:T(8,128)(2,1)S(1)} all-to-all(bf16[8,48,128]{2,1,0:T(8,128)(2,1)S(1)} %bitcast.58), channel_id=1, replica_groups=mesh['nets'=8,'region'=4] {'nets'}, dimensions={0} | all-to-all | bytes 196608 | tf_op jit(solution)/shard_map/all_to_all | solution.py:102
  43.6 9.5 %fusion = f32[384,1,128]{2,1,0:T(1,128)S(1)} fusion(bf16[1,1,384,128,128]{4,3,2,1,0:T(8,128)(2,1)} %param.15, bf16[384,128,1]{1,0,2:T(8,128)(2,1)S(1)} %bitcast.56), kind=kOutput, calls=%fused_computation.1 | convolution fusion | flops 12582912 | bytes 12877824 | tf_op jit(solution)/shard_map/tqe,te->tq/dot_general | solution.py:103
  53.1 8.7 %all-gather.1 = f32[4,387,128]{2,1,0:T(8,128)S(1)} all-gather(f32[1,387,128]{2,1,0:T(8,128)S(1)} %maximum_bitcast_fusion), channel_id=2, replica_groups=mesh['nets'=8,'region'=4] {'region'}, dimensions={0}, use_global_device_ids=true | all-gather | bytes 990720 | tf_op jit(solution)/shard_map/all_gather | solution.py:109
  61.9 0.2 reduce-precision_convert_fusion.1
  62.1 3.4 %fusion.4 = f32[2048,384]{1,0:T(8,128)S(1)} fusion(s32[1536]{0:T(1024)S(1)} %convert_element_type.54, bf16[1536,128]{1,0:T(8,128)(2,1)S(1)} %get-tuple-element.47, bf16[1536,128]{1,0:T(8,128)(2,1)S(1)} %get-tuple-element.48, bf16[1536,128]{1,0:T(8,128)(2,1)S(1)} %get-tuple-element.46), kind=kOutput, calls=%fused_computation.6 | convolution fusion | flops 2422603776 | bytes 4331520 | tf_op jit(solution)/shard_map/dot_general | solution.py:25
  65.5 0.1 slice_add_fusion
  65.8 1.0 %copy-done = f32[1024,256]{1,0:T(8,128)S(1)} copy-done((f32[1024,256]{1,0:T(8,128)S(1)}, f32[1024,256]{1,0:T(8,128)}, u32[]{:S(2)}) %copy-start) | copy-done | bytes 1048600
  66.7 0.2 multiply_reduce_fusion
  67.0 1.2 %subtract_multiply_fusion = f32[1024,256]{1,0:T(8,128)} fusion(f32[1024,256]{1,0:T(8,128)S(1)} %copy-done, f32[1024,128]{1,0:T(8,128)S(1)} %get-tuple-element.45, f32[1024,128]{1,0:T(8,128)S(1)} %get-tuple-element.44, f32[1024]{0:T(1024)S(1)} %multiply_reduce_fusion), kind=kLoop, calls=%fused_computation.21 | loop fusion | flops 786432 | bytes 3149824 | tf_op jit(solution)/shard_map/mul | solution.py:118
  (30 shorter events, 0.5 us)
Async XLA Ops:
  2.2 5.6 %copy-start.5 = (s32[1,1,8]{2,1,0:T(1,128)S(1)}, s32[1,1,8]{2,1,0:T(1,128)}, u32[]{:S(2)}) copy-start(s32[1,1,8]{2,1,0:T(1,128)} %param.18) | copy-start | bytes 100
  2.2 5.6 %copy-start.3 = (s32[1,1,384]{2,1,0:T(1,128)S(1)}, s32[1,1,384]{2,1,0:T(1,128)}, u32[]{:S(2)}) copy-start(s32[1,1,384]{2,1,0:T(1,128)} %param.16) | copy-start | bytes 4612
  2.2 5.6 %copy-start.4 = (s32[1,1,384]{2,1,0:T(1,128)S(1)}, s32[1,1,384]{2,1,0:T(1,128)}, u32[]{:S(2)}) copy-start(s32[1,1,384]{2,1,0:T(1,128)} %param.17) | copy-start | bytes 4612
  9.7 14.4 %copy-start.1 = (s32[1,8192]{1,0:T(1,128)S(1)}, s32[1,8192]{1,0:T(1,128)}, u32[]{:S(2)}) copy-start(s32[1,8192]{1,0:T(1,128)} %param.19) | copy-start | bytes 98308
  16.9 15.7 %all-to-all-start = ((f32[8,56,128]{2,1,0:T(8,128)}), f32[8,56,128]{2,1,0:T(8,128)S(1)}, u32[]{:S(2)}, u32[]{:S(2)}) async-start(f32[8,56,128]{2,1,0:T(8,128)} %maximum_maximum_fusion), calls=%async_computation | async-start | bytes 458752 | tf_op jit(solution)/shard_map/all_to_all | solution.py:91
  33.0 20.0 %copy-start.2 = (f32[64,128]{1,0:T(8,128)}, f32[64,128]{1,0:T(8,128)S(1)}, u32[]{:S(2)}) copy-start(f32[64,128]{1,0:T(8,128)S(1)} %slice_add_fusion.2) | copy-start | bytes 98308
  65.5 1.2 %copy-start = (f32[1024,256]{1,0:T(8,128)S(1)}, f32[1024,256]{1,0:T(8,128)}, u32[]{:S(2)}) copy-start(f32[1024,256]{1,0:T(8,128)} %shard_map.87) | copy-start | bytes 3145732

commit v18 on v15

--- a/solution.py
+++ b/solution.py
@@ -41,7 +41,7 @@
 def _softmax(logits, block_size):
     rows, width = logits.shape
     halves = width // block_size
-    step = min(rows, 512)
+    step = min(rows, 256)
     return pl.pallas_call(
         _softmax_kernel,
         grid=(rows // step,),

time: 66.4 us -> 67.9 us (1.023)
  Pallas kernels: 2.42 us -> 3.8 us
    pallas_call x1, Pallas kernels: 2.42 us -> 3.8 us  [_softmax(): pl.pallas_call(_softmax_kernel, grid=(rows // step,), in_specs=[pl.BlockS...]
where the time goes in v18:
time: 67.9 us; the launch traced here: 67.4 us
  matrix products  19.6 us (29%)
  blocking collectives  19 us (28%)
  waiting for transfers between devices  8.4 us (12%)
  starting transfers between devices  7.25 us (11%)
  other arithmetic  4.92 us (7%)
  Pallas kernels  3.8 us (6%)
  local copies, waits for them, and re-layouts  3.6 us (5%)
  between operations  0.77 us (1%)
    all_to_all x1, blocking collectives, shards(): lax.all_to_all(answer, 'nets', 0, 0, tiled=False).reshape(-1, block_size)  10.3 us
    dot_general x1, matrix products, shards(): jnp.einsum('tqe,te->tq', tile_block, slot_grads, preferred_element_type=j...  9.45 us
    all_gather x1, blocking collectives, shards(): gathered = lax.all_gather(packed, 'region', axis=0, tiled=False)  8.72 us
    all_to_all x1, waiting for transfers between devices, shards(): received = lax.all_to_all(payload, 'nets', 0, 0, tiled=False)  8.4 us
    all_to_all x1, starting transfers between devices, shards(): received = lax.all_to_all(payload, 'nets', 0, 0, tiled=False)  7.25 us
    dot_general x1, matrix products, shards(): jnp.einsum('tq,tqe->te', picked, tile_block, preferred_element_type=jnp.f...  6.35 us
    pallas_call x1, Pallas kernels, _softmax(): pl.pallas_call(_softmax_kernel, grid=(rows // step,), in_specs=[pl.BlockS...  3.8 us
    dot_general x2, matrix products, _add_rows(): out = jnp.dot(sel, parts, preferred_element_type=jnp.float32)  3.59 us
  transfers between devices with their start and end apart: 1, of which 1 were waited for; matrix products, arithmetic and copies ran while one was open for 0% of the time, Pallas kernels for 0%

profile of v18, /device:TPU:0, one launch (start us, length us, event | category | flops | bytes accessed | tf_op | source)
XLA Modules:
  0.0 67.4 jit_solution(17734522381457998063)
XLA Ops:
  0.6 0.7 %fusion.33 = s32[384]{0:T(512)S(1)} fusion(s32[1,1,384]{2,1,0:T(1,128)} %param.16), kind=kLoop, calls=%fused_computation.80 | loop fusion | flops 8064 | bytes 3072 | tf_op jit(solution)/shard_map/add | solution.py:83
  1.4 3.8 %shard_map.87 = (f32[1024,256]{1,0:T(8,128)}, bf16[2,1024,128]{2,1,0:T(8,128)(2,1)}) custom-call(f32[1024,256]{1,0:T(8,128)} %x_ref.1), custom_call_target="tpu_custom_call" | custom-call | flops 1310720 | bytes 2621440 | tf_op jit(solution)/shard_map/pallas_call | solution.py:45
  5.2 0.1 pad.18.clone
  5.2 0.7 %select_reduce_fusion = s32[384]{0:T(512)S(1)} fusion(s32[8]{0:T(128)} %bitcast.69, s32[384]{0:T(512)S(1)} %add_select_fusion), kind=kLoop, calls=%fused_computation.48 | loop fusion | flops 8832 | bytes 3104 | tf_op jit(solution)/shard_map/reduce_sum | solution.py:74
  6.0 0.7 %convert_reduce_fusion.1 = (f32[384]{0:T(512)S(1)}, f32[384]{0:T(512)S(1)}) fusion(s32[1,1,384]{2,1,0:T(1,128)} %param.17, s32[384]{0:T(512)S(1)} %select_reduce_fusion, s32[1,1,384]{2,1,0:T(1,128)} %param.16), kind=kLoop, calls=%fused_computation.79 | loop fusion | flops 12288 | bytes 7680 | tf_op jit(solution)/shard_map/convert_element_type | solution.py:91
  6.7 2.3 %gather_fusion = bf16[384,128]{1,0:T(8,128)(2,1)S(1)} fusion(bf16[2048,128]{1,0:T(8,128)(2,1)} %bitcast.60, s32[1024]{0:T(1024)S(1)} %pad_clamp_fusion), kind=kCustom, calls=%fused_computation | custom fusion | bytes 198144 | tf_op jit(solution)/shard_map/jit(_take)/gather | solution.py:84
  9.0 6.4 %fusion.2 = f32[384,1,128]{2,1,0:T(1,128)S(1)} fusion(bf16[1,1,384,128,128]{4,3,2,1,0:T(8,128)(2,1)} %param.15, bf16[384,128,1]{1,0,2:T(8,128)(2,1)S(1)} %bitcast.58), kind=kOutput, calls=%fused_computation.3 | convolution fusion | flops 12582912 | bytes 12877824 | tf_op jit(solution)/shard_map/tq,tqe->te/dot_general | solution.py:85
  15.4 0.8 %maximum_maximum_fusion = f32[8,56,128]{2,1,0:T(8,128)} fusion(f32[8,3,128]{2,1,0:T(4,128)S(1)} %broadcast_in_dim.43, f32[8,48,128]{2,1,0:T(8,128)S(1)} %bitcast.59, f32[56]{0:T(128)S(1)} %pad.18.clone), kind=kLoop, calls=%fused_computation.34 | loop fusion | flops 114688 | bytes 438496 | tf_op jit(solution)/shard_map/concatenate | solution.py:93
  16.1 7.3 %all-to-all-start = ((f32[8,56,128]{2,1,0:T(8,128)}), f32[8,56,128]{2,1,0:T(8,128)S(1)}, u32[]{:S(2)}, u32[]{:S(2)}) async-start(f32[8,56,128]{2,1,0:T(8,128)} %maximum_maximum_fusion), calls=%async_computation | async-start | bytes 458752 | tf_op jit(solution)/shard_map/all_to_all | solution.py:101
  23.4 8.4 %all-to-all-done = f32[8,56,128]{2,1,0:T(8,128)S(1)} async-done(((f32[8,56,128]{2,1,0:T(8,128)}), f32[8,56,128]{2,1,0:T(8,128)S(1)}, u32[]{:S(2)}, u32[]{:S(2)}) %all-to-all-start) | async-done | bytes 229408 | tf_op jit(solution)/shard_map/all_to_all | solution.py:101
  31.8 0.1 dynamic-slice_convert_fusion
  31.9 0.1 eq.28
  32.1 0.2 fusion.12
  32.3 0.2 convolution_convert_fusion
  32.6 10.3 %all_to_all.10 = bf16[8,48,128]{2,1,0:T(8,128)(2,1)S(1)} all-to-all(bf16[8,48,128]{2,1,0:T(8,128)(2,1)S(1)} %bitcast.63), channel_id=1, replica_groups=mesh['nets'=8,'region'=4] {'nets'}, dimensions={0} | all-to-all | bytes 196608 | tf_op jit(solution)/shard_map/all_to_all | solution.py:112
  42.8 9.5 %fusion = f32[384,1,128]{2,1,0:T(1,128)S(1)} fusion(bf16[1,1,384,128,128]{4,3,2,1,0:T(8,128)(2,1)} %param.15, bf16[384,128,1]{1,0,2:T(8,128)(2,1)S(1)} %bitcast.61), kind=kOutput, calls=%fused_computation.1 | convolution fusion | flops 12582912 | bytes 12877824 | tf_op jit(solution)/shard_map/tqe,te->tq/dot_general | solution.py:113
  52.3 8.7 %all-gather.1 = f32[4,387,128]{2,1,0:T(8,128)S(1)} all-gather(f32[1,387,128]{2,1,0:T(8,128)S(1)} %maximum_bitcast_fusion), channel_id=2, replica_groups=mesh['nets'=8,'region'=4] {'region'}, dimensions={0}, use_global_device_ids=true | all-gather | bytes 990720 | tf_op jit(solution)/shard_map/all_gather | solution.py:119
  61.1 0.2 reduce-precision_convert_fusion.1
  61.3 3.4 %fusion.4 = f32[2048,384]{1,0:T(8,128)S(1)} fusion(s32[1536]{0:T(1024)S(1)} %convert_element_type.50, bf16[1536,128]{1,0:T(8,128)(2,1)S(1)} %get-tuple-element.51, bf16[1536,128]{1,0:T(8,128)(2,1)S(1)} %get-tuple-element.52, bf16[1536,128]{1,0:T(8,128)(2,1)S(1)} %get-tuple-element.50), kind=kOutput, calls=%fused_computation.6 | convolution fusion | flops 2422603776 | bytes 4331520 | tf_op jit(solution)/shard_map/dot_general | solution.py:25
  64.8 0.1 slice_add_fusion
  64.9 0.1 fusion.37
  65.0 1.0 %copy-done = f32[1024,256]{1,0:T(8,128)S(1)} copy-done((f32[1024,256]{1,0:T(8,128)S(1)}, f32[1024,256]{1,0:T(8,128)}, u32[]{:S(2)}) %copy-start) | copy-done | bytes 1048600
  66.0 0.2 multiply_reduce_fusion
  66.2 1.2 %subtract_multiply_fusion = f32[1024,256]{1,0:T(8,128)} fusion(f32[1024,256]{1,0:T(8,128)S(1)} %copy-done, f32[1024,128]{1,0:T(8,128)S(1)} %get-tuple-element.49, f32[1024,128]{1,0:T(8,128)S(1)} %get-tuple-element.48, f32[1024]{0:T(1024)S(1)} %multiply_reduce_fusion), kind=kLoop, calls=%fused_computation.21 | loop fusion | flops 786432 | bytes 3149824 | tf_op jit(solution)/shard_map/mul | solution.py:128
  (19 shorter events, 0.3 us)
Async XLA Ops:
  9.0 14.4 %copy-start.1 = (s32[1,8192]{1,0:T(1,128)S(1)}, s32[1,8192]{1,0:T(1,128)}, u32[]{:S(2)}) copy-start(s32[1,8192]{1,0:T(1,128)} %param.19) | copy-start | bytes 98308
  16.1 15.7 %all-to-all-start = ((f32[8,56,128]{2,1,0:T(8,128)}), f32[8,56,128]{2,1,0:T(8,128)S(1)}, u32[]{:S(2)}, u32[]{:S(2)}) async-start(f32[8,56,128]{2,1,0:T(8,128)} %maximum_maximum_fusion), calls=%async_computation | async-start | bytes 458752 | tf_op jit(solution)/shard_map/all_to_all | solution.py:101
  32.3 20.0 %copy-start.2 = (f32[64,128]{1,0:T(8,128)}, f32[64,128]{1,0:T(8,128)S(1)}, u32[]{:S(2)}) copy-start(f32[64,128]{1,0:T(8,128)S(1)} %slice_add_fusion.2) | copy-start | bytes 98308
  64.8 1.2 %copy-start = (f32[1024,256]{1,0:T(8,128)S(1)}, f32[1024,256]{1,0:T(8,128)}, u32[]{:S(2)}) copy-start(f32[1024,256]{1,0:T(8,128)} %get-tuple-element.44) | copy-start | bytes 3145732

commit v19 on v17

--- a/solution.py
+++ b/solution.py
@@ -67,11 +67,12 @@
     live = slot % slot_count < slot_limit
     probs = _softmax(logits)
     segments, halves = logits.shape[0], logits.shape[1] // block_size
-    rows_sel = jnp.take(probs, pattern_idx[0] // halves, axis=0, mode="clip")
-    rows_sel = rows_sel.reshape(tile_count, halves, block_size)
-    which = (pattern_idx[0] % halves)[:, None, None] == jnp.arange(halves)[None, :, None]
-    picked = jnp.sum(jnp.where(which, rows_sel, 0.0), axis=1).astype(jnp.bfloat16)
+    half = probs.astype(jnp.bfloat16)
+    probs_half = jnp.concatenate(
+        [half[:, h * block_size : (h + 1) * block_size] for h in range(halves)], axis=0
+    )
     split_idx = (pattern_idx % halves) * segments + pattern_idx // halves
+    picked = jnp.take(probs_half, split_idx[0], axis=0, mode="clip")
     contrib = jnp.einsum("tq,tqe->te", picked, tile_block, preferred_element_type=jnp.float32)
     capacity_f = capacity.reshape(-1, block_size).astype(jnp.float32)
     owned_blocks = capacity_f.shape[0]
@@ -113,7 +114,7 @@
         .astype(jnp.int32)
         .reshape(1, -1)
     )
-    summed = _add_rows(all_idx, all_dp, halves * segments).reshape(halves, segments, block_size)
+    summed = _add_rows(all_idx, all_dp, probs_half.shape[0]).reshape(halves, segments, block_size)
     summed_grad = jnp.concatenate([summed[h] for h in range(halves)], axis=1)
     logit_grad = probs * (summed_grad - jnp.sum(probs * summed_grad, axis=-1, keepdims=True))
     return (logit_grad, usage_edges.reshape(capacity.shape))

time: 68.5 us -> 65.6 us (0.958)
  local copies, waits for them, and re-layouts: 4.43 us -> 2.82 us
  other arithmetic: 6.22 us -> 4.91 us
    reduce_sum x1 -> x0, other arithmetic: 1.84 us -> none  [shards(): jnp.sum(jnp.where(which, rows_sel, 0.0), axis=1).astype(jnp.bfloat16)]
    gather x1, local copies, waits for them, and re-layouts: 2.89 us -> 1.45 us  [shards(): picked = jnp.take(probs_half, split_idx[0], axis=0, mode='clip')]
    convert_element_type x0 -> x1, other arithmetic: none -> 1.28 us  [shards(): half = probs.astype(jnp.bfloat16)]
    add x0 -> x1, other arithmetic: none -> 0.74 us  [shards(): split_idx = pattern_idx % halves * segments + pattern_idx // halves]
    select_n x2 -> x0, other arithmetic: 0.72 us -> none  [the longest x1 0.71 us: shards(): rows_sel = jnp.take(probs, pattern_idx[0] // halves, axis=0, mode='clip')]
    unnamed x2 -> x1, other arithmetic: 0.74 us -> 0.04 us
where the time goes in v19:
time: 65.6 us; the launch traced here: 65.2 us
  matrix products  19.6 us (30%)
  blocking collectives  19 us (29%)
  waiting for transfers between devices  8.4 us (13%)
  starting transfers between devices  7.25 us (11%)
  other arithmetic  4.91 us (7%)
  local copies, waits for them, and re-layouts  2.82 us (4%)
  Pallas kernels  2.33 us (4%)
  between operations  0.83 us (1%)
    all_to_all x1, blocking collectives, shards(): lax.all_to_all(answer, 'nets', 0, 0, tiled=False).reshape(-1, block_size)  10.3 us
    dot_general x1, matrix products, shards(): jnp.einsum('tqe,te->tq', tile_block, slot_grads, preferred_element_type=j...  9.45 us
    all_gather x1, blocking collectives, shards(): gathered = lax.all_gather(packed, 'region', axis=0, tiled=False)  8.72 us
    all_to_all x1, waiting for transfers between devices, shards(): received = lax.all_to_all(payload, 'nets', 0, 0, tiled=False)  8.4 us
    all_to_all x1, starting transfers between devices, shards(): received = lax.all_to_all(payload, 'nets', 0, 0, tiled=False)  7.25 us
    dot_general x1, matrix products, shards(): jnp.einsum('tq,tqe->te', picked, tile_block, preferred_element_type=jnp.f...  6.35 us
    dot_general x2, matrix products, _add_rows(): out = jnp.dot(sel, parts, preferred_element_type=jnp.float32)  3.59 us
    pallas_call x1, Pallas kernels, _softmax(): pl.pallas_call(_softmax_kernel, grid=(rows // step,), in_specs=[pl.BlockS...  2.33 us
  transfers between devices with their start and end apart: 1, of which 1 were waited for; matrix products, arithmetic and copies ran while one was open for 0% of the time, Pallas kernels for 0%

profile of v19, /device:TPU:0, one launch (start us, length us, event | category | flops | bytes accessed | tf_op | source)
XLA Modules:
  0.0 65.2 jit_solution(8115092186147077405)
XLA Ops:
  0.7 0.7 %fusion.33 = s32[384]{0:T(512)S(1)} fusion(s32[1,1,384]{2,1,0:T(1,128)} %param.16), kind=kLoop, calls=%fused_computation.81 | loop fusion | flops 8064 | bytes 3072 | tf_op jit(solution)/shard_map/add | solution.py:74
  1.4 2.3 %shard_map.87 = f32[1024,256]{1,0:T(8,128)} custom-call(f32[1024,256]{1,0:T(8,128)} %x_ref.1), custom_call_target="tpu_custom_call" | custom-call | flops 1310720 | bytes 2097152 | tf_op jit(solution)/shard_map/pallas_call | solution.py:39
  3.8 1.3 %convert_element_type.45 = bf16[1024,256]{1,0:T(8,128)(2,1)S(1)} convert(f32[1024,256]{1,0:T(8,128)} %shard_map.87) | non-fusion elementwise | flops 262144 | bytes 1572864 | tf_op jit(solution)/shard_map/convert_element_type | solution.py:70
  5.1 0.1 pad.18.clone
  5.2 0.1 select_reduce_fusion
  5.3 1.4 %gather_fusion = bf16[384,128]{1,0:T(8,128)(2,1)S(1)} fusion(bf16[2048,128]{1,0:T(8,128)(2,1)S(1)} %pad_maximum_fusion.1, s32[1024]{0:T(1024)S(1)} %pad_clamp_fusion), kind=kCustom, calls=%fused_computation | custom fusion | bytes 198144 | tf_op jit(solution)/shard_map/jit(_take)/gather | solution.py:75
  6.8 6.4 %fusion.2 = f32[384,1,128]{2,1,0:T(1,128)S(1)} fusion(bf16[1,1,384,128,128]{4,3,2,1,0:T(8,128)(2,1)} %param.15, bf16[384,128,1]{1,0,2:T(8,128)(2,1)S(1)} %bitcast.57), kind=kOutput, calls=%fused_computation.3 | convolution fusion | flops 12582912 | bytes 12877824 | tf_op jit(solution)/shard_map/tq,tqe->te/dot_general | solution.py:76
  13.2 0.8 %maximum_maximum_fusion = f32[8,56,128]{2,1,0:T(8,128)} fusion(f32[8,3,128]{2,1,0:T(4,128)S(1)} %broadcast_in_dim.43, f32[8,48,128]{2,1,0:T(8,128)S(1)} %bitcast.58, f32[56]{0:T(128)S(1)} %pad.18.clone), kind=kLoop, calls=%fused_computation.35 | loop fusion | flops 114688 | bytes 438496 | tf_op jit(solution)/shard_map/concatenate | solution.py:84
  13.9 7.3 %all-to-all-start = ((f32[8,56,128]{2,1,0:T(8,128)}), f32[8,56,128]{2,1,0:T(8,128)S(1)}, u32[]{:S(2)}, u32[]{:S(2)}) async-start(f32[8,56,128]{2,1,0:T(8,128)} %maximum_maximum_fusion), calls=%async_computation | async-start | bytes 458752 | tf_op jit(solution)/shard_map/all_to_all | solution.py:92
  21.2 8.4 %all-to-all-done = f32[8,56,128]{2,1,0:T(8,128)S(1)} async-done(((f32[8,56,128]{2,1,0:T(8,128)}), f32[8,56,128]{2,1,0:T(8,128)S(1)}, u32[]{:S(2)}, u32[]{:S(2)}) %all-to-all-start) | async-done | bytes 229408 | tf_op jit(solution)/shard_map/all_to_all | solution.py:92
  29.6 0.1 dynamic-slice_convert_fusion
  29.7 0.1 eq.28
  29.9 0.2 fusion.12
  30.1 0.2 convolution_convert_fusion
  30.4 10.3 %all_to_all.10 = bf16[8,48,128]{2,1,0:T(8,128)(2,1)S(1)} all-to-all(bf16[8,48,128]{2,1,0:T(8,128)(2,1)S(1)} %bitcast.61), channel_id=1, replica_groups=mesh['nets'=8,'region'=4] {'nets'}, dimensions={0} | all-to-all | bytes 196608 | tf_op jit(solution)/shard_map/all_to_all | solution.py:103
  40.6 9.5 %fusion = f32[384,1,128]{2,1,0:T(1,128)S(1)} fusion(bf16[1,1,384,128,128]{4,3,2,1,0:T(8,128)(2,1)} %param.15, bf16[384,128,1]{1,0,2:T(8,128)(2,1)S(1)} %bitcast.59), kind=kOutput, calls=%fused_computation.1 | convolution fusion | flops 12582912 | bytes 12877824 | tf_op jit(solution)/shard_map/tqe,te->tq/dot_general | solution.py:104
  50.1 8.7 %all-gather.1 = f32[4,387,128]{2,1,0:T(8,128)S(1)} all-gather(f32[1,387,128]{2,1,0:T(8,128)S(1)} %maximum_bitcast_fusion), channel_id=2, replica_groups=mesh['nets'=8,'region'=4] {'region'}, dimensions={0}, use_global_device_ids=true | all-gather | bytes 990720 | tf_op jit(solution)/shard_map/all_gather | solution.py:110
  58.9 0.2 reduce-precision_convert_fusion.1
  59.1 3.4 %fusion.4 = f32[2048,384]{1,0:T(8,128)S(1)} fusion(s32[1536]{0:T(1024)S(1)} %convert_element_type.54, bf16[1536,128]{1,0:T(8,128)(2,1)S(1)} %get-tuple-element.47, bf16[1536,128]{1,0:T(8,128)(2,1)S(1)} %get-tuple-element.48, bf16[1536,128]{1,0:T(8,128)(2,1)S(1)} %get-tuple-element.46), kind=kOutput, calls=%fused_computation.6 | convolution fusion | flops 2422603776 | bytes 4331520 | tf_op jit(solution)/shard_map/dot_general | solution.py:25
  62.6 0.1 slice_add_fusion
  62.7 0.1 fusion.37
  62.8 1.0 %copy-done = f32[1024,256]{1,0:T(8,128)S(1)} copy-done((f32[1024,256]{1,0:T(8,128)S(1)}, f32[1024,256]{1,0:T(8,128)}, u32[]{:S(2)}) %copy-start) | copy-done | bytes 1048600
  63.8 0.2 multiply_reduce_fusion
  64.0 1.2 %subtract_multiply_fusion = f32[1024,256]{1,0:T(8,128)} fusion(f32[1024,256]{1,0:T(8,128)S(1)} %copy-done, f32[1024,128]{1,0:T(8,128)S(1)} %get-tuple-element.45, f32[1024,128]{1,0:T(8,128)S(1)} %get-tuple-element.44, f32[1024]{0:T(1024)S(1)} %multiply_reduce_fusion), kind=kLoop, calls=%fused_computation.21 | loop fusion | flops 786432 | bytes 3149824 | tf_op jit(solution)/shard_map/mul | solution.py:119
  (28 shorter events, 0.4 us)
Async XLA Ops:
  0.6 4.6 %copy-start.3 = (s32[1,1,384]{2,1,0:T(1,128)S(1)}, s32[1,1,384]{2,1,0:T(1,128)}, u32[]{:S(2)}) copy-start(s32[1,1,384]{2,1,0:T(1,128)} %param.16) | copy-start | bytes 4612
  0.6 4.5 %copy-start.5 = (s32[1,1,8]{2,1,0:T(1,128)S(1)}, s32[1,1,8]{2,1,0:T(1,128)}, u32[]{:S(2)}) copy-start(s32[1,1,8]{2,1,0:T(1,128)} %param.18) | copy-start | bytes 100
  0.7 4.6 %copy-start.4 = (s32[1,1,384]{2,1,0:T(1,128)S(1)}, s32[1,1,384]{2,1,0:T(1,128)}, u32[]{:S(2)}) copy-start(s32[1,1,384]{2,1,0:T(1,128)} %param.17) | copy-start | bytes 4612
  6.8 14.4 %copy-start.1 = (s32[1,8192]{1,0:T(1,128)S(1)}, s32[1,8192]{1,0:T(1,128)}, u32[]{:S(2)}) copy-start(s32[1,8192]{1,0:T(1,128)} %param.19) | copy-start | bytes 98308
  13.9 15.7 %all-to-all-start = ((f32[8,56,128]{2,1,0:T(8,128)}), f32[8,56,128]{2,1,0:T(8,128)S(1)}, u32[]{:S(2)}, u32[]{:S(2)}) async-start(f32[8,56,128]{2,1,0:T(8,128)} %maximum_maximum_fusion), calls=%async_computation | async-start | bytes 458752 | tf_op jit(solution)/shard_map/all_to_all | solution.py:92
  30.1 20.0 %copy-start.2 = (f32[64,128]{1,0:T(8,128)}, f32[64,128]{1,0:T(8,128)S(1)}, u32[]{:S(2)}) copy-start(f32[64,128]{1,0:T(8,128)S(1)} %slice_add_fusion.2) | copy-start | bytes 98308
  62.6 1.2 %copy-start = (f32[1024,256]{1,0:T(8,128)S(1)}, f32[1024,256]{1,0:T(8,128)}, u32[]{:S(2)}) copy-start(f32[1024,256]{1,0:T(8,128)} %shard_map.87) | copy-start | bytes 3145732

commit v20 on v19

--- a/solution.py
+++ b/solution.py
@@ -66,6 +66,7 @@
     )
     live = slot % slot_count < slot_limit
     probs = _softmax(logits)
+    probs, pattern_idx = lax.optimization_barrier((probs, pattern_idx))
     segments, halves = logits.shape[0], logits.shape[1] // block_size
     half = probs.astype(jnp.bfloat16)
     probs_half = jnp.concatenate(

time: 65.6 us -> 66.4 us (1.012)
  blocking collectives: 19 us -> 8.72 us
  waiting for transfers between devices: 8.4 us -> 15.5 us
  starting transfers between devices: 7.25 us -> 10.6 us
  matrix products: 19.6 us -> 20.3 us
    all_to_all x1 -> x0, blocking collectives: 10.3 us -> none  [shards(): lax.all_to_all(answer, 'nets', 0, 0, tiled=False).reshape(-1, block_size)]
    all_to_all x0 -> x1, waiting for transfers between devices: none -> 7.09 us  [shards(): lax.all_to_all(answer, 'nets', 0, 0, tiled=False).reshape(-1, block_size)]
    all_to_all x0 -> x1, starting transfers between devices: none -> 3.37 us  [shards(): lax.all_to_all(answer, 'nets', 0, 0, tiled=False).reshape(-1, block_size)]
  transfers between devices with their start and end apart: 1 -> 2, of which waited for: 1 -> 2; matrix products, arithmetic and copies ran while one was open for 0% -> 0% of each run, Pallas kernels for 0% -> 0%
where the time goes in v20:
time: 66.4 us; the launch traced here: 66 us
  matrix products  20.3 us (31%)
  waiting for transfers between devices  15.5 us (23%)
  starting transfers between devices  10.6 us (16%)
  blocking collectives  8.72 us (13%)
  other arithmetic  4.9 us (7%)
  local copies, waits for them, and re-layouts  2.82 us (4%)
  Pallas kernels  2.33 us (4%)
  between operations  0.82 us (1%)
    dot_general x1, matrix products, shards(): jnp.einsum('tqe,te->tq', tile_block, slot_grads, preferred_element_type=j...  9.45 us
    all_gather x1, blocking collectives, shards(): gathered = lax.all_gather(packed, 'region', axis=0, tiled=False)  8.72 us
    all_to_all x1, waiting for transfers between devices, shards(): received = lax.all_to_all(payload, 'nets', 0, 0, tiled=False)  8.4 us
    all_to_all x1, starting transfers between devices, shards(): received = lax.all_to_all(payload, 'nets', 0, 0, tiled=False)  7.25 us
    all_to_all x1, waiting for transfers between devices, shards(): lax.all_to_all(answer, 'nets', 0, 0, tiled=False).reshape(-1, block_size)  7.09 us
    dot_general x1, matrix products, shards(): jnp.einsum('tq,tqe->te', picked, tile_block, preferred_element_type=jnp.f...  6.35 us
    dot_general x2, matrix products, _add_rows(): out = jnp.dot(sel, parts, preferred_element_type=jnp.float32)  3.59 us
    all_to_all x1, starting transfers between devices, shards(): lax.all_to_all(answer, 'nets', 0, 0, tiled=False).reshape(-1, block_size)  3.37 us
  transfers between devices with their start and end apart: 2, of which 2 were waited for; matrix products, arithmetic and copies ran while one was open for 0% of the time, Pallas kernels for 0%

profile of v20, /device:TPU:0, one launch (start us, length us, event | category | flops | bytes accessed | tf_op | source)
XLA Modules:
  0.0 66.0 jit_solution(6599575779612657854)
XLA Ops:
  0.7 2.3 %shard_map.87 = f32[1024,256]{1,0:T(8,128)} custom-call(f32[1024,256]{1,0:T(8,128)} %x_ref.1), custom_call_target="tpu_custom_call" | custom-call | flops 1310720 | bytes 2097152 | tf_op jit(solution)/shard_map/pallas_call | solution.py:39
  3.0 0.7 %fusion.32 = (s32[384]{0:T(512)S(1)}, s32[1,384]{1,0:T(1,128)S(1)}) fusion(s32[1,384]{1,0:T(1,128)} %bitcast.52), kind=kLoop, calls=%fused_computation.77 | loop fusion | flops 8064 | bytes 4608 | tf_op jit(solution)/shard_map/add | solution.py:75
  3.7 1.3 %convert_element_type.42 = bf16[1024,256]{1,0:T(8,128)(2,1)S(1)} convert(f32[1024,256]{1,0:T(8,128)} %shard_map.87) | non-fusion elementwise | flops 262144 | bytes 1572864 | tf_op jit(solution)/shard_map/convert_element_type | solution.py:71
  5.1 0.1 pad.18.clone
  5.1 0.1 select_reduce_fusion
  5.3 1.4 %gather_fusion = bf16[384,128]{1,0:T(8,128)(2,1)S(1)} fusion(bf16[2048,128]{1,0:T(8,128)(2,1)S(1)} %pad_maximum_fusion.1, s32[1024]{0:T(1024)S(1)} %pad_clamp_fusion), kind=kCustom, calls=%fused_computation | custom fusion | bytes 198144 | tf_op jit(solution)/shard_map/jit(_take)/gather | solution.py:76
  6.8 6.4 %fusion.2 = f32[384,1,128]{2,1,0:T(1,128)S(1)} fusion(bf16[1,1,384,128,128]{4,3,2,1,0:T(8,128)(2,1)} %param.15, bf16[384,128,1]{1,0,2:T(8,128)(2,1)S(1)} %bitcast.43), kind=kOutput, calls=%fused_computation.3 | convolution fusion | flops 12582912 | bytes 12877824 | tf_op jit(solution)/shard_map/tq,tqe->te/dot_general | solution.py:77
  13.1 0.8 %maximum_maximum_fusion = f32[8,56,128]{2,1,0:T(8,128)} fusion(f32[8,3,128]{2,1,0:T(4,128)S(1)} %broadcast_in_dim.46, f32[8,48,128]{2,1,0:T(8,128)S(1)} %bitcast.44, f32[56]{0:T(128)S(1)} %pad.18.clone), kind=kLoop, calls=%fused_computation.35 | loop fusion | flops 114688 | bytes 438496 | tf_op jit(solution)/shard_map/concatenate | solution.py:85
  13.9 7.3 %all-to-all-start = ((f32[8,56,128]{2,1,0:T(8,128)}), f32[8,56,128]{2,1,0:T(8,128)S(1)}, u32[]{:S(2)}, u32[]{:S(2)}) async-start(f32[8,56,128]{2,1,0:T(8,128)} %maximum_maximum_fusion), calls=%async_computation | async-start | bytes 458752 | tf_op jit(solution)/shard_map/all_to_all | solution.py:93
  21.2 8.4 %all-to-all-done = f32[8,56,128]{2,1,0:T(8,128)S(1)} async-done(((f32[8,56,128]{2,1,0:T(8,128)}), f32[8,56,128]{2,1,0:T(8,128)S(1)}, u32[]{:S(2)}, u32[]{:S(2)}) %all-to-all-start) | async-done | bytes 229408 | tf_op jit(solution)/shard_map/all_to_all | solution.py:93
  29.6 0.1 dynamic-slice_convert_fusion
  29.7 0.1 eq.28
  29.8 0.2 fusion.12
  30.0 0.9 %convolution_convert_fusion = bf16[384,128]{1,0:T(8,128)(2,1)} fusion(s32[384]{0:T(512)S(1)} %eq.28, f32[64,128]{1,0:T(8,128)S(1)} %slice_add_fusion.2, f32[64,128]{1,0:T(8,128)S(1)} %bitcast.47), kind=kOutput, calls=%fused_computation.13 | convolution fusion | flops 6406144 | bytes 165376 | tf_op jit(solution)/shard_map/dot_general | solution.py:14
  30.9 3.4 %all-to-all-start.1 = ((bf16[8,48,128]{2,1,0:T(8,128)(2,1)}), bf16[8,48,128]{2,1,0:T(8,128)(2,1)S(1)}, u32[]{:S(2)}, u32[]{:S(2)}) async-start(bf16[8,48,128]{2,1,0:T(8,128)(2,1)} %bitcast.9), calls=%async_computation.1 | async-start | bytes 196608 | tf_op jit(solution)/shard_map/all_to_all | solution.py:104
  34.3 7.1 %all-to-all-done.1 = bf16[8,48,128]{2,1,0:T(8,128)(2,1)S(1)} async-done(((bf16[8,48,128]{2,1,0:T(8,128)(2,1)}), bf16[8,48,128]{2,1,0:T(8,128)(2,1)S(1)}, u32[]{:S(2)}, u32[]{:S(2)}) %all-to-all-start.1) | async-done | bytes 98336 | tf_op jit(solution)/shard_map/all_to_all | solution.py:104
  41.4 9.5 %fusion = f32[384,1,128]{2,1,0:T(1,128)S(1)} fusion(bf16[1,1,384,128,128]{4,3,2,1,0:T(8,128)(2,1)} %param.15, bf16[384,128,1]{1,0,2:T(8,128)(2,1)S(1)} %bitcast.45), kind=kOutput, calls=%fused_computation.1 | convolution fusion | flops 12582912 | bytes 12877824 | tf_op jit(solution)/shard_map/tqe,te->tq/dot_general | solution.py:105
  50.9 8.7 %all-gather.1 = f32[4,387,128]{2,1,0:T(8,128)S(1)} all-gather(f32[1,387,128]{2,1,0:T(8,128)S(1)} %maximum_bitcast_fusion), channel_id=2, replica_groups=mesh['nets'=8,'region'=4] {'region'}, dimensions={0}, use_global_device_ids=true | all-gather | bytes 990720 | tf_op jit(solution)/shard_map/all_gather | solution.py:111
  59.7 0.2 reduce-precision_convert_fusion.1
  59.9 3.4 %fusion.4 = f32[2048,384]{1,0:T(8,128)S(1)} fusion(s32[1536]{0:T(1024)S(1)} %convert_element_type.51, bf16[1536,128]{1,0:T(8,128)(2,1)S(1)} %get-tuple-element.51, bf16[1536,128]{1,0:T(8,128)(2,1)S(1)} %get-tuple-element.52, bf16[1536,128]{1,0:T(8,128)(2,1)S(1)} %get-tuple-element.50), kind=kOutput, calls=%fused_computation.6 | convolution fusion | flops 2422603776 | bytes 4331520 | tf_op jit(solution)/shard_map/dot_general | solution.py:25
  63.4 0.1 slice_add_fusion
  63.6 1.0 %copy-done = f32[1024,256]{1,0:T(8,128)S(1)} copy-done((f32[1024,256]{1,0:T(8,128)S(1)}, f32[1024,256]{1,0:T(8,128)}, u32[]{:S(2)}) %copy-start) | copy-done | bytes 1048600
  64.6 0.2 multiply_reduce_fusion
  64.8 1.2 %subtract_multiply_fusion = f32[1024,256]{1,0:T(8,128)} fusion(f32[1024,256]{1,0:T(8,128)S(1)} %copy-done, f32[1024,128]{1,0:T(8,128)S(1)} %get-tuple-element.49, f32[1024,128]{1,0:T(8,128)S(1)} %get-tuple-element.48, f32[1024]{0:T(1024)S(1)} %multiply_reduce_fusion), kind=kLoop, calls=%fused_computation.21 | loop fusion | flops 786432 | bytes 3149824 | tf_op jit(solution)/shard_map/mul | solution.py:120
  (28 shorter events, 0.5 us)
Async XLA Ops:
  0.6 4.5 %copy-start.4 = (s32[1,1,8]{2,1,0:T(1,128)S(1)}, s32[1,1,8]{2,1,0:T(1,128)}, u32[]{:S(2)}) copy-start(s32[1,1,8]{2,1,0:T(1,128)} %param.18) | copy-start | bytes 100
  0.6 4.6 %copy-start.3 = (s32[1,1,384]{2,1,0:T(1,128)S(1)}, s32[1,1,384]{2,1,0:T(1,128)}, u32[]{:S(2)}) copy-start(s32[1,1,384]{2,1,0:T(1,128)} %param.17) | copy-start | bytes 4612
  6.7 14.4 %copy-start.1 = (s32[1,8192]{1,0:T(1,128)S(1)}, s32[1,8192]{1,0:T(1,128)}, u32[]{:S(2)}) copy-start(s32[1,8192]{1,0:T(1,128)} %param.19) | copy-start | bytes 98308
  13.9 15.7 %all-to-all-start = ((f32[8,56,128]{2,1,0:T(8,128)}), f32[8,56,128]{2,1,0:T(8,128)S(1)}, u32[]{:S(2)}, u32[]{:S(2)}) async-start(f32[8,56,128]{2,1,0:T(8,128)} %maximum_maximum_fusion), calls=%async_computation | async-start | bytes 458752 | tf_op jit(solution)/shard_map/all_to_all | solution.py:93
  30.0 20.8 %copy-start.2 = (f32[64,128]{1,0:T(8,128)}, f32[64,128]{1,0:T(8,128)S(1)}, u32[]{:S(2)}) copy-start(f32[64,128]{1,0:T(8,128)S(1)} %slice_add_fusion.2) | copy-start | bytes 98308
  30.9 10.5 %all-to-all-start.1 = ((bf16[8,48,128]{2,1,0:T(8,128)(2,1)}), bf16[8,48,128]{2,1,0:T(8,128)(2,1)S(1)}, u32[]{:S(2)}, u32[]{:S(2)}) async-start(bf16[8,48,128]{2,1,0:T(8,128)(2,1)} %bitcast.9), calls=%async_computation.1 | async-start | bytes 196608 | tf_op jit(solution)/shard_map/all_to_all | solution.py:104
  63.3 1.2 %copy-start = (f32[1024,256]{1,0:T(8,128)S(1)}, f32[1024,256]{1,0:T(8,128)}, u32[]{:S(2)}) copy-start(f32[1024,256]{1,0:T(8,128)} %shard_map.87) | copy-start | bytes 3145732

commit v21 on v19

--- a/solution.py
+++ b/solution.py
@@ -72,7 +72,7 @@
         [half[:, h * block_size : (h + 1) * block_size] for h in range(halves)], axis=0
     )
     split_idx = (pattern_idx % halves) * segments + pattern_idx // halves
-    picked = jnp.take(probs_half, split_idx[0], axis=0, mode="clip")
+    picked = _take_rows(probs_half, split_idx)
     contrib = jnp.einsum("tq,tqe->te", picked, tile_block, preferred_element_type=jnp.float32)
     capacity_f = capacity.reshape(-1, block_size).astype(jnp.float32)
     owned_blocks = capacity_f.shape[0]

time: 65.6 us -> 65.1 us (level)
  local copies, waits for them, and re-layouts: 2.82 us -> 1.38 us
  matrix products: 19.6 us -> 20.7 us
    gather x1 -> x0, local copies, waits for them, and re-layouts: 1.45 us -> none  [shards(): picked = jnp.take(probs_half, split_idx[0], axis=0, mode='clip')]
    dot_general x1 -> x2, matrix products: 0.25 us -> 1.29 us  [_take_rows(): lax.dot_general(sel, table, (((0,), (0,)), ((), ())), preferred_element_t...]
    unnamed x1 -> x2, other arithmetic: 0.04 us -> 0.77 us
    add x1, other arithmetic: 0.74 us -> 0.02 us  [shards(): split_idx = pattern_idx % halves * segments + pattern_idx // halves]
where the time goes in v21:
time: 65.1 us; the launch traced here: 64.7 us
  matrix products  20.7 us (32%)
  blocking collectives  19 us (29%)
  waiting for transfers between devices  8.4 us (13%)
  starting transfers between devices  7.25 us (11%)
  other arithmetic  4.87 us (7%)
  Pallas kernels  2.33 us (4%)
  local copies, waits for them, and re-layouts  1.38 us (2%)
  between operations  0.82 us (1%)
    all_to_all x1, blocking collectives, shards(): lax.all_to_all(answer, 'nets', 0, 0, tiled=False).reshape(-1, block_size)  10.3 us
    dot_general x1, matrix products, shards(): jnp.einsum('tqe,te->tq', tile_block, slot_grads, preferred_element_type=j...  9.45 us
    all_gather x1, blocking collectives, shards(): gathered = lax.all_gather(packed, 'region', axis=0, tiled=False)  8.72 us
    all_to_all x1, waiting for transfers between devices, shards(): received = lax.all_to_all(payload, 'nets', 0, 0, tiled=False)  8.4 us
    all_to_all x1, starting transfers between devices, shards(): received = lax.all_to_all(payload, 'nets', 0, 0, tiled=False)  7.25 us
    dot_general x1, matrix products, shards(): jnp.einsum('tq,tqe->te', picked, tile_block, preferred_element_type=jnp.f...  6.36 us
    dot_general x2, matrix products, _add_rows(): out = jnp.dot(sel, parts, preferred_element_type=jnp.float32)  3.59 us
    pallas_call x1, Pallas kernels, _softmax(): pl.pallas_call(_softmax_kernel, grid=(rows // step,), in_specs=[pl.BlockS...  2.33 us
  transfers between devices with their start and end apart: 1, of which 1 were waited for; matrix products, arithmetic and copies ran while one was open for 0% of the time, Pallas kernels for 0%

profile of v21, /device:TPU:0, one launch (start us, length us, event | category | flops | bytes accessed | tf_op | source)
XLA Modules:
  0.0 64.7 jit_solution(9881564255216963226)
XLA Ops:
  0.7 0.7 %reduce.6 = s32[384]{0:T(512)S(1)} reduce(s32[1,1,384]{2,1,0:T(1,128)} %param.16, s32[]{:T(128)} %constant.117.clone.1), dimensions={0,1}, to_apply=%param.16.reduce_sub_computation | reduce | bytes 3076 | tf_op args[2]
  1.4 2.3 %shard_map.87 = f32[1024,256]{1,0:T(8,128)} custom-call(f32[1024,256]{1,0:T(8,128)} %x_ref.1), custom_call_target="tpu_custom_call" | custom-call | flops 1310720 | bytes 2097152 | tf_op jit(solution)/shard_map/pallas_call | solution.py:39
  3.7 1.3 %convert_element_type.49 = bf16[1024,256]{1,0:T(8,128)(2,1)S(1)} convert(f32[1024,256]{1,0:T(8,128)} %shard_map.87) | non-fusion elementwise | flops 262144 | bytes 1572864 | tf_op jit(solution)/shard_map/convert_element_type | solution.py:70
  5.1 0.1 pad.18.clone
  5.2 0.1 select_reduce_fusion
  5.3 1.0 %fusion.14 = bf16[384,128,1]{1,0,2:T(8,128)(2,1)S(1)} fusion(s32[384]{0:T(512)S(1)} %fusion.32, bf16[1024,128]{1,0:T(8,128)(2,1)S(1)} %get-tuple-element.50, bf16[1024,128]{1,0:T(8,128)(2,1)S(1)} %get-tuple-element.49), kind=kOutput, calls=%fused_computation.21 | convolution fusion | flops 203210752 | bytes 624128 | tf_op jit(solution)/shard_map/dot_general | solution.py:14
  6.4 6.4 %fusion.2 = f32[384,1,128]{2,1,0:T(1,128)S(1)} fusion(bf16[1,1,384,128,128]{4,3,2,1,0:T(8,128)(2,1)} %param.15, bf16[384,128,1]{1,0,2:T(8,128)(2,1)S(1)} %fusion.14), kind=kOutput, calls=%fused_computation.2 | convolution fusion | flops 12582912 | bytes 12877824 | tf_op jit(solution)/shard_map/tq,tqe->te/dot_general | solution.py:76
  12.7 0.8 %maximum_maximum_fusion = f32[8,56,128]{2,1,0:T(8,128)} fusion(f32[8,3,128]{2,1,0:T(4,128)S(1)} %broadcast_in_dim.42, f32[8,48,128]{2,1,0:T(8,128)S(1)} %bitcast.43, f32[56]{0:T(128)S(1)} %pad.18.clone), kind=kLoop, calls=%fused_computation.41 | loop fusion | flops 114688 | bytes 438496 | tf_op jit(solution)/shard_map/concatenate | solution.py:84
  13.5 7.3 %all-to-all-start = ((f32[8,56,128]{2,1,0:T(8,128)}), f32[8,56,128]{2,1,0:T(8,128)S(1)}, u32[]{:S(2)}, u32[]{:S(2)}) async-start(f32[8,56,128]{2,1,0:T(8,128)} %maximum_maximum_fusion), calls=%async_computation | async-start | bytes 458752 | tf_op jit(solution)/shard_map/all_to_all | solution.py:92
  20.8 8.4 %all-to-all-done = f32[8,56,128]{2,1,0:T(8,128)S(1)} async-done(((f32[8,56,128]{2,1,0:T(8,128)}), f32[8,56,128]{2,1,0:T(8,128)S(1)}, u32[]{:S(2)}, u32[]{:S(2)}) %all-to-all-start) | async-done | bytes 229408 | tf_op jit(solution)/shard_map/all_to_all | solution.py:92
  29.2 0.1 dynamic-slice_convert_fusion
  29.3 0.1 eq.72
  29.4 0.2 fusion.19
  29.6 0.2 convolution_convert_fusion
  29.9 10.3 %all_to_all.10 = bf16[8,48,128]{2,1,0:T(8,128)(2,1)S(1)} all-to-all(bf16[8,48,128]{2,1,0:T(8,128)(2,1)S(1)} %bitcast.46), channel_id=1, replica_groups=mesh['nets'=8,'region'=4] {'nets'}, dimensions={0} | all-to-all | bytes 196608 | tf_op jit(solution)/shard_map/all_to_all | solution.py:103
  40.2 9.5 %fusion = f32[384,1,128]{2,1,0:T(1,128)S(1)} fusion(bf16[1,1,384,128,128]{4,3,2,1,0:T(8,128)(2,1)} %param.15, bf16[384,128,1]{1,0,2:T(8,128)(2,1)S(1)} %bitcast.44), kind=kOutput, calls=%fused_computation | convolution fusion | flops 12582912 | bytes 12877824 | tf_op jit(solution)/shard_map/tqe,te->tq/dot_general | solution.py:104
  49.7 8.7 %all-gather.1 = f32[4,387,128]{2,1,0:T(8,128)S(1)} all-gather(f32[1,387,128]{2,1,0:T(8,128)S(1)} %maximum_bitcast_fusion), channel_id=2, replica_groups=mesh['nets'=8,'region'=4] {'region'}, dimensions={0}, use_global_device_ids=true | all-gather | bytes 990720 | tf_op jit(solution)/shard_map/all_gather | solution.py:110
  58.5 0.2 reduce-precision_convert_fusion.1
  58.7 3.4 %fusion.4 = f32[2048,384]{1,0:T(8,128)S(1)} fusion(s32[1536]{0:T(1024)S(1)} %convert_element_type.59, bf16[1536,128]{1,0:T(8,128)(2,1)S(1)} %get-tuple-element.47, bf16[1536,128]{1,0:T(8,128)(2,1)S(1)} %get-tuple-element.48, bf16[1536,128]{1,0:T(8,128)(2,1)S(1)} %get-tuple-element.46), kind=kOutput, calls=%fused_computation.5 | convolution fusion | flops 2422603776 | bytes 4331520 | tf_op jit(solution)/shard_map/dot_general | solution.py:25
  62.1 0.1 slice_add_fusion
  62.3 0.1 fusion.46
  62.4 1.0 %copy-done = f32[1024,256]{1,0:T(8,128)S(1)} copy-done((f32[1024,256]{1,0:T(8,128)S(1)}, f32[1024,256]{1,0:T(8,128)}, u32[]{:S(2)}) %copy-start) | copy-done | bytes 1048600
  63.3 0.2 multiply_reduce_fusion
  63.6 1.2 %subtract_multiply_fusion = f32[1024,256]{1,0:T(8,128)} fusion(f32[1024,256]{1,0:T(8,128)S(1)} %copy-done, f32[1024,128]{1,0:T(8,128)S(1)} %get-tuple-element.45, f32[1024,128]{1,0:T(8,128)S(1)} %get-tuple-element.44, f32[1024]{0:T(1024)S(1)} %multiply_reduce_fusion), kind=kLoop, calls=%fused_computation.25 | loop fusion | flops 786432 | bytes 3149824 | tf_op jit(solution)/shard_map/mul | solution.py:119
  (27 shorter events, 0.4 us)
Async XLA Ops:
  0.6 4.6 %copy-start.3 = (s32[1,1,384]{2,1,0:T(1,128)S(1)}, s32[1,1,384]{2,1,0:T(1,128)}, u32[]{:S(2)}) copy-start(s32[1,1,384]{2,1,0:T(1,128)} %param.16) | copy-start | bytes 4612
  0.6 4.5 %copy-start.5 = (s32[1,1,8]{2,1,0:T(1,128)S(1)}, s32[1,1,8]{2,1,0:T(1,128)}, u32[]{:S(2)}) copy-start(s32[1,1,8]{2,1,0:T(1,128)} %param.18) | copy-start | bytes 100
  0.7 4.6 %copy-start.4 = (s32[1,1,384]{2,1,0:T(1,128)S(1)}, s32[1,1,384]{2,1,0:T(1,128)}, u32[]{:S(2)}) copy-start(s32[1,1,384]{2,1,0:T(1,128)} %param.17) | copy-start | bytes 4612
  6.3 14.4 %copy-start.1 = (s32[1,8192]{1,0:T(1,128)S(1)}, s32[1,8192]{1,0:T(1,128)}, u32[]{:S(2)}) copy-start(s32[1,8192]{1,0:T(1,128)} %param.19) | copy-start | bytes 98308
  13.5 15.7 %all-to-all-start = ((f32[8,56,128]{2,1,0:T(8,128)}), f32[8,56,128]{2,1,0:T(8,128)S(1)}, u32[]{:S(2)}, u32[]{:S(2)}) async-start(f32[8,56,128]{2,1,0:T(8,128)} %maximum_maximum_fusion), calls=%async_computation | async-start | bytes 458752 | tf_op jit(solution)/shard_map/all_to_all | solution.py:92
  29.6 20.0 %copy-start.2 = (f32[64,128]{1,0:T(8,128)}, f32[64,128]{1,0:T(8,128)S(1)}, u32[]{:S(2)}) copy-start(f32[64,128]{1,0:T(8,128)S(1)} %slice_add_fusion.2) | copy-start | bytes 98308
  62.1 1.2 %copy-start = (f32[1024,256]{1,0:T(8,128)S(1)}, f32[1024,256]{1,0:T(8,128)}, u32[]{:S(2)}) copy-start(f32[1024,256]{1,0:T(8,128)} %shard_map.87) | copy-start | bytes 3145732

commit v22 on v21

--- a/solution.py
+++ b/solution.py
@@ -35,7 +35,7 @@
 
 def _softmax(logits):
     rows, width = logits.shape
-    step = min(rows, 512)
+    step = rows
     return pl.pallas_call(
         _softmax_kernel,
         grid=(rows // step,),

time: 65.1 us -> 65.4 us (level)
  no operation moved by 1% of the time
where the time goes in v22:
time: 65.4 us; the launch traced here: 65 us
  matrix products  20.7 us (32%)
  blocking collectives  19 us (29%)
  waiting for transfers between devices  8.4 us (13%)
  starting transfers between devices  7.25 us (11%)
  other arithmetic  4.87 us (7%)
  Pallas kernels  2.55 us (4%)
  local copies, waits for them, and re-layouts  1.38 us (2%)
  between operations  0.82 us (1%)
    all_to_all x1, blocking collectives, shards(): lax.all_to_all(answer, 'nets', 0, 0, tiled=False).reshape(-1, block_size)  10.3 us
    dot_general x1, matrix products, shards(): jnp.einsum('tqe,te->tq', tile_block, slot_grads, preferred_element_type=j...  9.45 us
    all_gather x1, blocking collectives, shards(): gathered = lax.all_gather(packed, 'region', axis=0, tiled=False)  8.72 us
    all_to_all x1, waiting for transfers between devices, shards(): received = lax.all_to_all(payload, 'nets', 0, 0, tiled=False)  8.4 us
    all_to_all x1, starting transfers between devices, shards(): received = lax.all_to_all(payload, 'nets', 0, 0, tiled=False)  7.25 us
    dot_general x1, matrix products, shards(): jnp.einsum('tq,tqe->te', picked, tile_block, preferred_element_type=jnp.f...  6.36 us
    dot_general x2, matrix products, _add_rows(): out = jnp.dot(sel, parts, preferred_element_type=jnp.float32)  3.6 us
    pallas_call x1, Pallas kernels, _softmax(): pl.pallas_call(_softmax_kernel, grid=(rows // step,), in_specs=[pl.BlockS...  2.55 us
  transfers between devices with their start and end apart: 1, of which 1 were waited for; matrix products, arithmetic and copies ran while one was open for 0% of the time, Pallas kernels for 0%

profile of v22, /device:TPU:0, one launch (start us, length us, event | category | flops | bytes accessed | tf_op | source)
XLA Modules:
  0.0 65.0 jit_solution(5646616304167167632)
XLA Ops:
  0.7 0.7 %reduce.6 = s32[384]{0:T(512)S(1)} reduce(s32[1,1,384]{2,1,0:T(1,128)} %param.16, s32[]{:T(128)} %constant.117.clone.1), dimensions={0,1}, to_apply=%param.16.reduce_sub_computation | reduce | bytes 3076 | tf_op args[2]
  1.4 2.5 %shard_map.87 = f32[1024,256]{1,0:T(8,128)} custom-call(f32[1024,256]{1,0:T(8,128)} %x_ref.1), custom_call_target="tpu_custom_call" | custom-call | flops 1310720 | bytes 2097152 | tf_op jit(solution)/shard_map/pallas_call | solution.py:39
  4.0 1.3 %convert_element_type.49 = bf16[1024,256]{1,0:T(8,128)(2,1)S(1)} convert(f32[1024,256]{1,0:T(8,128)} %shard_map.87) | non-fusion elementwise | flops 262144 | bytes 1572864 | tf_op jit(solution)/shard_map/convert_element_type | solution.py:70
  5.3 0.1 pad.18.clone
  5.4 0.1 select_reduce_fusion
  5.5 1.0 %fusion.14 = bf16[384,128,1]{1,0,2:T(8,128)(2,1)S(1)} fusion(s32[384]{0:T(512)S(1)} %fusion.32, bf16[1024,128]{1,0:T(8,128)(2,1)S(1)} %get-tuple-element.50, bf16[1024,128]{1,0:T(8,128)(2,1)S(1)} %get-tuple-element.49), kind=kOutput, calls=%fused_computation.21 | convolution fusion | flops 203210752 | bytes 624128 | tf_op jit(solution)/shard_map/dot_general | solution.py:14
  6.6 6.4 %fusion.2 = f32[384,1,128]{2,1,0:T(1,128)S(1)} fusion(bf16[1,1,384,128,128]{4,3,2,1,0:T(8,128)(2,1)} %param.15, bf16[384,128,1]{1,0,2:T(8,128)(2,1)S(1)} %fusion.14), kind=kOutput, calls=%fused_computation.2 | convolution fusion | flops 12582912 | bytes 12877824 | tf_op jit(solution)/shard_map/tq,tqe->te/dot_general | solution.py:76
  12.9 0.8 %maximum_maximum_fusion = f32[8,56,128]{2,1,0:T(8,128)} fusion(f32[8,3,128]{2,1,0:T(4,128)S(1)} %broadcast_in_dim.42, f32[8,48,128]{2,1,0:T(8,128)S(1)} %bitcast.43, f32[56]{0:T(128)S(1)} %pad.18.clone), kind=kLoop, calls=%fused_computation.41 | loop fusion | flops 114688 | bytes 438496 | tf_op jit(solution)/shard_map/concatenate | solution.py:84
  13.7 7.2 %all-to-all-start = ((f32[8,56,128]{2,1,0:T(8,128)}), f32[8,56,128]{2,1,0:T(8,128)S(1)}, u32[]{:S(2)}, u32[]{:S(2)}) async-start(f32[8,56,128]{2,1,0:T(8,128)} %maximum_maximum_fusion), calls=%async_computation | async-start | bytes 458752 | tf_op jit(solution)/shard_map/all_to_all | solution.py:92
  21.0 8.4 %all-to-all-done = f32[8,56,128]{2,1,0:T(8,128)S(1)} async-done(((f32[8,56,128]{2,1,0:T(8,128)}), f32[8,56,128]{2,1,0:T(8,128)S(1)}, u32[]{:S(2)}, u32[]{:S(2)}) %all-to-all-start) | async-done | bytes 229408 | tf_op jit(solution)/shard_map/all_to_all | solution.py:92
  29.4 0.1 dynamic-slice_convert_fusion
  29.5 0.1 eq.72
  29.6 0.2 fusion.19
  29.9 0.2 convolution_convert_fusion
  30.1 10.3 %all_to_all.10 = bf16[8,48,128]{2,1,0:T(8,128)(2,1)S(1)} all-to-all(bf16[8,48,128]{2,1,0:T(8,128)(2,1)S(1)} %bitcast.46), channel_id=1, replica_groups=mesh['nets'=8,'region'=4] {'nets'}, dimensions={0} | all-to-all | bytes 196608 | tf_op jit(solution)/shard_map/all_to_all | solution.py:103
  40.4 9.5 %fusion = f32[384,1,128]{2,1,0:T(1,128)S(1)} fusion(bf16[1,1,384,128,128]{4,3,2,1,0:T(8,128)(2,1)} %param.15, bf16[384,128,1]{1,0,2:T(8,128)(2,1)S(1)} %bitcast.44), kind=kOutput, calls=%fused_computation | convolution fusion | flops 12582912 | bytes 12877824 | tf_op jit(solution)/shard_map/tqe,te->tq/dot_general | solution.py:104
  49.9 8.7 %all-gather.1 = f32[4,387,128]{2,1,0:T(8,128)S(1)} all-gather(f32[1,387,128]{2,1,0:T(8,128)S(1)} %maximum_bitcast_fusion), channel_id=2, replica_groups=mesh['nets'=8,'region'=4] {'region'}, dimensions={0}, use_global_device_ids=true | all-gather | bytes 990720 | tf_op jit(solution)/shard_map/all_gather | solution.py:110
  58.7 0.2 reduce-precision_convert_fusion.1
  58.9 3.4 %fusion.4 = f32[2048,384]{1,0:T(8,128)S(1)} fusion(s32[1536]{0:T(1024)S(1)} %convert_element_type.59, bf16[1536,128]{1,0:T(8,128)(2,1)S(1)} %get-tuple-element.47, bf16[1536,128]{1,0:T(8,128)(2,1)S(1)} %get-tuple-element.48, bf16[1536,128]{1,0:T(8,128)(2,1)S(1)} %get-tuple-element.46), kind=kOutput, calls=%fused_computation.5 | convolution fusion | flops 2422603776 | bytes 4331520 | tf_op jit(solution)/shard_map/dot_general | solution.py:25
  62.3 0.1 slice_add_fusion
  62.5 0.1 fusion.46
  62.6 1.0 %copy-done = f32[1024,256]{1,0:T(8,128)S(1)} copy-done((f32[1024,256]{1,0:T(8,128)S(1)}, f32[1024,256]{1,0:T(8,128)}, u32[]{:S(2)}) %copy-start) | copy-done | bytes 1048600
  63.6 0.2 multiply_reduce_fusion
  63.8 1.2 %subtract_multiply_fusion = f32[1024,256]{1,0:T(8,128)} fusion(f32[1024,256]{1,0:T(8,128)S(1)} %copy-done, f32[1024,128]{1,0:T(8,128)S(1)} %get-tuple-element.45, f32[1024,128]{1,0:T(8,128)S(1)} %get-tuple-element.44, f32[1024]{0:T(1024)S(1)} %multiply_reduce_fusion), kind=kLoop, calls=%fused_computation.25 | loop fusion | flops 786432 | bytes 3149824 | tf_op jit(solution)/shard_map/mul | solution.py:119
  (27 shorter events, 0.4 us)
Async XLA Ops:
  0.6 4.8 %copy-start.3 = (s32[1,1,384]{2,1,0:T(1,128)S(1)}, s32[1,1,384]{2,1,0:T(1,128)}, u32[]{:S(2)}) copy-start(s32[1,1,384]{2,1,0:T(1,128)} %param.16) | copy-start | bytes 4612
  0.6 4.7 %copy-start.5 = (s32[1,1,8]{2,1,0:T(1,128)S(1)}, s32[1,1,8]{2,1,0:T(1,128)}, u32[]{:S(2)}) copy-start(s32[1,1,8]{2,1,0:T(1,128)} %param.18) | copy-start | bytes 100
  0.7 4.8 %copy-start.4 = (s32[1,1,384]{2,1,0:T(1,128)S(1)}, s32[1,1,384]{2,1,0:T(1,128)}, u32[]{:S(2)}) copy-start(s32[1,1,384]{2,1,0:T(1,128)} %param.17) | copy-start | bytes 4612
  6.6 14.4 %copy-start.1 = (s32[1,8192]{1,0:T(1,128)S(1)}, s32[1,8192]{1,0:T(1,128)}, u32[]{:S(2)}) copy-start(s32[1,8192]{1,0:T(1,128)} %param.19) | copy-start | bytes 98308
  13.7 15.7 %all-to-all-start = ((f32[8,56,128]{2,1,0:T(8,128)}), f32[8,56,128]{2,1,0:T(8,128)S(1)}, u32[]{:S(2)}, u32[]{:S(2)}) async-start(f32[8,56,128]{2,1,0:T(8,128)} %maximum_maximum_fusion), calls=%async_computation | async-start | bytes 458752 | tf_op jit(solution)/shard_map/all_to_all | solution.py:92
  29.8 20.0 %copy-start.2 = (f32[64,128]{1,0:T(8,128)}, f32[64,128]{1,0:T(8,128)S(1)}, u32[]{:S(2)}) copy-start(f32[64,128]{1,0:T(8,128)S(1)} %slice_add_fusion.2) | copy-start | bytes 98308
  62.3 1.2 %copy-start = (f32[1024,256]{1,0:T(8,128)S(1)}, f32[1024,256]{1,0:T(8,128)}, u32[]{:S(2)}) copy-start(f32[1024,256]{1,0:T(8,128)} %shard_map.87) | copy-start | bytes 3145732

commit v23 on v21

--- a/solution.py
+++ b/solution.py
@@ -58,12 +58,7 @@
     edge_idx = tile_edge[0]
     counts = tile_counts[0]
     slot = jnp.arange(tile_count, dtype=jnp.int32)[None, :]
-    owner_idx = slot // slot_count
-    slot_limit = jnp.sum(
-        jnp.where(owner_idx == jnp.arange(groups, dtype=jnp.int32)[:, None], counts.T, 0),
-        axis=0,
-        keepdims=True,
-    )
+    slot_limit = jnp.broadcast_to(counts[0][:, None], (groups, slot_count)).reshape(1, tile_count)
     live = slot % slot_count < slot_limit
     probs = _softmax(logits)
     segments, halves = logits.shape[0], logits.shape[1] // block_size

time: 65.1 us -> 65.9 us (1.012)
  local copies, waits for them, and re-layouts: 1.38 us -> 2.17 us
    broadcast_in_dim x0 -> x1, local copies, waits for them, and re-layouts: none -> 0.72 us  [shards(): jnp.broadcast_to(counts[0][:, None], (groups, slot_count))]
where the time goes in v23:
time: 65.9 us; the launch traced here: 65.5 us
  matrix products  20.7 us (31%)
  blocking collectives  19 us (29%)
  waiting for transfers between devices  8.4 us (13%)
  starting transfers between devices  7.25 us (11%)
  other arithmetic  4.8 us (7%)
  Pallas kernels  2.33 us (4%)
  local copies, waits for them, and re-layouts  2.17 us (3%)
  between operations  0.81 us (1%)
    all_to_all x1, blocking collectives, shards(): lax.all_to_all(answer, 'nets', 0, 0, tiled=False).reshape(-1, block_size)  10.3 us
    dot_general x1, matrix products, shards(): jnp.einsum('tqe,te->tq', tile_block, slot_grads, preferred_element_type=j...  9.45 us
    all_gather x1, blocking collectives, shards(): gathered = lax.all_gather(packed, 'region', axis=0, tiled=False)  8.72 us
    all_to_all x1, waiting for transfers between devices, shards(): received = lax.all_to_all(payload, 'nets', 0, 0, tiled=False)  8.4 us
    all_to_all x1, starting transfers between devices, shards(): received = lax.all_to_all(payload, 'nets', 0, 0, tiled=False)  7.25 us
    dot_general x1, matrix products, shards(): jnp.einsum('tq,tqe->te', picked, tile_block, preferred_element_type=jnp.f...  6.36 us
    dot_general x2, matrix products, _add_rows(): out = jnp.dot(sel, parts, preferred_element_type=jnp.float32)  3.59 us
    pallas_call x1, Pallas kernels, _softmax(): pl.pallas_call(_softmax_kernel, grid=(rows // step,), in_specs=[pl.BlockS...  2.33 us
  transfers between devices with their start and end apart: 1, of which 1 were waited for; matrix products, arithmetic and copies ran while one was open for 0% of the time, Pallas kernels for 0%

profile of v23, /device:TPU:0, one launch (start us, length us, event | category | flops | bytes accessed | tf_op | source)
XLA Modules:
  0.0 65.5 jit_solution(4185042196736098196)
XLA Ops:
  0.6 0.8 %reduce.6 = s32[384]{0:T(512)S(1)} reduce(s32[1,1,384]{2,1,0:T(1,128)} %param.16, s32[]{:T(128)} %constant.113.clone.1), dimensions={0,1}, to_apply=%param.16.reduce_sub_computation | reduce | bytes 3076 | tf_op args[2]
  1.4 0.7 %broadcast_in_dim.29 = s32[8,48]{1,0:T(8,128)S(1)} broadcast(s32[8]{0:T(128)} %bitcast.52), dimensions={0} | broadcast | bytes 1568 | tf_op jit(solution)/shard_map/broadcast_in_dim | solution.py:61
  2.1 0.1 reshape.253
  2.2 2.3 %shard_map.87 = f32[1024,256]{1,0:T(8,128)} custom-call(f32[1024,256]{1,0:T(8,128)} %x_ref.1), custom_call_target="tpu_custom_call" | custom-call | flops 1310720 | bytes 2097152 | tf_op jit(solution)/shard_map/pallas_call | solution.py:39
  4.6 1.3 %convert_element_type.49 = bf16[1024,256]{1,0:T(8,128)(2,1)S(1)} convert(f32[1024,256]{1,0:T(8,128)} %shard_map.87) | non-fusion elementwise | flops 262144 | bytes 1572864 | tf_op jit(solution)/shard_map/convert_element_type | solution.py:65
  5.9 0.1 pad.18.clone
  6.0 1.0 %fusion.14 = bf16[384,128,1]{1,0,2:T(8,128)(2,1)S(1)} fusion(s32[384]{0:T(512)S(1)} %fusion.32, bf16[1024,128]{1,0:T(8,128)(2,1)S(1)} %get-tuple-element.50, bf16[1024,128]{1,0:T(8,128)(2,1)S(1)} %get-tuple-element.49), kind=kOutput, calls=%fused_computation.21 | convolution fusion | flops 203210752 | bytes 624128 | tf_op jit(solution)/shard_map/dot_general | solution.py:14
  7.1 6.4 %fusion.2 = f32[384,1,128]{2,1,0:T(1,128)S(1)} fusion(bf16[1,1,384,128,128]{4,3,2,1,0:T(8,128)(2,1)} %param.15, bf16[384,128,1]{1,0,2:T(8,128)(2,1)S(1)} %fusion.14), kind=kOutput, calls=%fused_computation.2 | convolution fusion | flops 12582912 | bytes 12877824 | tf_op jit(solution)/shard_map/tq,tqe->te/dot_general | solution.py:71
  13.4 0.8 %maximum_maximum_fusion = f32[8,56,128]{2,1,0:T(8,128)} fusion(f32[8,3,128]{2,1,0:T(4,128)S(1)} %broadcast_in_dim.32, f32[8,48,128]{2,1,0:T(8,128)S(1)} %bitcast.43, f32[56]{0:T(128)S(1)} %pad.18.clone), kind=kLoop, calls=%fused_computation.41 | loop fusion | flops 114688 | bytes 438496 | tf_op jit(solution)/shard_map/concatenate | solution.py:79
  14.2 7.3 %all-to-all-start = ((f32[8,56,128]{2,1,0:T(8,128)}), f32[8,56,128]{2,1,0:T(8,128)S(1)}, u32[]{:S(2)}, u32[]{:S(2)}) async-start(f32[8,56,128]{2,1,0:T(8,128)} %maximum_maximum_fusion), calls=%async_computation | async-start | bytes 458752 | tf_op jit(solution)/shard_map/all_to_all | solution.py:87
  21.5 8.4 %all-to-all-done = f32[8,56,128]{2,1,0:T(8,128)S(1)} async-done(((f32[8,56,128]{2,1,0:T(8,128)}), f32[8,56,128]{2,1,0:T(8,128)S(1)}, u32[]{:S(2)}, u32[]{:S(2)}) %all-to-all-start) | async-done | bytes 229408 | tf_op jit(solution)/shard_map/all_to_all | solution.py:87
  29.9 0.1 dynamic-slice_convert_fusion
  30.0 0.1 eq.28
  30.1 0.2 fusion.19
  30.4 0.2 convolution_convert_fusion
  30.6 10.3 %all_to_all.10 = bf16[8,48,128]{2,1,0:T(8,128)(2,1)S(1)} all-to-all(bf16[8,48,128]{2,1,0:T(8,128)(2,1)S(1)} %bitcast.46), channel_id=1, replica_groups=mesh['nets'=8,'region'=4] {'nets'}, dimensions={0} | all-to-all | bytes 196608 | tf_op jit(solution)/shard_map/all_to_all | solution.py:98
  40.9 9.5 %fusion = f32[384,1,128]{2,1,0:T(1,128)S(1)} fusion(bf16[1,1,384,128,128]{4,3,2,1,0:T(8,128)(2,1)} %param.15, bf16[384,128,1]{1,0,2:T(8,128)(2,1)S(1)} %bitcast.44), kind=kOutput, calls=%fused_computation | convolution fusion | flops 12582912 | bytes 12877824 | tf_op jit(solution)/shard_map/tqe,te->tq/dot_general | solution.py:99
  50.4 8.7 %all-gather.1 = f32[4,387,128]{2,1,0:T(8,128)S(1)} all-gather(f32[1,387,128]{2,1,0:T(8,128)S(1)} %maximum_bitcast_fusion), channel_id=2, replica_groups=mesh['nets'=8,'region'=4] {'region'}, dimensions={0}, use_global_device_ids=true | all-gather | bytes 990720 | tf_op jit(solution)/shard_map/all_gather | solution.py:105
  59.2 0.2 reduce-precision_convert_fusion.1
  59.4 3.4 %fusion.4 = f32[2048,384]{1,0:T(8,128)S(1)} fusion(s32[1536]{0:T(1024)S(1)} %convert_element_type.59, bf16[1536,128]{1,0:T(8,128)(2,1)S(1)} %get-tuple-element.47, bf16[1536,128]{1,0:T(8,128)(2,1)S(1)} %get-tuple-element.48, bf16[1536,128]{1,0:T(8,128)(2,1)S(1)} %get-tuple-element.46), kind=kOutput, calls=%fused_computation.5 | convolution fusion | flops 2422603776 | bytes 4331520 | tf_op jit(solution)/shard_map/dot_general | solution.py:25
  62.8 0.1 slice_add_fusion
  63.1 1.0 %copy-done = f32[1024,256]{1,0:T(8,128)S(1)} copy-done((f32[1024,256]{1,0:T(8,128)S(1)}, f32[1024,256]{1,0:T(8,128)}, u32[]{:S(2)}) %copy-start) | copy-done | bytes 1048600
  64.1 0.2 multiply_reduce_fusion
  64.3 1.2 %subtract_multiply_fusion = f32[1024,256]{1,0:T(8,128)} fusion(f32[1024,256]{1,0:T(8,128)S(1)} %copy-done, f32[1024,128]{1,0:T(8,128)S(1)} %get-tuple-element.45, f32[1024,128]{1,0:T(8,128)S(1)} %get-tuple-element.44, f32[1024]{0:T(1024)S(1)} %multiply_reduce_fusion), kind=kLoop, calls=%fused_computation.25 | loop fusion | flops 786432 | bytes 3149824 | tf_op jit(solution)/shard_map/mul | solution.py:114
  (25 shorter events, 0.4 us)
Async XLA Ops:
  0.6 5.3 %copy-start.3 = (s32[1,1,384]{2,1,0:T(1,128)S(1)}, s32[1,1,384]{2,1,0:T(1,128)}, u32[]{:S(2)}) copy-start(s32[1,1,384]{2,1,0:T(1,128)} %param.16) | copy-start | bytes 4612
  0.6 5.3 %copy-start.4 = (s32[1,1,384]{2,1,0:T(1,128)S(1)}, s32[1,1,384]{2,1,0:T(1,128)}, u32[]{:S(2)}) copy-start(s32[1,1,384]{2,1,0:T(1,128)} %param.17) | copy-start | bytes 4612
  7.1 14.4 %copy-start.1 = (s32[1,8192]{1,0:T(1,128)S(1)}, s32[1,8192]{1,0:T(1,128)}, u32[]{:S(2)}) copy-start(s32[1,8192]{1,0:T(1,128)} %param.19) | copy-start | bytes 98308
  14.2 15.7 %all-to-all-start = ((f32[8,56,128]{2,1,0:T(8,128)}), f32[8,56,128]{2,1,0:T(8,128)S(1)}, u32[]{:S(2)}, u32[]{:S(2)}) async-start(f32[8,56,128]{2,1,0:T(8,128)} %maximum_maximum_fusion), calls=%async_computation | async-start | bytes 458752 | tf_op jit(solution)/shard_map/all_to_all | solution.py:87
  30.3 20.0 %copy-start.2 = (f32[64,128]{1,0:T(8,128)}, f32[64,128]{1,0:T(8,128)S(1)}, u32[]{:S(2)}) copy-start(f32[64,128]{1,0:T(8,128)S(1)} %slice_add_fusion.2) | copy-start | bytes 98308
  62.8 1.2 %copy-start = (f32[1024,256]{1,0:T(8,128)S(1)}, f32[1024,256]{1,0:T(8,128)}, u32[]{:S(2)}) copy-start(f32[1024,256]{1,0:T(8,128)} %shard_map.87) | copy-start | bytes 3145732

commit v24 on v22

--- a/solution.py
+++ b/solution.py
@@ -35,7 +35,7 @@
 
 def _softmax(logits):
     rows, width = logits.shape
-    step = rows
+    step = min(rows, 256)
     return pl.pallas_call(
         _softmax_kernel,
         grid=(rows // step,),

time: 65.4 us -> 66.6 us (1.018)
  Pallas kernels: 2.55 us -> 3.73 us
    pallas_call x1, Pallas kernels: 2.55 us -> 3.73 us  [_softmax(): pl.pallas_call(_softmax_kernel, grid=(rows // step,), in_specs=[pl.BlockS...]
where the time goes in v24:
time: 66.6 us; the launch traced here: 66.1 us
  matrix products  20.7 us (31%)
  blocking collectives  19 us (29%)
  waiting for transfers between devices  8.4 us (13%)
  starting transfers between devices  7.25 us (11%)
  other arithmetic  4.87 us (7%)
  Pallas kernels  3.73 us (6%)
  local copies, waits for them, and re-layouts  1.38 us (2%)
  between operations  0.82 us (1%)
    all_to_all x1, blocking collectives, shards(): lax.all_to_all(answer, 'nets', 0, 0, tiled=False).reshape(-1, block_size)  10.3 us
    dot_general x1, matrix products, shards(): jnp.einsum('tqe,te->tq', tile_block, slot_grads, preferred_element_type=j...  9.45 us
    all_gather x1, blocking collectives, shards(): gathered = lax.all_gather(packed, 'region', axis=0, tiled=False)  8.72 us
    all_to_all x1, waiting for transfers between devices, shards(): received = lax.all_to_all(payload, 'nets', 0, 0, tiled=False)  8.4 us
    all_to_all x1, starting transfers between devices, shards(): received = lax.all_to_all(payload, 'nets', 0, 0, tiled=False)  7.25 us
    dot_general x1, matrix products, shards(): jnp.einsum('tq,tqe->te', picked, tile_block, preferred_element_type=jnp.f...  6.36 us
    pallas_call x1, Pallas kernels, _softmax(): pl.pallas_call(_softmax_kernel, grid=(rows // step,), in_specs=[pl.BlockS...  3.73 us
    dot_general x2, matrix products, _add_rows(): out = jnp.dot(sel, parts, preferred_element_type=jnp.float32)  3.6 us
  transfers between devices with their start and end apart: 1, of which 1 were waited for; matrix products, arithmetic and copies ran while one was open for 0% of the time, Pallas kernels for 0%

profile of v24, /device:TPU:0, one launch (start us, length us, event | category | flops | bytes accessed | tf_op | source)
XLA Modules:
  0.0 66.1 jit_solution(14483178737329369706)
XLA Ops:
  0.7 0.7 %reduce.6 = s32[384]{0:T(512)S(1)} reduce(s32[1,1,384]{2,1,0:T(1,128)} %param.16, s32[]{:T(128)} %constant.117.clone.1), dimensions={0,1}, to_apply=%param.16.reduce_sub_computation | reduce | bytes 3076 | tf_op args[2]
  1.4 3.7 %shard_map.87 = f32[1024,256]{1,0:T(8,128)} custom-call(f32[1024,256]{1,0:T(8,128)} %x_ref.1), custom_call_target="tpu_custom_call" | custom-call | flops 1310720 | bytes 2097152 | tf_op jit(solution)/shard_map/pallas_call | solution.py:39
  5.2 1.3 %convert_element_type.49 = bf16[1024,256]{1,0:T(8,128)(2,1)S(1)} convert(f32[1024,256]{1,0:T(8,128)} %shard_map.87) | non-fusion elementwise | flops 262144 | bytes 1572864 | tf_op jit(solution)/shard_map/convert_element_type | solution.py:70
  6.5 0.1 pad.18.clone
  6.6 0.1 select_reduce_fusion
  6.7 1.0 %fusion.14 = bf16[384,128,1]{1,0,2:T(8,128)(2,1)S(1)} fusion(s32[384]{0:T(512)S(1)} %fusion.32, bf16[1024,128]{1,0:T(8,128)(2,1)S(1)} %get-tuple-element.50, bf16[1024,128]{1,0:T(8,128)(2,1)S(1)} %get-tuple-element.49), kind=kOutput, calls=%fused_computation.21 | convolution fusion | flops 203210752 | bytes 624128 | tf_op jit(solution)/shard_map/dot_general | solution.py:14
  7.8 6.4 %fusion.2 = f32[384,1,128]{2,1,0:T(1,128)S(1)} fusion(bf16[1,1,384,128,128]{4,3,2,1,0:T(8,128)(2,1)} %param.15, bf16[384,128,1]{1,0,2:T(8,128)(2,1)S(1)} %fusion.14), kind=kOutput, calls=%fused_computation.2 | convolution fusion | flops 12582912 | bytes 12877824 | tf_op jit(solution)/shard_map/tq,tqe->te/dot_general | solution.py:76
  14.1 0.8 %maximum_maximum_fusion = f32[8,56,128]{2,1,0:T(8,128)} fusion(f32[8,3,128]{2,1,0:T(4,128)S(1)} %broadcast_in_dim.42, f32[8,48,128]{2,1,0:T(8,128)S(1)} %bitcast.43, f32[56]{0:T(128)S(1)} %pad.18.clone), kind=kLoop, calls=%fused_computation.41 | loop fusion | flops 114688 | bytes 438496 | tf_op jit(solution)/shard_map/concatenate | solution.py:84
  14.9 7.3 %all-to-all-start = ((f32[8,56,128]{2,1,0:T(8,128)}), f32[8,56,128]{2,1,0:T(8,128)S(1)}, u32[]{:S(2)}, u32[]{:S(2)}) async-start(f32[8,56,128]{2,1,0:T(8,128)} %maximum_maximum_fusion), calls=%async_computation | async-start | bytes 458752 | tf_op jit(solution)/shard_map/all_to_all | solution.py:92
  22.2 8.4 %all-to-all-done = f32[8,56,128]{2,1,0:T(8,128)S(1)} async-done(((f32[8,56,128]{2,1,0:T(8,128)}), f32[8,56,128]{2,1,0:T(8,128)S(1)}, u32[]{:S(2)}, u32[]{:S(2)}) %all-to-all-start) | async-done | bytes 229408 | tf_op jit(solution)/shard_map/all_to_all | solution.py:92
  30.6 0.1 dynamic-slice_convert_fusion
  30.7 0.1 eq.72
  30.8 0.2 fusion.19
  31.0 0.2 convolution_convert_fusion
  31.3 10.3 %all_to_all.10 = bf16[8,48,128]{2,1,0:T(8,128)(2,1)S(1)} all-to-all(bf16[8,48,128]{2,1,0:T(8,128)(2,1)S(1)} %bitcast.46), channel_id=1, replica_groups=mesh['nets'=8,'region'=4] {'nets'}, dimensions={0} | all-to-all | bytes 196608 | tf_op jit(solution)/shard_map/all_to_all | solution.py:103
  41.6 9.5 %fusion = f32[384,1,128]{2,1,0:T(1,128)S(1)} fusion(bf16[1,1,384,128,128]{4,3,2,1,0:T(8,128)(2,1)} %param.15, bf16[384,128,1]{1,0,2:T(8,128)(2,1)S(1)} %bitcast.44), kind=kOutput, calls=%fused_computation | convolution fusion | flops 12582912 | bytes 12877824 | tf_op jit(solution)/shard_map/tqe,te->tq/dot_general | solution.py:104
  51.1 8.7 %all-gather.1 = f32[4,387,128]{2,1,0:T(8,128)S(1)} all-gather(f32[1,387,128]{2,1,0:T(8,128)S(1)} %maximum_bitcast_fusion), channel_id=2, replica_groups=mesh['nets'=8,'region'=4] {'region'}, dimensions={0}, use_global_device_ids=true | all-gather | bytes 990720 | tf_op jit(solution)/shard_map/all_gather | solution.py:110
  59.9 0.2 reduce-precision_convert_fusion.1
  60.1 3.4 %fusion.4 = f32[2048,384]{1,0:T(8,128)S(1)} fusion(s32[1536]{0:T(1024)S(1)} %convert_element_type.59, bf16[1536,128]{1,0:T(8,128)(2,1)S(1)} %get-tuple-element.47, bf16[1536,128]{1,0:T(8,128)(2,1)S(1)} %get-tuple-element.48, bf16[1536,128]{1,0:T(8,128)(2,1)S(1)} %get-tuple-element.46), kind=kOutput, calls=%fused_computation.5 | convolution fusion | flops 2422603776 | bytes 4331520 | tf_op jit(solution)/shard_map/dot_general | solution.py:25
  63.5 0.1 slice_add_fusion
  63.7 0.1 fusion.46
  63.8 1.0 %copy-done = f32[1024,256]{1,0:T(8,128)S(1)} copy-done((f32[1024,256]{1,0:T(8,128)S(1)}, f32[1024,256]{1,0:T(8,128)}, u32[]{:S(2)}) %copy-start) | copy-done | bytes 1048600
  64.8 0.2 multiply_reduce_fusion
  65.0 1.2 %subtract_multiply_fusion = f32[1024,256]{1,0:T(8,128)} fusion(f32[1024,256]{1,0:T(8,128)S(1)} %copy-done, f32[1024,128]{1,0:T(8,128)S(1)} %get-tuple-element.45, f32[1024,128]{1,0:T(8,128)S(1)} %get-tuple-element.44, f32[1024]{0:T(1024)S(1)} %multiply_reduce_fusion), kind=kLoop, calls=%fused_computation.25 | loop fusion | flops 786432 | bytes 3149824 | tf_op jit(solution)/shard_map/mul | solution.py:119
  (27 shorter events, 0.4 us)
Async XLA Ops:
  0.6 6.0 %copy-start.3 = (s32[1,1,384]{2,1,0:T(1,128)S(1)}, s32[1,1,384]{2,1,0:T(1,128)}, u32[]{:S(2)}) copy-start(s32[1,1,384]{2,1,0:T(1,128)} %param.16) | copy-start | bytes 4612
  0.6 5.9 %copy-start.5 = (s32[1,1,8]{2,1,0:T(1,128)S(1)}, s32[1,1,8]{2,1,0:T(1,128)}, u32[]{:S(2)}) copy-start(s32[1,1,8]{2,1,0:T(1,128)} %param.18) | copy-start | bytes 100
  0.7 6.0 %copy-start.4 = (s32[1,1,384]{2,1,0:T(1,128)S(1)}, s32[1,1,384]{2,1,0:T(1,128)}, u32[]{:S(2)}) copy-start(s32[1,1,384]{2,1,0:T(1,128)} %param.17) | copy-start | bytes 4612
  7.7 14.4 %copy-start.1 = (s32[1,8192]{1,0:T(1,128)S(1)}, s32[1,8192]{1,0:T(1,128)}, u32[]{:S(2)}) copy-start(s32[1,8192]{1,0:T(1,128)} %param.19) | copy-start | bytes 98308
  14.9 15.7 %all-to-all-start = ((f32[8,56,128]{2,1,0:T(8,128)}), f32[8,56,128]{2,1,0:T(8,128)S(1)}, u32[]{:S(2)}, u32[]{:S(2)}) async-start(f32[8,56,128]{2,1,0:T(8,128)} %maximum_maximum_fusion), calls=%async_computation | async-start | bytes 458752 | tf_op jit(solution)/shard_map/all_to_all | solution.py:92
  31.0 20.0 %copy-start.2 = (f32[64,128]{1,0:T(8,128)}, f32[64,128]{1,0:T(8,128)S(1)}, u32[]{:S(2)}) copy-start(f32[64,128]{1,0:T(8,128)S(1)} %slice_add_fusion.2) | copy-start | bytes 98308
  63.5 1.2 %copy-start = (f32[1024,256]{1,0:T(8,128)S(1)}, f32[1024,256]{1,0:T(8,128)}, u32[]{:S(2)}) copy-start(f32[1024,256]{1,0:T(8,128)} %shard_map.87) | copy-start | bytes 3145732
